TPU v7x, 32 devices: a whole 2x2x4 slice. The times are simulated.
32 devices in a mesh: groups: 2 (over y), prompt: 4 (over x, core), resp: 4 (over z).
Axes of the slice: x: 2, y: 2, z: 4, core: 2. Of those that a mesh axis runs over, the one named last changes fastest.
Arguments:
- queries: bfloat16 [8, 4, 32, 8192], P(('groups', 'prompt'), 'resp'), parts along dimension 0, may hold values from -90 to 90
- cotangent: bfloat16 [8, 4, 32, 8192], P(('groups', 'prompt'), 'resp'), parts along dimension 0, may hold values from -6 to 6
- resp_keys: bfloat16 [8, 4, 32, 512], P(('groups', 'prompt'), 'resp'), parts along dimension 0, may hold values from -6 to 6
- resp_values: bfloat16 [8, 4, 32, 512], P(('groups', 'prompt'), 'resp'), parts along dimension 0, may hold values from -6 to 6
- prefix_keys: bfloat16 [8, 512, 512], P(('groups', 'prompt'), 'resp'), parts along dimension 0, may hold values from -5 to 5
- prefix_values: bfloat16 [8, 512, 512], P(('groups', 'prompt'), 'resp'), parts along dimension 0, may hold values from -6 to 6
- counts: int32 [8], P(('groups', 'prompt')), parts along dimension 0, may hold values from 1 to 4, as said below
- lengths: int32 [8, 4], P(('groups', 'prompt'), 'resp'), parts along dimension 0, may hold values from 8 to 32, as said below
- policy_likelihood: float32 [8, 4], P(('groups', 'prompt'), 'resp'), parts along dimension 0, may hold values from -8 to 8
- reference_likelihood: float32 [8, 4], P(('groups', 'prompt'), 'resp'), parts along dimension 0, may hold values from -8 to 8
Outputs:
- grad_queries: bfloat16 [8, 4, 32, 8192], P(('groups', 'prompt'), 'resp'), parts along dimension 0
- grad_resp_keys: bfloat16 [8, 4, 32, 512], P(('groups', 'prompt'), 'resp'), parts along dimension 0
- grad_resp_values: bfloat16 [8, 4, 32, 512], P(('groups', 'prompt'), 'resp'), parts along dimension 0
- grad_prefix_keys: bfloat16 [8, 512, 512], P(('groups', 'prompt'), 'resp'), parts along dimension 0
- grad_prefix_values: bfloat16 [8, 512, 512], P(('groups', 'prompt'), 'resp'), parts along dimension 0
- forget_loss: float32 [8], P(('groups', 'prompt')), parts along dimension 0
There are 2 independent parts, one for each index of `groups`. A program takes and returns all parts, laid end to end along the dimension named above; each array names one. Nothing has to cross between parts.
Inputs may be any that keep to these rules, and one draw needn't show every extreme that they name: `counts`: live responses of a prompt fill its first slots; some prompt has all 4. `lengths`: tokens of a response are its first slots, the rest padding; each prompt has a live response of 32 tokens.
All inputs are finite; a program needn't handle non-finite values.
Results may differ from a plain program's by a relative error of at most 0.0085.
Values may be sent and summed in bfloat16 or wider, within the bound.
No kernel may reach another device: no remote copies, remote signals or barrier semaphores. Data moves between devices by JAX's collectives and lax.ppermute only.
A program may use at most 128 MiB of HBM per device.

v0:
```python
import math

import jax
import jax.numpy as jnp
from jax import lax
from jax.sharding import PartitionSpec as P

HEADS = 64
KV_HEADS = 4
HEAD_DIM = 128


loss_beta = 0.5
masked_score = -1e30


def head_block(values_in, position, column_span):
    return lax.slice_in_dim(
        values_in, position * column_span, (position + 1) * column_span, axis=values_in.ndim - 1
    )


def across_rows(left_side, right_side):
    return lax.dot_general(
        left_side, right_side, (((1,), (1,)), ((), ())), preferred_element_type=jnp.float32
    )


def down_columns(left_side, right_side):
    return lax.dot_general(
        left_side, right_side, (((0,), (0,)), ((), ())), preferred_element_type=jnp.float32
    )


def own_scores(query_four, own_keys, scaling):
    resp_len = own_keys.shape[1]
    scores = (
        jnp.einsum("sqgd,skd->sqgk", query_four, own_keys, preferred_element_type=jnp.float32)
        * scaling
    )
    positions = jnp.arange(resp_len, dtype=jnp.int32)
    causal = positions[:, None] >= positions[None, :]
    return jnp.where(causal[None, :, None, :], scores, masked_score).reshape(-1, resp_len)


def own_slopes(grad_four, own_values):
    resp_len = own_values.shape[1]
    return jnp.einsum(
        "sqgd,skd->sqgk", grad_four, own_values, preferred_element_type=jnp.float32
    ).reshape(-1, resp_len)


def own_grads(shift_own, weights_own, query_four, grad_four, own_keys, scaling):
    four_shape = query_four.shape[:3] + (own_keys.shape[1],)
    shift_four = shift_own.reshape(four_shape)
    weight_four = weights_own.astype(jnp.bfloat16).reshape(four_shape)
    query_grad = (
        jnp.einsum("sqgk,skd->sqgd", shift_four, own_keys, preferred_element_type=jnp.float32)
        * scaling
    )
    key_grad = (
        jnp.einsum("sqgk,sqgd->skd", shift_four, query_four, preferred_element_type=jnp.float32)
        * scaling
    )
    value_grad = jnp.einsum(
        "sqgk,sqgd->skd", weight_four, grad_four, preferred_element_type=jnp.float32
    )
    return (query_grad.reshape(-1, own_keys.shape[2]), key_grad, value_grad)


def on_device(
    queries,
    cotangent,
    resp_keys,
    resp_values,
    prefix_keys,
    prefix_values,
    counts,
    lengths,
    policy_likelihood,
    reference_likelihood,
):
    group_size = HEADS // KV_HEADS
    group_width = group_size * HEAD_DIM
    scaling = 1.0 / math.sqrt(HEAD_DIM)
    slot_count = queries.shape[1]
    resp_len = queries.shape[2]
    local_keys = prefix_keys[0]
    local_values = prefix_values[0]
    prefix_len = local_keys.shape[0] * lax.axis_size("resp")
    live_count = counts[0]
    count_real = live_count.astype(jnp.float32)
    slot_ids = lax.axis_index("resp") * slot_count + jnp.arange(slot_count, dtype=jnp.int32)
    live_slots = slot_ids < live_count
    margin = policy_likelihood[0] - reference_likelihood[0]
    weight = jnp.where(live_slots, 2.0 * jax.nn.sigmoid(loss_beta * margin) / count_real, 0.0)
    loss_terms = jnp.where(live_slots, 2.0 / loss_beta * jax.nn.softplus(loss_beta * margin), 0.0)
    forget_loss = (lax.psum(jnp.sum(loss_terms), "resp") / count_real).reshape(1)
    positions = jnp.arange(resp_len, dtype=jnp.int32)
    kept_tokens = positions[None, :] < lengths[0][:, None]
    factor = jnp.where(kept_tokens, weight[:, None], 0.0)
    grad_out = (cotangent[0].astype(jnp.float32) * factor[:, :, None]).astype(jnp.bfloat16)
    query_fours, grad_fours, query_rows, grad_rows = ([], [], [], [])
    keys_own, scores_own, slopes_own = ([], [], [])
    for group_index in range(KV_HEADS):
        query_four = head_block(queries[0], group_index, group_width).reshape(
            slot_count, resp_len, group_size, HEAD_DIM
        )
        grad_four = head_block(grad_out, group_index, group_width).reshape(
            slot_count, resp_len, group_size, HEAD_DIM
        )
        own_keys = head_block(resp_keys[0], group_index, HEAD_DIM)
        own_values = head_block(resp_values[0], group_index, HEAD_DIM)
        query_fours.append(query_four)
        grad_fours.append(grad_four)
        query_rows.append(query_four.reshape(-1, HEAD_DIM))
        grad_rows.append(grad_four.reshape(-1, HEAD_DIM))
        keys_own.append(own_keys)
        scores_own.append(own_scores(query_four, own_keys, scaling))
        slopes_own.append(own_slopes(grad_four, own_values))
    query_grads, key_grads, value_grads = ([], [], [])
    start_peaks = jnp.stack(
        [jnp.max(scores_own[group_index], axis=1) for group_index in range(KV_HEADS)]
    )
    start_totals = jnp.stack(
        [
            jnp.sum(jnp.exp(scores_own[group_index] - start_peaks[group_index][:, None]), axis=1)
            for group_index in range(KV_HEADS)
        ]
    )
    arrived = lax.all_gather(local_keys, "resp", axis=0, tiled=True)
    peaks_out = []
    totals_out = []
    for add_group_index in range(KV_HEADS):
        scores_pre = (
            across_rows(query_rows[add_group_index], head_block(arrived, add_group_index, HEAD_DIM))
            * scaling
        )
        peaks_new = jnp.maximum(start_peaks[add_group_index], jnp.max(scores_pre, axis=1))
        totals_new = start_totals[add_group_index] * jnp.exp(
            start_peaks[add_group_index] - peaks_new
        ) + jnp.sum(jnp.exp(scores_pre - peaks_new[:, None]), axis=1)
        peaks_out.append(peaks_new)
        totals_out.append(totals_new)
    row_peaks = jnp.stack(peaks_out)
    totals = jnp.stack(totals_out)
    log_total = row_peaks + jnp.log(totals)
    weights_own = [
        jnp.exp(scores_own[group_index] - log_total[group_index][:, None])
        for group_index in range(KV_HEADS)
    ]
    start_centre = jnp.stack(
        [
            jnp.sum(weights_own[group_index] * slopes_own[group_index], axis=1)
            for group_index in range(KV_HEADS)
        ]
    )

    def add_centre(running, arrived):
        piece_keys, piece_values = arrived
        new_centre = []
        for group_index in range(KV_HEADS):
            scores_pre = (
                across_rows(query_rows[group_index], head_block(piece_keys, group_index, HEAD_DIM))
                * scaling
            )
            weights_pre = jnp.exp(scores_pre - log_total[group_index][:, None])
            slope_pre = across_rows(
                grad_rows[group_index], head_block(piece_values, group_index, HEAD_DIM)
            )
            new_centre.append(running[group_index] + jnp.sum(weights_pre * slope_pre, axis=1))
        return jnp.stack(new_centre)

    centre = add_centre(
        start_centre,
        (
            lax.all_gather(local_keys, "resp", axis=0, tiled=True),
            lax.all_gather(local_values, "resp", axis=0, tiled=True),
        ),
    )
    start_query = []
    for group_index in range(KV_HEADS):
        shift_mine = (
            weights_own[group_index] * (slopes_own[group_index] - centre[group_index][:, None])
        ).astype(jnp.bfloat16)
        query_grad, key_grad, value_grad = own_grads(
            shift_mine,
            weights_own[group_index],
            query_fours[group_index],
            grad_fours[group_index],
            keys_own[group_index],
            scaling,
        )
        start_query.append(query_grad)
        key_grads.append(key_grad)
        value_grads.append(value_grad)
    empty_rows = jnp.zeros((prefix_len, KV_HEADS * HEAD_DIM), jnp.float32)

    def add_terms(running, arrived):
        query_in, keys_in, values_in = running
        piece_keys, piece_values = arrived
        query_out, key_cols, value_cols = ([], [], [])
        for group_index in range(KV_HEADS):
            head_keys = head_block(piece_keys, group_index, HEAD_DIM)
            scores_pre = across_rows(query_rows[group_index], head_keys) * scaling
            weights_pre = jnp.exp(scores_pre - log_total[group_index][:, None])
            slope_pre = across_rows(
                grad_rows[group_index], head_block(piece_values, group_index, HEAD_DIM)
            )
            shift_pre = (weights_pre * (slope_pre - centre[group_index][:, None])).astype(
                jnp.bfloat16
            )
            query_out.append(
                query_in[group_index]
                + jnp.dot(shift_pre, head_keys, preferred_element_type=jnp.float32) * scaling
            )
            key_cols.append(down_columns(shift_pre, query_rows[group_index]) * scaling)
            value_cols.append(
                down_columns(weights_pre.astype(jnp.bfloat16), grad_rows[group_index])
            )
        keys_out = jnp.concatenate(key_cols, axis=1)
        values_out = jnp.concatenate(value_cols, axis=1)
        return (jnp.stack(query_out), keys_out, values_out)

    query_sum, partial_keys, partial_values = add_terms(
        (jnp.stack(start_query), empty_rows, empty_rows),
        (
            lax.all_gather(local_keys, "resp", axis=0, tiled=True),
            lax.all_gather(local_values, "resp", axis=0, tiled=True),
        ),
    )
    query_grads = [query_sum[group_index] for group_index in range(KV_HEADS)]
    grad_queries = jnp.concatenate(
        [
            query_grads[group_index].reshape(slot_count, resp_len, group_width)
            for group_index in range(KV_HEADS)
        ],
        axis=2,
    ).astype(jnp.bfloat16)
    grad_resp_keys = jnp.concatenate(key_grads, axis=2).astype(jnp.bfloat16)
    grad_resp_values = jnp.concatenate(value_grads, axis=2).astype(jnp.bfloat16)
    summed_keys, summed_values = (
        lax.psum_scatter(
            partial_keys.astype(jnp.bfloat16), "resp", scatter_dimension=0, tiled=True
        ).astype(jnp.float32),
        lax.psum_scatter(
            partial_values.astype(jnp.bfloat16), "resp", scatter_dimension=0, tiled=True
        ).astype(jnp.float32),
    )
    return (
        grad_queries[None],
        grad_resp_keys[None],
        grad_resp_values[None],
        summed_keys.astype(jnp.bfloat16)[None],
        summed_values.astype(jnp.bfloat16)[None],
        forget_loss,
    )


def solution(mesh):
    placed = (
        P(("groups", "prompt"), "resp", None, None),
        P(("groups", "prompt"), "resp", None, None),
        P(("groups", "prompt"), "resp", None, None),
        P(("groups", "prompt"), "resp", None, None),
        P(("groups", "prompt"), "resp", None),
        P(("groups", "prompt"), "resp", None),
        P(("groups", "prompt")),
        P(("groups", "prompt"), "resp"),
        P(("groups", "prompt"), "resp"),
        P(("groups", "prompt"), "resp"),
    )
    return jax.shard_map(
        on_device,
        mesh=mesh,
        in_specs=placed,
        out_specs=(
            P(("groups", "prompt"), "resp", None, None),
            P(("groups", "prompt"), "resp", None, None),
            P(("groups", "prompt"), "resp", None, None),
            P(("groups", "prompt"), "resp", None),
            P(("groups", "prompt"), "resp", None),
            P(("groups", "prompt")),
        ),
        check_vma=False,
    )
```

profile of v0, /device:TPU:0, one launch (start us, length us, event | category | flops | bytes accessed | tf_op | source)
XLA Modules:
  0.0 151.5 jit_solution(3817466985412128707)
XLA Ops:
  7.2 1.3 slice_bitcast_fusion.27
  17.3 17.4 %all-gather = bf16[1,512,512]{2,1,0:T(8,128)(2,1)S(1)} all-gather(bf16[1,128,512]{2,1,0:T(8,128)(2,1)S(1)} %copy-done.58), channel_id=2, replica_groups=mesh['groups'=2,'prompt'=4,'resp'=4] {'resp'}, dimensions={1}, use_global_device_ids=true | all-gather | bytes 655360 | tf_op jit(solution)/shard_map/all_gather | solution.py:131
  34.9 0.9 slice_bitcast_fusion.23
  45.7 1.2 fusion.74
  52.4 0.9 pad_maximum_fusion.2
  53.2 2.1 %copy.87 = bf16[512,512]{1,0:T(8,128)(2,1)} copy(bf16[512,512]{0,1:T(8,128)(2,1)} %pad_maximum_fusion.2) | data formatting | bytes 1048576
  55.4 19.7 %all-gather.1 = bf16[1,512,512]{2,1,0:T(8,128)(2,1)S(1)} all-gather(bf16[1,128,512]{2,1,0:T(8,128)(2,1)} %param.15), channel_id=3, replica_groups=mesh['groups'=2,'prompt'=4,'resp'=4] {'resp'}, dimensions={1}, use_global_device_ids=true | all-gather | bytes 655360 | tf_op jit(solution)/shard_map/all_gather | solution.py:178
  75.1 3.1 %multiply_reduce_fusion.3 = (f32[512]{0:T(512)}, f32[512,512]{0,1:T(8,128)}) fusion(f32[512,512]{0,1:T(8,128)} %copy-done, f32[512]{0:T(512)S(1)} %bitcast.309, bf16[512,128]{1,0:T(8,128)(2,1)S(1)} %dot_general.148, bf16[512,512]{1,0:T(8,128)(2,1)S(1)} %bitcast.255), kind=kOutput, calls=%fused_computation.80 | convolution fusion | flops 67894784 | bytes 2363392 | tf_op jit(solution)/shard_map/dot_general | solution.py:24
  78.3 1.9 %multiply_reduce_fusion.2 = (f32[512]{0:T(512)}, f32[512,512]{0,1:T(8,128)}) fusion(f32[512,512]{0,1:T(8,128)S(1)} %get-tuple-element.67, f32[512]{0:T(512)S(1)} %bitcast.304, bf16[512,128]{1,0:T(8,128)(2,1)S(1)} %copy-done.18, bf16[512,512]{1,0:T(8,128)(2,1)S(1)} %bitcast.256), kind=kOutput, calls=%fused_computation.77 | convolution fusion | flops 67894784 | bytes 2363392 | tf_op jit(solution)/shard_map/dot_general | solution.py:24
  80.2 1.9 %multiply_reduce_fusion.1 = (f32[512]{0:T(512)}, f32[512,512]{0,1:T(8,128)}) fusion(f32[512,512]{0,1:T(8,128)S(1)} %get-tuple-element.63, f32[512]{0:T(512)S(1)} %bitcast.299, bf16[512,128]{1,0:T(8,128)(2,1)S(1)} %copy-done.20, bf16[512,512]{1,0:T(8,128)(2,1)S(1)} %bitcast.257), kind=kOutput, calls=%fused_computation.74 | convolution fusion | flops 67894784 | bytes 2363392 | tf_op jit(solution)/shard_map/dot_general | solution.py:24
  82.0 1.9 %multiply_reduce_fusion = (f32[512]{0:T(512)}, f32[512,512]{0,1:T(8,128)}) fusion(f32[512,512]{0,1:T(8,128)S(1)} %get-tuple-element.59, f32[512]{0:T(512)S(1)} %bitcast.294, bf16[512,128]{1,0:T(8,128)(2,1)S(1)} %copy-done.22, bf16[512,512]{1,0:T(8,128)(2,1)S(1)} %bitcast.258), kind=kOutput, calls=%fused_computation.71 | convolution fusion | flops 67894784 | bytes 2363392 | tf_op jit(solution)/shard_map/dot_general | solution.py:24
  84.7 1.7 %copy.74 = f32[512,32]{0,1:T(8,128)} copy(f32[512,32]{1,0:T(8,128)} %bitcast.252) | data formatting | bytes 131072 | tf_op jit(solution)/shard_map/reshape | solution.py:43
  86.3 1.7 %copy.72 = f32[512,32]{0,1:T(8,128)} copy(f32[512,32]{1,0:T(8,128)} %bitcast.253) | data formatting | bytes 131072 | tf_op jit(solution)/shard_map/reshape | solution.py:43
  88.0 1.7 %copy.70 = f32[512,32]{0,1:T(8,128)} copy(f32[512,32]{1,0:T(8,128)} %bitcast.254) | data formatting | bytes 131072 | tf_op jit(solution)/shard_map/reshape | solution.py:43
  89.7 1.8 %multiply_reduce_fusion.4 = (f32[512]{0:T(512)S(1)}, f32[512,32]{0,1:T(8,128)}) fusion(f32[512,32]{0,1:T(8,128)} %copy.76, f32[512]{0:T(512)S(1)} %bitcast.295, bf16[512,128]{1,0:T(8,128)(2,1)} %dot_general.163, bf16[1,32,512]{2,1,0:T(8,128)(2,1)} %bitcast.313), kind=kOutput, calls=%fused_computation.126 | convolution fusion | flops 4242944 | bytes 274432 | tf_op jit(solution)/shard_map/sqgd,skd->sqgk/dot_general | solution.py:48
  91.5 1.7 %multiply_reduce_fusion.5 = (f32[512]{0:T(512)S(1)}, f32[512,32]{0,1:T(8,128)}) fusion(f32[512,32]{0,1:T(8,128)} %copy.74, f32[512]{0:T(512)S(1)} %bitcast.300, bf16[512,128]{1,0:T(8,128)(2,1)} %dot_general.158, bf16[1,32,512]{2,1,0:T(8,128)(2,1)} %bitcast.314), kind=kOutput, calls=%fused_computation.129 | convolution fusion | flops 4242944 | bytes 274432 | tf_op jit(solution)/shard_map/sqgd,skd->sqgk/dot_general | solution.py:48
  93.2 1.7 %multiply_reduce_fusion.6 = (f32[512]{0:T(512)S(1)}, f32[512,32]{0,1:T(8,128)}) fusion(f32[512,32]{0,1:T(8,128)} %copy.72, f32[512]{0:T(512)S(1)} %bitcast.305, bf16[512,128]{1,0:T(8,128)(2,1)} %dot_general.153, bf16[1,32,512]{2,1,0:T(8,128)(2,1)} %bitcast.315), kind=kOutput, calls=%fused_computation.132 | convolution fusion | flops 4242944 | bytes 274432 | tf_op jit(solution)/shard_map/sqgd,skd->sqgk/dot_general | solution.py:48
  94.9 1.6 %multiply_reduce_fusion.7 = (f32[512]{0:T(512)S(1)}, f32[512,32]{0,1:T(8,128)}) fusion(f32[512,32]{0,1:T(8,128)} %copy.70, f32[512]{0:T(512)S(1)} %bitcast.310, bf16[512,128]{1,0:T(8,128)(2,1)S(1)} %dot_general.148, bf16[1,32,512]{2,1,0:T(8,128)(2,1)} %bitcast.316), kind=kOutput, calls=%fused_computation.135 | convolution fusion | flops 4242944 | bytes 274432 | tf_op jit(solution)/shard_map/sqgd,skd->sqgk/dot_general | solution.py:48
  97.2 1.6 %multiply_convert_fusion.3 = bf16[512,512]{0,1:T(8,128)(2,1)S(1)} fusion(f32[512,512]{0,1:T(8,128)} %get-tuple-element.87, f32[512,512]{0,1:T(8,128)S(1)} %copy-done.1, f32[512]{0:T(512)S(1)} %add.106, f32[512]{0:T(512)S(1)} %bitcast.311), kind=kLoop, calls=%fused_computation.79 | loop fusion | flops 1048576 | bytes 2625536 | tf_op jit(solution)/shard_map/convert_element_type | solution.py:210
  103.8 0.9 pad_maximum_fusion.1
  104.7 0.8 copy-done.36
  106.5 0.8 fusion.35
  109.1 0.8 fusion.34
  111.6 0.8 fusion.33
  112.4 0.9 convolution_multiply_fusion.11
  114.2 0.8 fusion.32
  115.0 0.9 convolution_multiply_fusion.9
  120.1 1.0 fusion.15
  127.3 12.0 %psum.7 = f32[]{:T(128)} all-reduce(f32[]{:T(128)} %bitcast.64), channel_id=1, replica_groups=mesh['groups'=2,'prompt'=4,'resp'=4] {'resp'}, use_global_device_ids=true, to_apply=%region_26.27 | all-reduce | flops 1 | bytes 8 | tf_op jit(solution)/shard_map/psum | solution.py:98
  140.9 0.8 pad_maximum_fusion
  141.7 1.0 copy.88
  142.8 0.8 copy.82
  (270 shorter events, 44.2 us)
Async XLA Ops:
  7.2 134.6 %reduce-scatter.7.cloned.1.call-start = ((), (), s32[]{:S(2)}) async-start(), calls=%async_computation.3 | async-start | bytes 655360
  10.4 30.2 %copy-start.11 = (f32[32,16,32]{2,1,0:T(8,128)}, f32[32,16,32]{2,1,0:T(8,128)S(1)}, u32[]{:S(2)}) copy-start(f32[32,16,32]{2,1,0:T(8,128)S(1)} %get-tuple-element.61) | copy-start | bytes 196612
  11.8 29.7 %copy-start.13 = (f32[32,16,32]{2,1,0:T(8,128)}, f32[32,16,32]{2,1,0:T(8,128)S(1)}, u32[]{:S(2)}) copy-start(f32[32,16,32]{2,1,0:T(8,128)S(1)} %get-tuple-element.65) | copy-start | bytes 196612
  12.6 4.7 %copy-start.58 = (bf16[1,128,512]{2,1,0:T(8,128)(2,1)S(1)}, bf16[1,128,512]{2,1,0:T(8,128)(2,1)}, u32[]{:S(2)}) copy-start(bf16[1,128,512]{2,1,0:T(8,128)(2,1)} %param.14) | copy-start | bytes 393220
  12.7 22.1 %copy-start.52 = (bf16[1,1,32,8192]{3,2,1,0:T(8,128)(2,1)S(1)}, bf16[1,1,32,8192]{3,2,1,0:T(8,128)(2,1)}, u32[]{:S(2)}) copy-start(bf16[1,1,32,8192]{3,2,1,0:T(8,128)(2,1)} %param.11) | copy-start | bytes 1572868
  13.3 29.2 %copy-start.15 = (f32[32,16,32]{2,1,0:T(8,128)}, f32[32,16,32]{2,1,0:T(8,128)S(1)}, u32[]{:S(2)}) copy-start(f32[32,16,32]{2,1,0:T(8,128)S(1)} %get-tuple-element.69) | copy-start | bytes 196612
  34.7 9.4 %copy-start.6 = (bf16[1,512,512]{2,1,0:T(8,128)(2,1)}, bf16[1,512,512]{2,1,0:T(8,128)(2,1)S(1)}, u32[]{:S(2)}) copy-start(bf16[1,512,512]{2,1,0:T(8,128)(2,1)S(1)} %all-gather) | copy-start | bytes 1572868
  39.6 4.1 %copy-start.27 = (bf16[512,128]{1,0:T(8,128)(2,1)}, bf16[512,128]{1,0:T(8,128)(2,1)S(1)}, u32[]{:S(2)}) copy-start(bf16[512,128]{1,0:T(8,128)(2,1)S(1)} %reshape_reshape.17) | copy-start | bytes 393220
  39.7 3.7 %copy-start.29 = (bf16[512,128]{1,0:T(8,128)(2,1)}, bf16[512,128]{1,0:T(8,128)(2,1)S(1)}, u32[]{:S(2)}) copy-start(bf16[512,128]{1,0:T(8,128)(2,1)S(1)} %reshape_reshape.16) | copy-start | bytes 393220
  43.7 8.3 %copy-start = (f32[512,512]{0,1:T(8,128)}, f32[512,512]{0,1:T(8,128)S(1)}, u32[]{:S(2)}) copy-start(f32[512,512]{0,1:T(8,128)S(1)} %get-tuple-element.71) | copy-start | bytes 3145732
  55.4 88.2 %reduce-scatter.5.cloned.1.call-start = ((), (), s32[]{:S(2)}) async-start(), calls=%async_computation.2 | async-start | bytes 655360 | tf_op jit(solution)/shard_map/reduce_scatter | solution.py:243
  75.1 3.1 %copy-start.18 = (bf16[512,128]{1,0:T(8,128)(2,1)S(1)}, bf16[512,128]{1,0:T(8,128)(2,1)}, u32[]{:S(2)}) copy-start(bf16[512,128]{1,0:T(8,128)(2,1)} %dot_general.153) | copy-start | bytes 393220
  78.3 1.9 %copy-start.20 = (bf16[512,128]{1,0:T(8,128)(2,1)S(1)}, bf16[512,128]{1,0:T(8,128)(2,1)}, u32[]{:S(2)}) copy-start(bf16[512,128]{1,0:T(8,128)(2,1)} %dot_general.158) | copy-start | bytes 393220
  80.2 1.9 %copy-start.22 = (bf16[512,128]{1,0:T(8,128)(2,1)S(1)}, bf16[512,128]{1,0:T(8,128)(2,1)}, u32[]{:S(2)}) copy-start(bf16[512,128]{1,0:T(8,128)(2,1)} %dot_general.163) | copy-start | bytes 393220
  89.7 7.5 %copy-start.1 = (f32[512,512]{0,1:T(8,128)S(1)}, f32[512,512]{0,1:T(8,128)}, u32[]{:S(2)}) copy-start(f32[512,512]{0,1:T(8,128)} %copy-done) | copy-start | bytes 3145732
  97.2 1.6 %copy-start.30 = (bf16[512,128]{1,0:T(8,128)(2,1)S(1)}, bf16[512,128]{1,0:T(8,128)(2,1)}, u32[]{:S(2)}) copy-start(bf16[512,128]{1,0:T(8,128)(2,1)} %copy-done.29) | copy-start | bytes 393220
  97.2 2.6 %copy-start.10 = (f32[512,512]{0,1:T(8,128)S(1)}, f32[512,512]{0,1:T(8,128)}, u32[]{:S(2)}) copy-start(f32[512,512]{0,1:T(8,128)} %get-tuple-element.83) | copy-start | bytes 3145732
  98.8 1.3 copy-start.2
  99.8 1.3 copy-start.9
  100.1 1.7 %copy-start.4 = (bf16[512,512]{0,1:T(8,128)(2,1)}, bf16[512,512]{0,1:T(8,128)(2,1)S(1)}, u32[]{:S(2)}) copy-start(bf16[512,512]{0,1:T(8,128)(2,1)S(1)} %multiply_convert_fusion.2) | copy-start | bytes 1572868
  101.4 1.3 copy-start.8
  114.2 1.7 %copy-start.48 = (bf16[4,8,16,128]{3,1,2,0:T(8,128)(2,1)S(1)}, bf16[4,8,16,128]{3,1,2,0:T(8,128)(2,1)}, u32[]{:S(2)}) copy-start(bf16[4,8,16,128]{3,1,2,0:T(8,128)(2,1)} %get-tuple-element.36) | copy-start | bytes 393220
  115.0 1.6 %copy-start.47 = (bf16[4,8,16,128]{3,1,2,0:T(8,128)(2,1)S(1)}, bf16[4,8,16,128]{3,1,2,0:T(8,128)(2,1)}, u32[]{:S(2)}) copy-start(bf16[4,8,16,128]{3,1,2,0:T(8,128)(2,1)} %get-tuple-element.37) | copy-start | bytes 393220
  115.0 2.2 %copy-start.46 = (bf16[4,8,16,128]{3,1,2,0:T(8,128)(2,1)S(1)}, bf16[4,8,16,128]{3,1,2,0:T(8,128)(2,1)}, u32[]{:S(2)}) copy-start(bf16[4,8,16,128]{3,1,2,0:T(8,128)(2,1)} %get-tuple-element.38) | copy-start | bytes 393220
  115.0 2.9 %copy-start.45 = (bf16[4,8,16,128]{3,1,2,0:T(8,128)(2,1)S(1)}, bf16[4,8,16,128]{3,1,2,0:T(8,128)(2,1)}, u32[]{:S(2)}) copy-start(bf16[4,8,16,128]{3,1,2,0:T(8,128)(2,1)} %get-tuple-element.39) | copy-start | bytes 393220
  115.9 2.1 %copy-start.71 = (f32[512]{0:T(512)S(1)}, f32[512]{0:T(512)}, u32[]{:S(2)}) copy-start(f32[512]{0:T(512)} %get-tuple-element.24) | copy-start | bytes 6148
  115.9 4.2 %copy-start.3 = (bf16[512,512]{0,1:T(8,128)(2,1)S(1)}, bf16[512,512]{0,1:T(8,128)(2,1)}, u32[]{:S(2)}) copy-start(bf16[512,512]{0,1:T(8,128)(2,1)} %copy-done.2) | copy-start | bytes 1572868
  115.9 4.2 %copy-start.7 = (bf16[1,512,512]{2,1,0:T(8,128)(2,1)S(1)}, bf16[1,512,512]{2,1,0:T(8,128)(2,1)}, u32[]{:S(2)}) copy-start(bf16[1,512,512]{2,1,0:T(8,128)(2,1)} %copy-done.6) | copy-start | bytes 1572868
  117.2 1.4 copy-start.70
  117.2 2.1 %copy-start.69 = (f32[512]{0:T(512)S(1)}, f32[512]{0:T(512)}, u32[]{:S(2)}) copy-start(f32[512]{0:T(512)} %get-tuple-element.26) | copy-start | bytes 6148
  117.2 2.8 %copy-start.68 = (f32[512]{0:T(512)S(1)}, f32[512]{0:T(512)}, u32[]{:S(2)}) copy-start(f32[512]{0:T(512)} %get-tuple-element.27) | copy-start | bytes 6148
  126.2 13.0 %copy-start.53 = (bf16[512,128]{1,0:T(8,128)(2,1)S(1)}, bf16[512,128]{1,0:T(8,128)(2,1)}, u32[]{:S(2)}) copy-start(bf16[512,128]{1,0:T(8,128)(2,1)} %fusion.15) | copy-start | bytes 393220
  (54 other events, 46.4 us)
Sparse Core Ops, SparseCore 0:
  55.5 24.7 reduce-scatter.6
  104.9 21.6 reduce-scatter.4
where the time goes:
time: 153 us; the launch traced here: 152 us
  blocking collectives  49.1 us (32%)
  local copies, waits for them, and re-layouts  44.7 us (29%)
  matrix products  29.8 us (19%)
  between operations  19.5 us (13%)
  other arithmetic  8.31 us (5%)
    unnamed x181, local copies, waits for them, and re-layouts  25.9 us
    all_gather x1, blocking collectives, on_device(): lax.all_gather(local_values, 'resp', axis=0, tiled=True)  19.7 us
    all_gather x1, blocking collectives, on_device(): arrived = lax.all_gather(local_keys, 'resp', axis=0, tiled=True)  17.4 us
    psum x1, blocking collectives, on_device(): lax.psum(jnp.sum(loss_terms), 'resp') / count_real  12 us
    dot_general x8, matrix products, across_rows(): lax.dot_general(left_side, right_side, (((1,), (1,)), ((), ())), preferre...  10.9 us
    dot_general x4, matrix products, own_slopes(): jnp.einsum('sqgd,skd->sqgk', grad_four, own_values, preferred_element_typ...  6.84 us
    reshape x4, local copies, waits for them, and re-layouts, own_scores(): jnp.where(causal[None, :, None, :], scores, masked_score)  5.78 us
    dot_general x4, matrix products, own_grads(): jnp.einsum('sqgk,sqgd->skd', shift_four, query_four, preferred_element_ty...  3.16 us
  transfers between devices with their start and end apart: 2, of which 0 were waited for; matrix products, arithmetic and copies ran while one was open for 29% of the time, Pallas kernels for 0%

commit v1 on v0

v1 whole, which is shorter than its diff:
```python
import functools
import math

import jax
import jax.numpy as jnp
from jax import lax
from jax.experimental import pallas as pl
from jax.experimental.pallas import tpu as pltpu
from jax.sharding import PartitionSpec as P

HEADS = 64
KV_HEADS = 4
HEAD_DIM = 128


loss_beta = 0.5
masked_score = -1e30


def attention_kernel(n_pieces, factor_ref, q_ref, cot_ref, kown_ref, vown_ref, *rest):
    piece_refs = rest[:n_pieces]
    dq_ref, dkown_ref, dvown_ref = rest[n_pieces:n_pieces + 3]
    part_refs = rest[n_pieces + 3:]
    group_size = HEADS // KV_HEADS
    group_width = group_size * HEAD_DIM
    kv_width = KV_HEADS * HEAD_DIM
    resp_len = q_ref.shape[0]
    piece_len = piece_refs[0].shape[0]
    scaling = 1.0 / math.sqrt(HEAD_DIM)
    rows = group_size * resp_len
    factor = factor_ref[...]
    token_of_row = lax.broadcasted_iota(jnp.int32, (rows, resp_len), 0) % resp_len
    own_pos = lax.broadcasted_iota(jnp.int32, (rows, resp_len), 1)
    causal = token_of_row >= own_pos
    contract_rows = (((0,), (0,)), ((), ()))
    contract_cols = (((1,), (1,)), ((), ()))
    for g in range(KV_HEADS):
        base = g * group_width
        q_rows = jnp.concatenate(
            [q_ref[:, base + h * HEAD_DIM:base + (h + 1) * HEAD_DIM] for h in range(group_size)], axis=0
        )
        g_rows = jnp.concatenate(
            [
                (cot_ref[:, base + h * HEAD_DIM:base + (h + 1) * HEAD_DIM].astype(jnp.float32) * factor).astype(
                    jnp.bfloat16
                )
                for h in range(group_size)
            ],
            axis=0,
        )
        k_cols = slice(g * HEAD_DIM, (g + 1) * HEAD_DIM)
        v_cols = slice(kv_width + g * HEAD_DIM, kv_width + (g + 1) * HEAD_DIM)
        k_pre = jnp.concatenate([r[:, k_cols] for r in piece_refs], axis=0)
        v_pre = jnp.concatenate([r[:, v_cols] for r in piece_refs], axis=0)
        k_own = kown_ref[:, k_cols]
        v_own = vown_ref[:, k_cols]
        s_pre = lax.dot_general(q_rows, k_pre, contract_cols, preferred_element_type=jnp.float32) * scaling
        s_own = lax.dot_general(q_rows, k_own, contract_cols, preferred_element_type=jnp.float32) * scaling
        s_own = jnp.where(causal, s_own, masked_score)
        peak = jnp.maximum(jnp.max(s_pre, axis=1, keepdims=True), jnp.max(s_own, axis=1, keepdims=True))
        total = jnp.sum(jnp.exp(s_pre - peak), axis=1, keepdims=True) + jnp.sum(
            jnp.exp(s_own - peak), axis=1, keepdims=True
        )
        log_total = peak + jnp.log(total)
        p_pre = jnp.exp(s_pre - log_total)
        p_own = jnp.exp(s_own - log_total)
        dp_pre = lax.dot_general(g_rows, v_pre, contract_cols, preferred_element_type=jnp.float32)
        dp_own = lax.dot_general(g_rows, v_own, contract_cols, preferred_element_type=jnp.float32)
        centre = jnp.sum(p_pre * dp_pre, axis=1, keepdims=True) + jnp.sum(p_own * dp_own, axis=1, keepdims=True)
        ds_pre = (p_pre * (dp_pre - centre)).astype(jnp.bfloat16)
        ds_own = (p_own * (dp_own - centre)).astype(jnp.bfloat16)
        pl_pre = p_pre.astype(jnp.bfloat16)
        pl_own = p_own.astype(jnp.bfloat16)
        dq_rows = (
            jnp.dot(ds_pre, k_pre, preferred_element_type=jnp.float32) * scaling
            + jnp.dot(ds_own, k_own, preferred_element_type=jnp.float32) * scaling
        )
        for h in range(group_size):
            dq_ref[:, base + h * HEAD_DIM:base + (h + 1) * HEAD_DIM] = dq_rows[
                h * resp_len:(h + 1) * resp_len
            ].astype(jnp.bfloat16)
        dk_own = lax.dot_general(ds_own, q_rows, contract_rows, preferred_element_type=jnp.float32) * scaling
        dv_own = lax.dot_general(pl_own, g_rows, contract_rows, preferred_element_type=jnp.float32)
        dkown_ref[:, k_cols] = dk_own.astype(jnp.bfloat16)
        dvown_ref[:, k_cols] = dv_own.astype(jnp.bfloat16)
        dk_pre = lax.dot_general(ds_pre, q_rows, contract_rows, preferred_element_type=jnp.float32) * scaling
        dv_pre = lax.dot_general(pl_pre, g_rows, contract_rows, preferred_element_type=jnp.float32)
        for i, r in enumerate(part_refs):
            r[:, k_cols] = dk_pre[i * piece_len:(i + 1) * piece_len].astype(jnp.bfloat16)
            r[:, v_cols] = dv_pre[i * piece_len:(i + 1) * piece_len].astype(jnp.bfloat16)


def shifted(value, shift, n):
    return lax.ppermute(value, "resp", [(i, (i + shift) % n) for i in range(n)])


def on_device(
    queries,
    cotangent,
    resp_keys,
    resp_values,
    prefix_keys,
    prefix_values,
    counts,
    lengths,
    policy_likelihood,
    reference_likelihood,
):
    n = lax.axis_size("resp")
    slot_count = queries.shape[1]
    assert slot_count == 1
    resp_len = queries.shape[2]
    piece_len = prefix_keys.shape[1]
    kv_width = KV_HEADS * HEAD_DIM
    local_kv = jnp.concatenate([prefix_keys[0], prefix_values[0]], axis=1)
    pieces = [local_kv] + [shifted(local_kv, k, n) for k in range(1, n)]
    live_count = counts[0]
    count_real = live_count.astype(jnp.float32)
    slot_ids = lax.axis_index("resp") * slot_count + jnp.arange(slot_count, dtype=jnp.int32)
    live_slots = slot_ids < live_count
    margin = policy_likelihood[0] - reference_likelihood[0]
    weight = jnp.where(live_slots, 2.0 * jax.nn.sigmoid(loss_beta * margin) / count_real, 0.0)
    loss_terms = jnp.where(live_slots, 2.0 / loss_beta * jax.nn.softplus(loss_beta * margin), 0.0)
    all_terms = [loss_terms] + [shifted(loss_terms, k, n) for k in range(1, n)]
    forget_loss = (jnp.sum(jnp.concatenate(all_terms)) / count_real).reshape(1)
    positions = jnp.arange(resp_len, dtype=jnp.int32)
    factor = jnp.where(positions[None, :] < lengths[0][:, None], weight[:, None], 0.0)
    factor = factor.reshape(resp_len, 1).astype(jnp.float32)
    out_shape = (
        jax.ShapeDtypeStruct(queries.shape[2:], jnp.bfloat16),
        jax.ShapeDtypeStruct(resp_keys.shape[2:], jnp.bfloat16),
        jax.ShapeDtypeStruct(resp_values.shape[2:], jnp.bfloat16),
    ) + tuple(jax.ShapeDtypeStruct((piece_len, 2 * kv_width), jnp.bfloat16) for _ in range(n))
    results = pl.pallas_call(
        functools.partial(attention_kernel, n),
        out_shape=out_shape,
    )(factor, queries[0, 0], cotangent[0, 0], resp_keys[0, 0], resp_values[0, 0], *pieces)
    grad_q, grad_k, grad_v = results[:3]
    parts = results[3:]
    summed = parts[0].astype(jnp.float32)
    for k in range(1, n):
        summed = summed + shifted(parts[k], -k, n).astype(jnp.float32)
    summed = summed.astype(jnp.bfloat16)
    return (
        grad_q[None, None],
        grad_k[None, None],
        grad_v[None, None],
        summed[:, :kv_width][None],
        summed[:, kv_width:][None],
        forget_loss,
    )


def solution(mesh):
    placed = (
        P(("groups", "prompt"), "resp", None, None),
        P(("groups", "prompt"), "resp", None, None),
        P(("groups", "prompt"), "resp", None, None),
        P(("groups", "prompt"), "resp", None, None),
        P(("groups", "prompt"), "resp", None),
        P(("groups", "prompt"), "resp", None),
        P(("groups", "prompt")),
        P(("groups", "prompt"), "resp"),
        P(("groups", "prompt"), "resp"),
        P(("groups", "prompt"), "resp"),
    )
    return jax.shard_map(
        on_device,
        mesh=mesh,
        in_specs=placed,
        out_specs=(
            P(("groups", "prompt"), "resp", None, None),
            P(("groups", "prompt"), "resp", None, None),
            P(("groups", "prompt"), "resp", None, None),
            P(("groups", "prompt"), "resp", None),
            P(("groups", "prompt"), "resp", None),
            P(("groups", "prompt")),
        ),
        check_vma=False,
    )
```

time: 153 us -> 73.3 us (0.48)
  blocking collectives: 49.1 us -> 0 us
  local copies, waits for them, and re-layouts: 44.7 us -> 1.55 us
  starting transfers between devices: 0.08 us -> 31.7 us
  matrix products: 29.8 us -> 0 us
  waiting for transfers between devices: 0.04 us -> 22.2 us
  between operations: 19.5 us -> 6.66 us
  Pallas kernels: 0 us -> 8.26 us
  other arithmetic: 8.31 us -> 2.72 us
    all_gather x2 -> x0, blocking collectives: 37.1 us -> none  [the longest x1 19.7 us: on_device(): lax.all_gather(local_values, 'resp', axis=0, tiled=True)]
    ppermute x0 -> x9, starting transfers between devices: none -> 31.7 us  [shifted(): return lax.ppermute(value, 'resp', [(i, (i + shift) % n) for i in range(n)])]
    dot_general x40 -> x0, matrix products: 29.8 us -> none  [the longest x8 10.9 us: across_rows(): lax.dot_general(left_side, right_side, (((1,), (1,)), ((), ())), preferre...]
    unnamed x181 -> x8, local copies, waits for them, and re-layouts: 25.9 us -> 0.83 us
    ppermute x0 -> x9, waiting for transfers between devices: none -> 22.2 us  [shifted(): return lax.ppermute(value, 'resp', [(i, (i + shift) % n) for i in range(n)])]
    psum x1 -> x0, blocking collectives: 12 us -> none  [on_device(): lax.psum(jnp.sum(loss_terms), 'resp') / count_real]
    pallas_call x0 -> x1, Pallas kernels: none -> 8.26 us  [on_device(): pl.pallas_call(functools.partial(attention_kernel, n), out_shape=out_shape)]
    reshape x4 -> x0, local copies, waits for them, and re-layouts: 5.78 us -> none  [own_scores(): jnp.where(causal[None, :, None, :], scores, masked_score)]
  transfers between devices with their start and end apart: 2 -> 9, of which waited for: 0 -> 3; matrix products, arithmetic and copies ran while one was open for 29% -> 1% of each run, Pallas kernels for 0% -> 0%
where the time goes in v1:
time: 73.3 us; the launch traced here: 73.1 us
  starting transfers between devices  31.7 us (43%)
  waiting for transfers between devices  22.2 us (30%)
  Pallas kernels  8.26 us (11%)
  between operations  6.66 us (9%)
  other arithmetic  2.72 us (4%)
  local copies, waits for them, and re-layouts  1.55 us (2%)
    ppermute x9, starting transfers between devices, shifted(): return lax.ppermute(value, 'resp', [(i, (i + shift) % n) for i in range(n)])  31.7 us
    ppermute x9, waiting for transfers between devices, shifted(): return lax.ppermute(value, 'resp', [(i, (i + shift) % n) for i in range(n)])  22.2 us
    pallas_call x1, Pallas kernels, on_device(): pl.pallas_call(functools.partial(attention_kernel, n), out_shape=out_shape)  8.26 us
  transfers between devices with their start and end apart: 9, of which 3 were waited for; matrix products, arithmetic and copies ran while one was open for 1% of the time, Pallas kernels for 0%

profile of v1, /device:TPU:0, one launch (start us, length us, event | category | flops | bytes accessed | tf_op | source)
XLA Modules:
  0.0 73.1 jit_solution(3991599116554855940)
XLA Ops:
  0.6 1.0 %pad_maximum_fusion.rest_0_ = bf16[128,1024]{1,0:T(8,128)(2,1)S(1)} fusion(bf16[128,512]{1,0:T(8,128)(2,1)} %bitcast.20, bf16[128,512]{1,0:T(8,128)(2,1)} %bitcast.21), kind=kLoop, calls=%fused_computation.1 | loop fusion | flops 524288 | bytes 524288 | tf_op jit(solution)/shard_map/concatenate | solution.py:115
  1.6 0.0 copy-start
  1.6 5.1 %collective-permute-start.2 = (bf16[128,1024]{1,0:T(8,128)(2,1)S(1)}, bf16[128,1024]{1,0:T(8,128)(2,1)S(1)}, u32[]{:S(2)}, u32[]{:S(2)}) collective-permute-start(bf16[128,1024]{1,0:T(8,128)(2,1)S(1)} %pad_maximum_fusion.rest_0_), channel_id=1, source_target_pairs={{0,3},{1,0},{2,1},{3,2},{4,7},{5,4},{6,5},{7,6},{8,11},{9,8},{10,9... | collective-permute-start | bytes 786440 | tf_op jit(solution)/shard_map/ppermute | solution.py:94
  6.7 0.0 collective-permute-start.1
  6.7 1.0 %collective-permute-start = (bf16[128,1024]{1,0:T(8,128)(2,1)S(1)}, bf16[128,1024]{1,0:T(8,128)(2,1)S(1)}, u32[]{:S(2)}, u32[]{:S(2)}) collective-permute-start(bf16[128,1024]{1,0:T(8,128)(2,1)S(1)} %pad_maximum_fusion.rest_0_), channel_id=1, source_target_pairs={{0,1},{1,2},{2,3},{3,0},{4,5},{5,6},{6,7},{7,4},{8,9},{9,10},{10,1... | collective-permute-start | bytes 786440 | tf_op jit(solution)/shard_map/ppermute | solution.py:94
  10.5 0.6 fusion.factor_ref
  11.1 2.4 %collective-permute-done.2.rest_3_ = bf16[128,1024]{1,0:T(8,128)(2,1)S(1)} collective-permute-done((bf16[128,1024]{1,0:T(8,128)(2,1)S(1)}, bf16[128,1024]{1,0:T(8,128)(2,1)S(1)}, u32[]{:S(2)}, u32[]{:S(2)}) %collective-permute-start.2) | collective-permute-done | bytes 262176 | tf_op jit(solution)/shard_map/ppermute | solution.py:94
  13.5 0.0 copy-start.1
  13.5 15.6 %collective-permute-done.1.rest_2_ = bf16[128,1024]{1,0:T(8,128)(2,1)S(1)} collective-permute-done((bf16[128,1024]{1,0:T(8,128)(2,1)S(1)}, bf16[128,1024]{1,0:T(8,128)(2,1)S(1)}, u32[]{:S(2)}, u32[]{:S(2)}) %collective-permute-start.1) | collective-permute-done | bytes 262176 | tf_op jit(solution)/shard_map/ppermute | solution.py:94
  29.0 0.0 copy-start.2
  29.1 0.0 collective-permute-done.rest_1_
  29.1 0.0 copy-start.3
  29.1 0.0 copy-done
  29.1 0.0 copy-done.1
  29.1 0.7 copy-done.2
  29.8 0.1 copy-done.3
  29.9 8.3 %shard_map.145 = (bf16[32,8192]{1,0:T(8,128)(2,1)}, bf16[32,512]{1,0:T(8,128)(2,1)}, bf16[32,512]{1,0:T(8,128)(2,1)}, bf16[128,1024]{1,0:T(8,128)(2,1)}, bf16[12...) custom-call(f32[32,1]{1,0:T(8,128)} %fusion.factor_ref, bf16[32,8192]{1,0:T(8,128)(2,1)} %bitcast.18, ...), custom_call_target="tpu_custom_call" | custom-call | tf_op jit(solution)/shard_map/pallas_call | solution.py:134
  38.2 0.0 collective-permute-start.3
  38.2 2.7 %collective-permute-start.4 = (bf16[128,1024]{1,0:T(8,128)(2,1)}, bf16[128,1024]{1,0:T(8,128)(2,1)S(1)}, u32[]{:S(2)}, u32[]{:S(2)}) collective-permute-start(bf16[128,1024]{1,0:T(8,128)(2,1)} %get-tuple-element.18), channel_id=1, source_target_pairs={{0,2},{1,3},{2,0},{3,1},{4,6},{5,7},{6,4},{7,5},{8,10},{9,11},{10,... | collective-permute-start | bytes 786440 | tf_op jit(solution)/shard_map/ppermute | solution.py:94
  40.8 2.0 %collective-permute-start.5 = (bf16[128,1024]{1,0:T(8,128)(2,1)}, bf16[128,1024]{1,0:T(8,128)(2,1)S(1)}, u32[]{:S(2)}, u32[]{:S(2)}) collective-permute-start(bf16[128,1024]{1,0:T(8,128)(2,1)} %get-tuple-element.19), channel_id=1, source_target_pairs={{0,1},{1,2},{2,3},{3,0},{4,5},{5,6},{6,7},{7,4},{8,9},{9,10},{10,1... | collective-permute-start | bytes 786440 | tf_op jit(solution)/shard_map/ppermute | solution.py:94
  42.9 11.8 %collective-permute-start.8 = (f32[1]{0:T(128)}, f32[1]{0:T(128)}, u32[]{:S(2)}, u32[]{:S(2)}) collective-permute-start(f32[1]{0:T(128)} %select_n.27), channel_id=1, source_target_pairs={{0,3},{1,0},{2,1},{3,2},{4,7},{5,4},{6,5},{7,6},{8,11},{9,8},{10,9... | collective-permute-start | bytes 20 | tf_op jit(solution)/shard_map/ppermute | solution.py:94
  54.8 1.3 %collective-permute-start.6 = (f32[1]{0:T(128)}, f32[1]{0:T(128)}, u32[]{:S(2)}, u32[]{:S(2)}) collective-permute-start(f32[1]{0:T(128)} %select_n.27), channel_id=1, source_target_pairs={{0,1},{1,2},{2,3},{3,0},{4,5},{5,6},{6,7},{7,4},{8,9},{9,10},{10,1... | collective-permute-start | bytes 20 | tf_op jit(solution)/shard_map/ppermute | solution.py:94
  56.1 4.2 %collective-permute-done.6 = f32[1]{0:T(128)} collective-permute-done((f32[1]{0:T(128)}, f32[1]{0:T(128)}, u32[]{:S(2)}, u32[]{:S(2)}) %collective-permute-start.6) | collective-permute-done | bytes 36 | tf_op jit(solution)/shard_map/ppermute | solution.py:94
  60.3 7.7 %collective-permute-start.7 = (f32[1]{0:T(128)}, f32[1]{0:T(128)}, u32[]{:S(2)}, u32[]{:S(2)}) collective-permute-start(f32[1]{0:T(128)} %select_n.27), channel_id=1, source_target_pairs={{0,2},{1,3},{2,0},{3,1},{4,6},{5,7},{6,4},{7,5},{8,10},{9,11},{10,... | collective-permute-start | bytes 20 | tf_op jit(solution)/shard_map/ppermute | solution.py:94
  68.7 0.0 collective-permute-done.7
  69.3 0.0 collective-permute-done.8
  70.1 0.0 collective-permute-done.3
  70.1 0.0 collective-permute-done.4
  70.1 0.0 collective-permute-done.5
  70.1 1.1 %add_convert_fusion = bf16[128,1024]{1,0:T(8,128)(2,1)S(1)} fusion(bf16[128,1024]{1,0:T(8,128)(2,1)S(1)} %collective-permute-done.5, bf16[128,1024]{1,0:T(8,128)(2,1)S(1)} %collective-permute-done.4, bf16[128,1024]{1,0:T(8,128)(2,1)S(1)} %collective-permute-done.3, bf16[128,1024]{1,0:T(8,128)(2,1)} %get-tuple-element.16), kind=kLoop, calls=%fused_computation | loop fusion | flops 1048576 | bytes 1310720 | tf_op jit(solution)/shard_map/convert_element_type | solution.py:143
  71.2 0.7 slice_bitcast_fusion
Async XLA Ops:
  1.6 27.4 %copy-start = (bf16[128,1024]{1,0:T(8,128)(2,1)}, bf16[128,1024]{1,0:T(8,128)(2,1)S(1)}, u32[]{:S(2)}) copy-start(bf16[128,1024]{1,0:T(8,128)(2,1)S(1)} %pad_maximum_fusion.rest_0_) | copy-start | bytes 786436
  1.6 11.9 %collective-permute-start.2 = (bf16[128,1024]{1,0:T(8,128)(2,1)S(1)}, bf16[128,1024]{1,0:T(8,128)(2,1)S(1)}, u32[]{:S(2)}, u32[]{:S(2)}) collective-permute-start(bf16[128,1024]{1,0:T(8,128)(2,1)S(1)} %pad_maximum_fusion.rest_0_), channel_id=1, source_target_pairs={{0,3},{1,0},{2,1},{3,2},{4,7},{5,4},{6,5},{7,6},{8,11},{9,8},{10,9... | collective-permute-start | bytes 786440 | tf_op jit(solution)/shard_map/ppermute | solution.py:94
  6.7 22.3 %collective-permute-start.1 = (bf16[128,1024]{1,0:T(8,128)(2,1)S(1)}, bf16[128,1024]{1,0:T(8,128)(2,1)S(1)}, u32[]{:S(2)}, u32[]{:S(2)}) collective-permute-start(bf16[128,1024]{1,0:T(8,128)(2,1)S(1)} %pad_maximum_fusion.rest_0_), channel_id=1, source_target_pairs={{0,2},{1,3},{2,0},{3,1},{4,6},{5,7},{6,4},{7,5},{8,10},{9,11},{10,... | collective-permute-start | bytes 786440 | tf_op jit(solution)/shard_map/ppermute | solution.py:94
  6.7 22.3 %collective-permute-start = (bf16[128,1024]{1,0:T(8,128)(2,1)S(1)}, bf16[128,1024]{1,0:T(8,128)(2,1)S(1)}, u32[]{:S(2)}, u32[]{:S(2)}) collective-permute-start(bf16[128,1024]{1,0:T(8,128)(2,1)S(1)} %pad_maximum_fusion.rest_0_), channel_id=1, source_target_pairs={{0,1},{1,2},{2,3},{3,0},{4,5},{5,6},{6,7},{7,4},{8,9},{9,10},{10,1... | collective-permute-start | bytes 786440 | tf_op jit(solution)/shard_map/ppermute | solution.py:94
  13.5 15.6 %copy-start.1 = (bf16[128,1024]{1,0:T(8,128)(2,1)}, bf16[128,1024]{1,0:T(8,128)(2,1)S(1)}, u32[]{:S(2)}) copy-start(bf16[128,1024]{1,0:T(8,128)(2,1)S(1)} %collective-permute-done.2.rest_3_) | copy-start | bytes 786436
  29.0 0.7 copy-start.2
  29.1 0.8 %copy-start.3 = (bf16[128,1024]{1,0:T(8,128)(2,1)}, bf16[128,1024]{1,0:T(8,128)(2,1)S(1)}, u32[]{:S(2)}) copy-start(bf16[128,1024]{1,0:T(8,128)(2,1)S(1)} %collective-permute-done.rest_1_) | copy-start | bytes 786436
  38.2 31.9 %collective-permute-start.3 = (bf16[128,1024]{1,0:T(8,128)(2,1)}, bf16[128,1024]{1,0:T(8,128)(2,1)S(1)}, u32[]{:S(2)}, u32[]{:S(2)}) collective-permute-start(bf16[128,1024]{1,0:T(8,128)(2,1)} %get-tuple-element.17), channel_id=1, source_target_pairs={{0,3},{1,0},{2,1},{3,2},{4,7},{5,4},{6,5},{7,6},{8,11},{9,8},{10,9... | collective-permute-start | bytes 786440 | tf_op jit(solution)/shard_map/ppermute | solution.py:94
  38.2 31.9 %collective-permute-start.4 = (bf16[128,1024]{1,0:T(8,128)(2,1)}, bf16[128,1024]{1,0:T(8,128)(2,1)S(1)}, u32[]{:S(2)}, u32[]{:S(2)}) collective-permute-start(bf16[128,1024]{1,0:T(8,128)(2,1)} %get-tuple-element.18), channel_id=1, source_target_pairs={{0,2},{1,3},{2,0},{3,1},{4,6},{5,7},{6,4},{7,5},{8,10},{9,11},{10,... | collective-permute-start | bytes 786440 | tf_op jit(solution)/shard_map/ppermute | solution.py:94
  40.8 29.2 %collective-permute-start.5 = (bf16[128,1024]{1,0:T(8,128)(2,1)}, bf16[128,1024]{1,0:T(8,128)(2,1)S(1)}, u32[]{:S(2)}, u32[]{:S(2)}) collective-permute-start(bf16[128,1024]{1,0:T(8,128)(2,1)} %get-tuple-element.19), channel_id=1, source_target_pairs={{0,1},{1,2},{2,3},{3,0},{4,5},{5,6},{6,7},{7,4},{8,9},{9,10},{10,1... | collective-permute-start | bytes 786440 | tf_op jit(solution)/shard_map/ppermute | solution.py:94
  42.9 26.4 %collective-permute-start.8 = (f32[1]{0:T(128)}, f32[1]{0:T(128)}, u32[]{:S(2)}, u32[]{:S(2)}) collective-permute-start(f32[1]{0:T(128)} %select_n.27), channel_id=1, source_target_pairs={{0,3},{1,0},{2,1},{3,2},{4,7},{5,4},{6,5},{7,6},{8,11},{9,8},{10,9... | collective-permute-start | bytes 20 | tf_op jit(solution)/shard_map/ppermute | solution.py:94
  54.8 5.5 %collective-permute-start.6 = (f32[1]{0:T(128)}, f32[1]{0:T(128)}, u32[]{:S(2)}, u32[]{:S(2)}) collective-permute-start(f32[1]{0:T(128)} %select_n.27), channel_id=1, source_target_pairs={{0,1},{1,2},{2,3},{3,0},{4,5},{5,6},{6,7},{7,4},{8,9},{9,10},{10,1... | collective-permute-start | bytes 20 | tf_op jit(solution)/shard_map/ppermute | solution.py:94
  60.3 8.4 %collective-permute-start.7 = (f32[1]{0:T(128)}, f32[1]{0:T(128)}, u32[]{:S(2)}, u32[]{:S(2)}) collective-permute-start(f32[1]{0:T(128)} %select_n.27), channel_id=1, source_target_pairs={{0,2},{1,3},{2,0},{3,1},{4,6},{5,7},{6,4},{7,5},{8,10},{9,11},{10,... | collective-permute-start | bytes 20 | tf_op jit(solution)/shard_map/ppermute | solution.py:94

commit v2 on v1

--- a/solution.py
+++ b/solution.py
@@ -17,15 +17,26 @@
 masked_score = -1e30
 
 
-def attention_kernel(n_pieces, factor_ref, q_ref, cot_ref, kown_ref, vown_ref, *rest):
-    piece_refs = rest[:n_pieces]
-    dq_ref, dkown_ref, dvown_ref = rest[n_pieces:n_pieces + 3]
-    part_refs = rest[n_pieces + 3:]
+def slot_columns(refs, columns):
+    if len(refs) == 1:
+        return refs[0][:, columns]
+    total = refs[0][:, columns].astype(jnp.float32)
+    for r in refs[1:]:
+        total = total + r[:, columns].astype(jnp.float32)
+    return total.astype(jnp.bfloat16)
+
+
+def attention_kernel(slot_spec, factor_ref, q_ref, cot_ref, kown_ref, vown_ref, *rest):
+    n_inputs = sum(len(s) for s in slot_spec)
+    input_refs = rest[:n_inputs]
+    piece_refs = [[input_refs[i] for i in s] for s in slot_spec]
+    dq_ref, dkown_ref, dvown_ref = rest[n_inputs:n_inputs + 3]
+    part_refs = rest[n_inputs + 3:]
     group_size = HEADS // KV_HEADS
     group_width = group_size * HEAD_DIM
     kv_width = KV_HEADS * HEAD_DIM
     resp_len = q_ref.shape[0]
-    piece_len = piece_refs[0].shape[0]
+    piece_len = input_refs[0].shape[0]
     scaling = 1.0 / math.sqrt(HEAD_DIM)
     rows = group_size * resp_len
     factor = factor_ref[...]
@@ -50,8 +61,8 @@
         )
         k_cols = slice(g * HEAD_DIM, (g + 1) * HEAD_DIM)
         v_cols = slice(kv_width + g * HEAD_DIM, kv_width + (g + 1) * HEAD_DIM)
-        k_pre = jnp.concatenate([r[:, k_cols] for r in piece_refs], axis=0)
-        v_pre = jnp.concatenate([r[:, v_cols] for r in piece_refs], axis=0)
+        k_pre = jnp.concatenate([slot_columns(r, k_cols) for r in piece_refs], axis=0)
+        v_pre = jnp.concatenate([slot_columns(r, v_cols) for r in piece_refs], axis=0)
         k_own = kown_ref[:, k_cols]
         v_own = vown_ref[:, k_cols]
         s_pre = lax.dot_general(q_rows, k_pre, contract_cols, preferred_element_type=jnp.float32) * scaling
@@ -92,6 +103,41 @@
 
 def shifted(value, shift, n):
     return lax.ppermute(value, "resp", [(i, (i + shift) % n) for i in range(n)])
+
+
+def moved(value, pairs):
+    return lax.ppermute(value, "resp", pairs)
+
+
+def line_pairs(n, shift):
+    return [(i, i + shift) for i in range(n) if 0 <= i + shift < n]
+
+
+def gather_line4(local):
+    right_one = moved(local, line_pairs(4, 1))
+    left_one = moved(local, line_pairs(4, -1))
+    right_two = moved(local, line_pairs(4, 2))
+    left_two = moved(local, line_pairs(4, -2))
+    fwd_right = moved(right_two, [(2, 3)])
+    fwd_left = moved(left_two, [(1, 0)])
+    return [local, (right_one, fwd_left), (left_one, fwd_right), (right_two, left_two)]
+
+
+def scatter_line4(parts):
+    own, slot_one, slot_two, slot_three = parts
+    fwd_right = moved(slot_one, [(0, 1)])
+    fwd_left = moved(slot_two, [(3, 2)])
+    left_one = moved(slot_one, line_pairs(4, -1))
+    right_one = moved(slot_two, line_pairs(4, 1))
+    merged = (
+        slot_three.astype(jnp.float32) + fwd_right.astype(jnp.float32) + fwd_left.astype(jnp.float32)
+    ).astype(jnp.bfloat16)
+    right_two = moved(merged, line_pairs(4, 2))
+    left_two = moved(merged, line_pairs(4, -2))
+    total = own.astype(jnp.float32)
+    for piece in (left_one, right_one, right_two, left_two):
+        total = total + piece.astype(jnp.float32)
+    return total
 
 
 def on_device(
@@ -113,7 +159,16 @@
     piece_len = prefix_keys.shape[1]
     kv_width = KV_HEADS * HEAD_DIM
     local_kv = jnp.concatenate([prefix_keys[0], prefix_values[0]], axis=1)
-    pieces = [local_kv] + [shifted(local_kv, k, n) for k in range(1, n)]
+    if n == 4:
+        slots = gather_line4(local_kv)
+    else:
+        slots = [local_kv] + [shifted(local_kv, k, n) for k in range(1, n)]
+    slots = [s if isinstance(s, tuple) else (s,) for s in slots]
+    slot_spec = []
+    pieces = []
+    for s in slots:
+        slot_spec.append(tuple(range(len(pieces), len(pieces) + len(s))))
+        pieces.extend(s)
     live_count = counts[0]
     count_real = live_count.astype(jnp.float32)
     slot_ids = lax.axis_index("resp") * slot_count + jnp.arange(slot_count, dtype=jnp.int32)
@@ -126,20 +181,24 @@
     positions = jnp.arange(resp_len, dtype=jnp.int32)
     factor = jnp.where(positions[None, :] < lengths[0][:, None], weight[:, None], 0.0)
     factor = factor.reshape(resp_len, 1).astype(jnp.float32)
+    forget_loss, factor, *pieces = lax.optimization_barrier((forget_loss, factor, *pieces))
     out_shape = (
         jax.ShapeDtypeStruct(queries.shape[2:], jnp.bfloat16),
         jax.ShapeDtypeStruct(resp_keys.shape[2:], jnp.bfloat16),
         jax.ShapeDtypeStruct(resp_values.shape[2:], jnp.bfloat16),
     ) + tuple(jax.ShapeDtypeStruct((piece_len, 2 * kv_width), jnp.bfloat16) for _ in range(n))
     results = pl.pallas_call(
-        functools.partial(attention_kernel, n),
+        functools.partial(attention_kernel, tuple(slot_spec)),
         out_shape=out_shape,
     )(factor, queries[0, 0], cotangent[0, 0], resp_keys[0, 0], resp_values[0, 0], *pieces)
     grad_q, grad_k, grad_v = results[:3]
     parts = results[3:]
-    summed = parts[0].astype(jnp.float32)
-    for k in range(1, n):
-        summed = summed + shifted(parts[k], -k, n).astype(jnp.float32)
+    if n == 4:
+        summed = scatter_line4(parts)
+    else:
+        summed = parts[0].astype(jnp.float32)
+        for k in range(1, n):
+            summed = summed + shifted(parts[k], -k, n).astype(jnp.float32)
     summed = summed.astype(jnp.bfloat16)
     return (
         grad_q[None, None],

time: 73.3 us -> 77.6 us (1.059); the launches traced: 73.1 us -> 76.4 us
  starting transfers between devices: 31.7 us -> 39.2 us
  waiting for transfers between devices: 22.2 us -> 17.5 us
    ppermute x0 -> x12, starting transfers between devices: none -> 31.1 us  [moved(): return lax.ppermute(value, 'resp', pairs)]
    ppermute x9 -> x3, starting transfers between devices: 31.7 us -> 8.01 us  [shifted(): return lax.ppermute(value, 'resp', [(i, (i + shift) % n) for i in range(n)])]
    ppermute x9 -> x3, waiting for transfers between devices: 22.2 us -> 2.79 us  [shifted(): return lax.ppermute(value, 'resp', [(i, (i + shift) % n) for i in range(n)])]
    ppermute x0 -> x12, waiting for transfers between devices: none -> 14.7 us  [moved(): return lax.ppermute(value, 'resp', pairs)]
    convert_element_type x0 -> x1, other arithmetic: none -> 1.11 us  [scatter_line4(): merged = (slot_three.astype(jnp.float32) + fwd_right.astype(jnp.float32)...]
    convert_element_type x1, other arithmetic: 1.12 us -> 0.22 us  [on_device(): summed = summed.astype(jnp.bfloat16)]
  transfers between devices with their start and end apart: 9 -> 15, of which waited for: 3 -> 4; matrix products, arithmetic and copies ran while one was open for 1% -> 2% of each run, Pallas kernels for 0% -> 0%
where the time goes in v2:
time: 77.6 us; the launch traced here: 76.4 us
  starting transfers between devices  39.2 us (51%)
  waiting for transfers between devices  17.5 us (23%)
  Pallas kernels  8.5 us (11%)
  between operations  6.74 us (9%)
  other arithmetic  2.93 us (4%)
  local copies, waits for them, and re-layouts  1.64 us (2%)
    ppermute x12, starting transfers between devices, moved(): return lax.ppermute(value, 'resp', pairs)  31.1 us
    ppermute x12, waiting for transfers between devices, moved(): return lax.ppermute(value, 'resp', pairs)  14.7 us
    pallas_call x1, Pallas kernels, on_device(): pl.pallas_call(functools.partial(attention_kernel, tuple(slot_spec)), out...  8.5 us
    ppermute x3, starting transfers between devices, shifted(): return lax.ppermute(value, 'resp', [(i, (i + shift) % n) for i in range(n)])  8.01 us
    ppermute x3, waiting for transfers between devices, shifted(): return lax.ppermute(value, 'resp', [(i, (i + shift) % n) for i in range(n)])  2.79 us
  transfers between devices with their start and end apart: 15, of which 4 were waited for; matrix products, arithmetic and copies ran while one was open for 2% of the time, Pallas kernels for 0%

profile of v2, /device:TPU:0, one launch (start us, length us, event | category | flops | bytes accessed | tf_op | source)
XLA Modules:
  0.0 76.4 jit_solution(2768560034261607293)
XLA Ops:
  0.6 1.0 %pad_maximum_fusion.rest_0_ = bf16[128,1024]{1,0:T(8,128)(2,1)S(1)} fusion(bf16[128,512]{1,0:T(8,128)(2,1)} %bitcast.20, bf16[128,512]{1,0:T(8,128)(2,1)} %bitcast.21), kind=kLoop, calls=%fused_computation.2 | loop fusion | flops 524288 | bytes 524288 | tf_op jit(solution)/shard_map/concatenate | solution.py:161
  1.6 6.0 %collective-permute-start.7 = (bf16[128,1024]{1,0:T(8,128)(2,1)S(1)}, bf16[128,1024]{1,0:T(8,128)(2,1)S(1)}, u32[]{:S(2)}, u32[]{:S(2)}) collective-permute-start(bf16[128,1024]{1,0:T(8,128)(2,1)S(1)} %pad_maximum_fusion.rest_0_), channel_id=1, source_target_pairs={{0,2},{1,3},{4,6},{5,7},{8,10},{9,11},{12,14},{13,15},{16,18},{17,... | collective-permute-start | bytes 786440 | tf_op jit(solution)/shard_map/ppermute | solution.py:109
  7.6 1.3 %collective-permute-start.4 = (bf16[128,1024]{1,0:T(8,128)(2,1)S(1)}, bf16[128,1024]{1,0:T(8,128)(2,1)S(1)}, u32[]{:S(2)}, u32[]{:S(2)}) collective-permute-start(bf16[128,1024]{1,0:T(8,128)(2,1)S(1)} %pad_maximum_fusion.rest_0_), channel_id=1, source_target_pairs={{2,0},{3,1},{6,4},{7,5},{10,8},{11,9},{14,12},{15,13},{18,16},{19,... | collective-permute-start | bytes 786440 | tf_op jit(solution)/shard_map/ppermute | solution.py:109
  8.9 1.3 %collective-permute-start.6 = (bf16[128,1024]{1,0:T(8,128)(2,1)S(1)}, bf16[128,1024]{1,0:T(8,128)(2,1)S(1)}, u32[]{:S(2)}, u32[]{:S(2)}) collective-permute-start(bf16[128,1024]{1,0:T(8,128)(2,1)S(1)} %pad_maximum_fusion.rest_0_), channel_id=1, source_target_pairs={{1,0},{2,1},{3,2},{5,4},{6,5},{7,6},{9,8},{10,9},{11,10},{13,12},{... | collective-permute-start | bytes 786440 | tf_op jit(solution)/shard_map/ppermute | solution.py:109
  10.2 4.6 %collective-permute-start.3 = (bf16[128,1024]{1,0:T(8,128)(2,1)S(1)}, bf16[128,1024]{1,0:T(8,128)(2,1)S(1)}, u32[]{:S(2)}, u32[]{:S(2)}) collective-permute-start(bf16[128,1024]{1,0:T(8,128)(2,1)S(1)} %pad_maximum_fusion.rest_0_), channel_id=1, source_target_pairs={{0,1},{1,2},{2,3},{4,5},{5,6},{6,7},{8,9},{9,10},{10,11},{12,13},{... | collective-permute-start | bytes 786440 | tf_op jit(solution)/shard_map/ppermute | solution.py:109
  14.8 0.0 collective-permute-done.7.rest_5_
  14.8 0.7 collective-permute-start.8
  15.5 9.5 %collective-permute-done.4.rest_6_ = bf16[128,1024]{1,0:T(8,128)(2,1)S(1)} collective-permute-done((bf16[128,1024]{1,0:T(8,128)(2,1)S(1)}, bf16[128,1024]{1,0:T(8,128)(2,1)S(1)}, u32[]{:S(2)}, u32[]{:S(2)}) %collective-permute-start.4) | collective-permute-done | bytes 262176 | tf_op jit(solution)/shard_map/ppermute | solution.py:109
  24.9 1.3 %collective-permute-start.5 = (bf16[128,1024]{1,0:T(8,128)(2,1)S(1)}, bf16[128,1024]{1,0:T(8,128)(2,1)S(1)}, u32[]{:S(2)}, u32[]{:S(2)}) collective-permute-start(bf16[128,1024]{1,0:T(8,128)(2,1)S(1)} %collective-permute-done.4.rest_6_), channel_id=1, source_target_pairs={{1,0},{5,4},{9,8},{13,12},{17,16},{21,20},{25,24},{29,28}} | collective-permute-start | bytes 786440 | tf_op jit(solution)/shard_map/ppermute | solution.py:109
  28.3 4.0 %collective-permute-start = (f32[1]{0:T(128)}, f32[1]{0:T(128)}, u32[]{:S(2)}, u32[]{:S(2)}) collective-permute-start(f32[1]{0:T(128)} %select_n.25), channel_id=1, source_target_pairs={{0,1},{1,2},{2,3},{3,0},{4,5},{5,6},{6,7},{7,4},{8,9},{9,10},{10,1... | collective-permute-start | bytes 20 | tf_op jit(solution)/shard_map/ppermute | solution.py:105
  33.0 0.6 fusion.factor_ref
  33.7 1.5 %collective-permute-start.1 = (f32[1]{0:T(128)}, f32[1]{0:T(128)}, u32[]{:S(2)}, u32[]{:S(2)}) collective-permute-start(f32[1]{0:T(128)} %select_n.25), channel_id=1, source_target_pairs={{0,2},{1,3},{2,0},{3,1},{4,6},{5,7},{6,4},{7,5},{8,10},{9,11},{10,... | collective-permute-start | bytes 20 | tf_op jit(solution)/shard_map/ppermute | solution.py:105
  35.8 2.4 %collective-permute-done.1 = f32[1]{0:T(128)} collective-permute-done((f32[1]{0:T(128)}, f32[1]{0:T(128)}, u32[]{:S(2)}, u32[]{:S(2)}) %collective-permute-start.1) | collective-permute-done | bytes 36 | tf_op jit(solution)/shard_map/ppermute | solution.py:105
  38.2 2.5 %collective-permute-start.2 = (f32[1]{0:T(128)}, f32[1]{0:T(128)}, u32[]{:S(2)}, u32[]{:S(2)}) collective-permute-start(f32[1]{0:T(128)} %select_n.25), channel_id=1, source_target_pairs={{0,3},{1,0},{2,1},{3,2},{4,7},{5,4},{6,5},{7,6},{8,11},{9,8},{10,9... | collective-permute-start | bytes 20 | tf_op jit(solution)/shard_map/ppermute | solution.py:105
  41.3 0.4 collective-permute-done.2
  42.4 0.0 collective-permute-done.6.rest_3_
  42.4 0.0 collective-permute-done.3.rest_1_
  42.5 0.6 copy-done.3
  43.1 0.1 copy-done.4
  43.2 0.1 copy-done.5
  43.3 0.1 copy-done.6
  43.4 8.5 %shard_map.145 = (bf16[32,8192]{1,0:T(8,128)(2,1)}, bf16[32,512]{1,0:T(8,128)(2,1)}, bf16[32,512]{1,0:T(8,128)(2,1)}, bf16[128,1024]{1,0:T(8,128)(2,1)}, bf16[12...) custom-call(f32[32,1]{1,0:T(8,128)} %fusion.factor_ref, bf16[32,8192]{1,0:T(8,128)(2,1)} %bitcast.18, ...), custom_call_target="tpu_custom_call" | custom-call | tf_op jit(solution)/shard_map/pallas_call | solution.py:190
  51.9 2.7 %collective-permute-start.11 = (bf16[128,1024]{1,0:T(8,128)(2,1)}, bf16[128,1024]{1,0:T(8,128)(2,1)S(1)}, u32[]{:S(2)}, u32[]{:S(2)}) collective-permute-start(bf16[128,1024]{1,0:T(8,128)(2,1)} %get-tuple-element.34), channel_id=1, source_target_pairs={{0,1},{4,5},{8,9},{12,13},{16,17},{20,21},{24,25},{28,29}} | collective-permute-start | bytes 786440 | tf_op jit(solution)/shard_map/ppermute | solution.py:109
  54.6 0.7 collective-permute-start.12
  55.3 1.3 %collective-permute-start.9 = (bf16[128,1024]{1,0:T(8,128)(2,1)}, bf16[128,1024]{1,0:T(8,128)(2,1)S(1)}, u32[]{:S(2)}, u32[]{:S(2)}) collective-permute-start(bf16[128,1024]{1,0:T(8,128)(2,1)} %get-tuple-element.34), channel_id=1, source_target_pairs={{1,0},{2,1},{3,2},{5,4},{6,5},{7,6},{9,8},{10,9},{11,10},{13,12},{... | collective-permute-start | bytes 786440 | tf_op jit(solution)/shard_map/ppermute | solution.py:109
  56.6 4.6 %collective-permute-start.10 = (bf16[128,1024]{1,0:T(8,128)(2,1)}, bf16[128,1024]{1,0:T(8,128)(2,1)S(1)}, u32[]{:S(2)}, u32[]{:S(2)}) collective-permute-start(bf16[128,1024]{1,0:T(8,128)(2,1)} %get-tuple-element.35), channel_id=1, source_target_pairs={{0,1},{1,2},{2,3},{4,5},{5,6},{6,7},{8,9},{9,10},{10,11},{12,13},{... | collective-permute-start | bytes 786440 | tf_op jit(solution)/shard_map/ppermute | solution.py:109
  61.2 1.1 %add_convert_fusion.1 = bf16[128,1024]{1,0:T(8,128)(2,1)S(1)} fusion(bf16[128,1024]{1,0:T(8,128)(2,1)S(1)} %collective-permute-done.12, bf16[128,1024]{1,0:T(8,128)(2,1)S(1)} %collective-permute-done.11, bf16[128,1024]{1,0:T(8,128)(2,1)} %get-tuple-element.36), kind=kLoop, calls=%fused_computation.1 | loop fusion | flops 786432 | bytes 1048576 | tf_op jit(solution)/shard_map/convert_element_type | solution.py:134
  62.3 1.3 %collective-permute-start.14 = (bf16[128,1024]{1,0:T(8,128)(2,1)S(1)}, bf16[128,1024]{1,0:T(8,128)(2,1)S(1)}, u32[]{:S(2)}, u32[]{:S(2)}) collective-permute-start(bf16[128,1024]{1,0:T(8,128)(2,1)S(1)} %add_convert_fusion.1), channel_id=1, source_target_pairs={{2,0},{3,1},{6,4},{7,5},{10,8},{11,9},{14,12},{15,13},{18,16},{19,... | collective-permute-start | bytes 786440 | tf_op jit(solution)/shard_map/ppermute | solution.py:109
  63.6 5.5 %collective-permute-start.13 = (bf16[128,1024]{1,0:T(8,128)(2,1)S(1)}, bf16[128,1024]{1,0:T(8,128)(2,1)S(1)}, u32[]{:S(2)}, u32[]{:S(2)}) collective-permute-start(bf16[128,1024]{1,0:T(8,128)(2,1)S(1)} %add_convert_fusion.1), channel_id=1, source_target_pairs={{0,2},{1,3},{4,6},{5,7},{8,10},{9,11},{12,14},{13,15},{16,18},{17,... | collective-permute-start | bytes 786440 | tf_op jit(solution)/shard_map/ppermute | solution.py:109
  69.2 5.2 %collective-permute-done.14 = bf16[128,1024]{1,0:T(8,128)(2,1)S(1)} collective-permute-done((bf16[128,1024]{1,0:T(8,128)(2,1)S(1)}, bf16[128,1024]{1,0:T(8,128)(2,1)S(1)}, u32[]{:S(2)}, u32[]{:S(2)}) %collective-permute-start.14) | collective-permute-done | bytes 262176 | tf_op jit(solution)/shard_map/ppermute | solution.py:109
  74.4 0.2 add_convert_fusion
  74.6 0.7 slice_bitcast_fusion
  (20 shorter events, 0.0 us)
Async XLA Ops:
  1.6 40.8 %copy-start = (bf16[128,1024]{1,0:T(8,128)(2,1)}, bf16[128,1024]{1,0:T(8,128)(2,1)S(1)}, u32[]{:S(2)}) copy-start(bf16[128,1024]{1,0:T(8,128)(2,1)S(1)} %pad_maximum_fusion.rest_0_) | copy-start | bytes 786436
  1.6 13.1 %collective-permute-start.7 = (bf16[128,1024]{1,0:T(8,128)(2,1)S(1)}, bf16[128,1024]{1,0:T(8,128)(2,1)S(1)}, u32[]{:S(2)}, u32[]{:S(2)}) collective-permute-start(bf16[128,1024]{1,0:T(8,128)(2,1)S(1)} %pad_maximum_fusion.rest_0_), channel_id=1, source_target_pairs={{0,2},{1,3},{4,6},{5,7},{8,10},{9,11},{12,14},{13,15},{16,18},{17,... | collective-permute-start | bytes 786440 | tf_op jit(solution)/shard_map/ppermute | solution.py:109
  7.6 17.3 %collective-permute-start.4 = (bf16[128,1024]{1,0:T(8,128)(2,1)S(1)}, bf16[128,1024]{1,0:T(8,128)(2,1)S(1)}, u32[]{:S(2)}, u32[]{:S(2)}) collective-permute-start(bf16[128,1024]{1,0:T(8,128)(2,1)S(1)} %pad_maximum_fusion.rest_0_), channel_id=1, source_target_pairs={{2,0},{3,1},{6,4},{7,5},{10,8},{11,9},{14,12},{15,13},{18,16},{19,... | collective-permute-start | bytes 786440 | tf_op jit(solution)/shard_map/ppermute | solution.py:109
  8.9 33.5 %collective-permute-start.6 = (bf16[128,1024]{1,0:T(8,128)(2,1)S(1)}, bf16[128,1024]{1,0:T(8,128)(2,1)S(1)}, u32[]{:S(2)}, u32[]{:S(2)}) collective-permute-start(bf16[128,1024]{1,0:T(8,128)(2,1)S(1)} %pad_maximum_fusion.rest_0_), channel_id=1, source_target_pairs={{1,0},{2,1},{3,2},{5,4},{6,5},{7,6},{9,8},{10,9},{11,10},{13,12},{... | collective-permute-start | bytes 786440 | tf_op jit(solution)/shard_map/ppermute | solution.py:109
  10.2 32.2 %collective-permute-start.3 = (bf16[128,1024]{1,0:T(8,128)(2,1)S(1)}, bf16[128,1024]{1,0:T(8,128)(2,1)S(1)}, u32[]{:S(2)}, u32[]{:S(2)}) collective-permute-start(bf16[128,1024]{1,0:T(8,128)(2,1)S(1)} %pad_maximum_fusion.rest_0_), channel_id=1, source_target_pairs={{0,1},{1,2},{2,3},{4,5},{5,6},{6,7},{8,9},{9,10},{10,11},{12,13},{... | collective-permute-start | bytes 786440 | tf_op jit(solution)/shard_map/ppermute | solution.py:109
  14.8 27.7 %copy-start.1 = (bf16[128,1024]{1,0:T(8,128)(2,1)}, bf16[128,1024]{1,0:T(8,128)(2,1)S(1)}, u32[]{:S(2)}) copy-start(bf16[128,1024]{1,0:T(8,128)(2,1)S(1)} %collective-permute-done.7.rest_5_) | copy-start | bytes 786436
  14.8 27.6 %collective-permute-start.8 = (bf16[128,1024]{1,0:T(8,128)(2,1)S(1)}, bf16[128,1024]{1,0:T(8,128)(2,1)S(1)}, u32[]{:S(2)}, u32[]{:S(2)}) collective-permute-start(bf16[128,1024]{1,0:T(8,128)(2,1)S(1)} %collective-permute-done.7.rest_5_), channel_id=1, source_target_pairs={{2,3},{6,7},{10,11},{14,15},{18,19},{22,23},{26,27},{30,31}} | collective-permute-start | bytes 786440 | tf_op jit(solution)/shard_map/ppermute | solution.py:109
  24.9 17.5 %copy-start.2 = (bf16[128,1024]{1,0:T(8,128)(2,1)}, bf16[128,1024]{1,0:T(8,128)(2,1)S(1)}, u32[]{:S(2)}) copy-start(bf16[128,1024]{1,0:T(8,128)(2,1)S(1)} %collective-permute-done.4.rest_6_) | copy-start | bytes 786436
  24.9 17.5 %collective-permute-start.5 = (bf16[128,1024]{1,0:T(8,128)(2,1)S(1)}, bf16[128,1024]{1,0:T(8,128)(2,1)S(1)}, u32[]{:S(2)}, u32[]{:S(2)}) collective-permute-start(bf16[128,1024]{1,0:T(8,128)(2,1)S(1)} %collective-permute-done.4.rest_6_), channel_id=1, source_target_pairs={{1,0},{5,4},{9,8},{13,12},{17,16},{21,20},{25,24},{29,28}} | collective-permute-start | bytes 786440 | tf_op jit(solution)/shard_map/ppermute | solution.py:109
  28.3 5.4 %collective-permute-start = (f32[1]{0:T(128)}, f32[1]{0:T(128)}, u32[]{:S(2)}, u32[]{:S(2)}) collective-permute-start(f32[1]{0:T(128)} %select_n.25), channel_id=1, source_target_pairs={{0,1},{1,2},{2,3},{3,0},{4,5},{5,6},{6,7},{7,4},{8,9},{9,10},{10,1... | collective-permute-start | bytes 20 | tf_op jit(solution)/shard_map/ppermute | solution.py:105
  33.7 4.5 %collective-permute-start.1 = (f32[1]{0:T(128)}, f32[1]{0:T(128)}, u32[]{:S(2)}, u32[]{:S(2)}) collective-permute-start(f32[1]{0:T(128)} %select_n.25), channel_id=1, source_target_pairs={{0,2},{1,3},{2,0},{3,1},{4,6},{5,7},{6,4},{7,5},{8,10},{9,11},{10,... | collective-permute-start | bytes 20 | tf_op jit(solution)/shard_map/ppermute | solution.py:105
  38.2 3.5 %collective-permute-start.2 = (f32[1]{0:T(128)}, f32[1]{0:T(128)}, u32[]{:S(2)}, u32[]{:S(2)}) collective-permute-start(f32[1]{0:T(128)} %select_n.25), channel_id=1, source_target_pairs={{0,3},{1,0},{2,1},{3,2},{4,7},{5,4},{6,5},{7,6},{8,11},{9,8},{10,9... | collective-permute-start | bytes 20 | tf_op jit(solution)/shard_map/ppermute | solution.py:105
  42.4 0.7 copy-start.3
  42.4 0.8 %copy-start.4 = (bf16[128,1024]{1,0:T(8,128)(2,1)}, bf16[128,1024]{1,0:T(8,128)(2,1)S(1)}, u32[]{:S(2)}) copy-start(bf16[128,1024]{1,0:T(8,128)(2,1)S(1)} %collective-permute-done.3.rest_1_) | copy-start | bytes 786436
  42.4 0.9 %copy-start.5 = (bf16[128,1024]{1,0:T(8,128)(2,1)}, bf16[128,1024]{1,0:T(8,128)(2,1)S(1)}, u32[]{:S(2)}) copy-start(bf16[128,1024]{1,0:T(8,128)(2,1)S(1)} %collective-permute-done.8.rest_4_) | copy-start | bytes 786436
  42.4 0.9 %copy-start.6 = (bf16[128,1024]{1,0:T(8,128)(2,1)}, bf16[128,1024]{1,0:T(8,128)(2,1)S(1)}, u32[]{:S(2)}) copy-start(bf16[128,1024]{1,0:T(8,128)(2,1)S(1)} %collective-permute-done.5.rest_2_) | copy-start | bytes 786436
  51.9 9.3 %collective-permute-start.11 = (bf16[128,1024]{1,0:T(8,128)(2,1)}, bf16[128,1024]{1,0:T(8,128)(2,1)S(1)}, u32[]{:S(2)}, u32[]{:S(2)}) collective-permute-start(bf16[128,1024]{1,0:T(8,128)(2,1)} %get-tuple-element.34), channel_id=1, source_target_pairs={{0,1},{4,5},{8,9},{12,13},{16,17},{20,21},{24,25},{28,29}} | collective-permute-start | bytes 786440 | tf_op jit(solution)/shard_map/ppermute | solution.py:109
  54.6 6.6 %collective-permute-start.12 = (bf16[128,1024]{1,0:T(8,128)(2,1)}, bf16[128,1024]{1,0:T(8,128)(2,1)S(1)}, u32[]{:S(2)}, u32[]{:S(2)}) collective-permute-start(bf16[128,1024]{1,0:T(8,128)(2,1)} %get-tuple-element.35), channel_id=1, source_target_pairs={{3,2},{7,6},{11,10},{15,14},{19,18},{23,22},{27,26},{31,30}} | collective-permute-start | bytes 786440 | tf_op jit(solution)/shard_map/ppermute | solution.py:109
  55.3 13.9 %collective-permute-start.9 = (bf16[128,1024]{1,0:T(8,128)(2,1)}, bf16[128,1024]{1,0:T(8,128)(2,1)S(1)}, u32[]{:S(2)}, u32[]{:S(2)}) collective-permute-start(bf16[128,1024]{1,0:T(8,128)(2,1)} %get-tuple-element.34), channel_id=1, source_target_pairs={{1,0},{2,1},{3,2},{5,4},{6,5},{7,6},{9,8},{10,9},{11,10},{13,12},{... | collective-permute-start | bytes 786440 | tf_op jit(solution)/shard_map/ppermute | solution.py:109
  56.6 12.6 %collective-permute-start.10 = (bf16[128,1024]{1,0:T(8,128)(2,1)}, bf16[128,1024]{1,0:T(8,128)(2,1)S(1)}, u32[]{:S(2)}, u32[]{:S(2)}) collective-permute-start(bf16[128,1024]{1,0:T(8,128)(2,1)} %get-tuple-element.35), channel_id=1, source_target_pairs={{0,1},{1,2},{2,3},{4,5},{5,6},{6,7},{8,9},{9,10},{10,11},{12,13},{... | collective-permute-start | bytes 786440 | tf_op jit(solution)/shard_map/ppermute | solution.py:109
  61.2 13.2 %copy-start.7 = (bf16[128,1024]{1,0:T(8,128)(2,1)S(1)}, bf16[128,1024]{1,0:T(8,128)(2,1)}, u32[]{:S(2)}) copy-start(bf16[128,1024]{1,0:T(8,128)(2,1)} %get-tuple-element.33) | copy-start | bytes 786436
  62.3 12.0 %collective-permute-start.14 = (bf16[128,1024]{1,0:T(8,128)(2,1)S(1)}, bf16[128,1024]{1,0:T(8,128)(2,1)S(1)}, u32[]{:S(2)}, u32[]{:S(2)}) collective-permute-start(bf16[128,1024]{1,0:T(8,128)(2,1)S(1)} %add_convert_fusion.1), channel_id=1, source_target_pairs={{2,0},{3,1},{6,4},{7,5},{10,8},{11,9},{14,12},{15,13},{18,16},{19,... | collective-permute-start | bytes 786440 | tf_op jit(solution)/shard_map/ppermute | solution.py:109
  63.6 10.8 %collective-permute-start.13 = (bf16[128,1024]{1,0:T(8,128)(2,1)S(1)}, bf16[128,1024]{1,0:T(8,128)(2,1)S(1)}, u32[]{:S(2)}, u32[]{:S(2)}) collective-permute-start(bf16[128,1024]{1,0:T(8,128)(2,1)S(1)} %add_convert_fusion.1), channel_id=1, source_target_pairs={{0,2},{1,3},{4,6},{5,7},{8,10},{9,11},{12,14},{13,15},{16,18},{17,... | collective-permute-start | bytes 786440 | tf_op jit(solution)/shard_map/ppermute | solution.py:109

commit v3 on v1

--- a/solution.py
+++ b/solution.py
@@ -17,15 +17,26 @@
 masked_score = -1e30
 
 
-def attention_kernel(n_pieces, factor_ref, q_ref, cot_ref, kown_ref, vown_ref, *rest):
-    piece_refs = rest[:n_pieces]
-    dq_ref, dkown_ref, dvown_ref = rest[n_pieces:n_pieces + 3]
-    part_refs = rest[n_pieces + 3:]
+def slot_columns(refs, columns):
+    if len(refs) == 1:
+        return refs[0][:, columns]
+    total = refs[0][:, columns].astype(jnp.float32)
+    for r in refs[1:]:
+        total = total + r[:, columns].astype(jnp.float32)
+    return total.astype(jnp.bfloat16)
+
+
+def attention_kernel(slot_spec, factor_ref, q_ref, cot_ref, kown_ref, vown_ref, *rest):
+    n_inputs = sum(len(s) for s in slot_spec)
+    input_refs = rest[:n_inputs]
+    piece_refs = [[input_refs[i] for i in s] for s in slot_spec]
+    dq_ref, dkown_ref, dvown_ref = rest[n_inputs:n_inputs + 3]
+    part_refs = rest[n_inputs + 3:]
     group_size = HEADS // KV_HEADS
     group_width = group_size * HEAD_DIM
     kv_width = KV_HEADS * HEAD_DIM
     resp_len = q_ref.shape[0]
-    piece_len = piece_refs[0].shape[0]
+    piece_len = input_refs[0].shape[0]
     scaling = 1.0 / math.sqrt(HEAD_DIM)
     rows = group_size * resp_len
     factor = factor_ref[...]
@@ -50,8 +61,8 @@
         )
         k_cols = slice(g * HEAD_DIM, (g + 1) * HEAD_DIM)
         v_cols = slice(kv_width + g * HEAD_DIM, kv_width + (g + 1) * HEAD_DIM)
-        k_pre = jnp.concatenate([r[:, k_cols] for r in piece_refs], axis=0)
-        v_pre = jnp.concatenate([r[:, v_cols] for r in piece_refs], axis=0)
+        k_pre = jnp.concatenate([slot_columns(r, k_cols) for r in piece_refs], axis=0)
+        v_pre = jnp.concatenate([slot_columns(r, v_cols) for r in piece_refs], axis=0)
         k_own = kown_ref[:, k_cols]
         v_own = vown_ref[:, k_cols]
         s_pre = lax.dot_general(q_rows, k_pre, contract_cols, preferred_element_type=jnp.float32) * scaling
@@ -113,7 +124,13 @@
     piece_len = prefix_keys.shape[1]
     kv_width = KV_HEADS * HEAD_DIM
     local_kv = jnp.concatenate([prefix_keys[0], prefix_values[0]], axis=1)
-    pieces = [local_kv] + [shifted(local_kv, k, n) for k in range(1, n)]
+    slots = [local_kv] + [shifted(local_kv, k, n) for k in range(1, n)]
+    slots = [s if isinstance(s, tuple) else (s,) for s in slots]
+    slot_spec = []
+    pieces = []
+    for s in slots:
+        slot_spec.append(tuple(range(len(pieces), len(pieces) + len(s))))
+        pieces.extend(s)
     live_count = counts[0]
     count_real = live_count.astype(jnp.float32)
     slot_ids = lax.axis_index("resp") * slot_count + jnp.arange(slot_count, dtype=jnp.int32)
@@ -121,18 +138,18 @@
     margin = policy_likelihood[0] - reference_likelihood[0]
     weight = jnp.where(live_slots, 2.0 * jax.nn.sigmoid(loss_beta * margin) / count_real, 0.0)
     loss_terms = jnp.where(live_slots, 2.0 / loss_beta * jax.nn.softplus(loss_beta * margin), 0.0)
-    all_terms = [loss_terms] + [shifted(loss_terms, k, n) for k in range(1, n)]
-    forget_loss = (jnp.sum(jnp.concatenate(all_terms)) / count_real).reshape(1)
+    forget_loss = (lax.psum(jnp.sum(loss_terms), "resp") / count_real).reshape(1)
     positions = jnp.arange(resp_len, dtype=jnp.int32)
     factor = jnp.where(positions[None, :] < lengths[0][:, None], weight[:, None], 0.0)
     factor = factor.reshape(resp_len, 1).astype(jnp.float32)
+    forget_loss, factor, *pieces = lax.optimization_barrier((forget_loss, factor, *pieces))
     out_shape = (
         jax.ShapeDtypeStruct(queries.shape[2:], jnp.bfloat16),
         jax.ShapeDtypeStruct(resp_keys.shape[2:], jnp.bfloat16),
         jax.ShapeDtypeStruct(resp_values.shape[2:], jnp.bfloat16),
     ) + tuple(jax.ShapeDtypeStruct((piece_len, 2 * kv_width), jnp.bfloat16) for _ in range(n))
     results = pl.pallas_call(
-        functools.partial(attention_kernel, n),
+        functools.partial(attention_kernel, tuple(slot_spec)),
         out_shape=out_shape,
     )(factor, queries[0, 0], cotangent[0, 0], resp_keys[0, 0], resp_values[0, 0], *pieces)
     grad_q, grad_k, grad_v = results[:3]

time: 73.3 us -> 70.5 us (0.962)
  blocking collectives: 0 us -> 20.5 us
  starting transfers between devices: 31.7 us -> 12 us
  waiting for transfers between devices: 22.2 us -> 19.9 us
  between operations: 6.66 us -> 5.3 us
    psum x0 -> x1, blocking collectives: none -> 20.5 us  [on_device(): lax.psum(jnp.sum(loss_terms), 'resp') / count_real]
    ppermute x9 -> x6, starting transfers between devices: 31.7 us -> 12 us  [shifted(): return lax.ppermute(value, 'resp', [(i, (i + shift) % n) for i in range(n)])]
    ppermute x9 -> x6, waiting for transfers between devices: 22.2 us -> 19.9 us  [shifted(): return lax.ppermute(value, 'resp', [(i, (i + shift) % n) for i in range(n)])]
  transfers between devices with their start and end apart: 9 -> 6, of which waited for: 3 -> 2; matrix products, arithmetic and copies ran while one was open for 1% -> 1% of each run, Pallas kernels for 0% -> 0%
where the time goes in v3:
time: 70.5 us; the launch traced here: 70.2 us
  blocking collectives  20.5 us (29%)
  waiting for transfers between devices  19.9 us (28%)
  starting transfers between devices  12 us (17%)
  Pallas kernels  8.25 us (12%)
  between operations  5.3 us (8%)
  other arithmetic  2.72 us (4%)
  local copies, waits for them, and re-layouts  1.56 us (2%)
    psum x1, blocking collectives, on_device(): lax.psum(jnp.sum(loss_terms), 'resp') / count_real  20.5 us
    ppermute x6, waiting for transfers between devices, shifted(): return lax.ppermute(value, 'resp', [(i, (i + shift) % n) for i in range(n)])  19.9 us
    ppermute x6, starting transfers between devices, shifted(): return lax.ppermute(value, 'resp', [(i, (i + shift) % n) for i in range(n)])  12 us
    pallas_call x1, Pallas kernels, on_device(): pl.pallas_call(functools.partial(attention_kernel, tuple(slot_spec)), out...  8.25 us
  transfers between devices with their start and end apart: 6, of which 2 were waited for; matrix products, arithmetic and copies ran while one was open for 1% of the time, Pallas kernels for 0%

profile of v3, /device:TPU:0, one launch (start us, length us, event | category | flops | bytes accessed | tf_op | source)
XLA Modules:
  0.0 70.2 jit_solution(4922313495498701932)
XLA Ops:
  0.6 1.0 %pad_maximum_fusion.rest_0_ = bf16[128,1024]{1,0:T(8,128)(2,1)S(1)} fusion(bf16[128,512]{1,0:T(8,128)(2,1)} %bitcast.23, bf16[128,512]{1,0:T(8,128)(2,1)} %bitcast.24), kind=kLoop, calls=%fused_computation.1 | loop fusion | flops 524288 | bytes 524288 | tf_op jit(solution)/shard_map/concatenate | solution.py:126
  1.6 0.0 copy-start
  1.6 5.1 %collective-permute-start.2 = (bf16[128,1024]{1,0:T(8,128)(2,1)S(1)}, bf16[128,1024]{1,0:T(8,128)(2,1)S(1)}, u32[]{:S(2)}, u32[]{:S(2)}) collective-permute-start(bf16[128,1024]{1,0:T(8,128)(2,1)S(1)} %pad_maximum_fusion.rest_0_), channel_id=1, source_target_pairs={{0,3},{1,0},{2,1},{3,2},{4,7},{5,4},{6,5},{7,6},{8,11},{9,8},{10,9... | collective-permute-start | bytes 786440 | tf_op jit(solution)/shard_map/ppermute | solution.py:105
  6.7 0.0 collective-permute-start.1
  6.7 1.0 %collective-permute-start = (bf16[128,1024]{1,0:T(8,128)(2,1)S(1)}, bf16[128,1024]{1,0:T(8,128)(2,1)S(1)}, u32[]{:S(2)}, u32[]{:S(2)}) collective-permute-start(bf16[128,1024]{1,0:T(8,128)(2,1)S(1)} %pad_maximum_fusion.rest_0_), channel_id=1, source_target_pairs={{0,1},{1,2},{2,3},{3,0},{4,5},{5,6},{6,7},{7,4},{8,9},{9,10},{10,1... | collective-permute-start | bytes 786440 | tf_op jit(solution)/shard_map/ppermute | solution.py:105
  9.8 20.5 %psum.7 = f32[]{:T(128)} all-reduce(f32[]{:T(128)} %bitcast.2), channel_id=1, replica_groups=mesh['groups'=2,'prompt'=4,'resp'=4] {'resp'}, use_global_device_ids=true, to_apply=%region_0.1 | all-reduce | flops 1 | bytes 8 | tf_op jit(solution)/shard_map/psum | solution.py:141
  31.7 0.6 fusion.factor_ref
  32.3 0.0 collective-permute-done.2.rest_3_
  32.3 0.0 copy-start.1
  32.3 0.0 collective-permute-done.1.rest_2_
  32.3 0.0 copy-start.2
  32.4 0.0 collective-permute-done.rest_1_
  32.4 0.0 copy-start.3
  32.4 0.0 copy-done
  32.4 0.6 copy-done.1
  33.0 0.1 copy-done.2
  33.1 0.1 copy-done.3
  33.2 8.2 %shard_map.145 = (bf16[32,8192]{1,0:T(8,128)(2,1)}, bf16[32,512]{1,0:T(8,128)(2,1)}, bf16[32,512]{1,0:T(8,128)(2,1)}, bf16[128,1024]{1,0:T(8,128)(2,1)}, bf16[12...) custom-call(f32[32,1]{1,0:T(8,128)} %fusion.factor_ref, bf16[32,8192]{1,0:T(8,128)(2,1)} %bitcast.21, ...), custom_call_target="tpu_custom_call" | custom-call | tf_op jit(solution)/shard_map/pallas_call | solution.py:151
  41.5 5.4 %collective-permute-start.3 = (bf16[128,1024]{1,0:T(8,128)(2,1)}, bf16[128,1024]{1,0:T(8,128)(2,1)S(1)}, u32[]{:S(2)}, u32[]{:S(2)}) collective-permute-start(bf16[128,1024]{1,0:T(8,128)(2,1)} %get-tuple-element.28), channel_id=1, source_target_pairs={{0,3},{1,0},{2,1},{3,2},{4,7},{5,4},{6,5},{7,6},{8,11},{9,8},{10,9... | collective-permute-start | bytes 786440 | tf_op jit(solution)/shard_map/ppermute | solution.py:105
  46.8 0.0 collective-permute-start.4
  46.8 0.6 collective-permute-start.5
  47.4 6.5 %collective-permute-done.3 = bf16[128,1024]{1,0:T(8,128)(2,1)S(1)} collective-permute-done((bf16[128,1024]{1,0:T(8,128)(2,1)}, bf16[128,1024]{1,0:T(8,128)(2,1)S(1)}, u32[]{:S(2)}, u32[]{:S(2)}) %collective-permute-start.3) | collective-permute-done | bytes 262176 | tf_op jit(solution)/shard_map/ppermute | solution.py:105
  53.9 13.3 %collective-permute-done.4 = bf16[128,1024]{1,0:T(8,128)(2,1)S(1)} collective-permute-done((bf16[128,1024]{1,0:T(8,128)(2,1)}, bf16[128,1024]{1,0:T(8,128)(2,1)S(1)}, u32[]{:S(2)}, u32[]{:S(2)}) %collective-permute-start.4) | collective-permute-done | bytes 262176 | tf_op jit(solution)/shard_map/ppermute | solution.py:105
  67.3 0.0 collective-permute-done.5
  67.3 1.1 %add_convert_fusion = bf16[128,1024]{1,0:T(8,128)(2,1)S(1)} fusion(bf16[128,1024]{1,0:T(8,128)(2,1)S(1)} %collective-permute-done.5, bf16[128,1024]{1,0:T(8,128)(2,1)S(1)} %collective-permute-done.4, bf16[128,1024]{1,0:T(8,128)(2,1)S(1)} %collective-permute-done.3, bf16[128,1024]{1,0:T(8,128)(2,1)} %get-tuple-element.27), kind=kLoop, calls=%fused_computation | loop fusion | flops 1048576 | bytes 1310720 | tf_op jit(solution)/shard_map/convert_element_type | solution.py:160
  68.4 0.7 %slice_bitcast_fusion = (bf16[1,128,512]{2,1,0:T(8,128)(2,1)}, bf16[1,128,512]{2,1,0:T(8,128)(2,1)}) fusion(bf16[128,1024]{1,0:T(8,128)(2,1)S(1)} %add_convert_fusion), kind=kLoop, calls=%fused_computation.2 | loop fusion | bytes 524288 | tf_op jit(solution)/shard_map/broadcast_in_dim | solution.py:166
Async XLA Ops:
  1.6 30.8 %copy-start = (bf16[128,1024]{1,0:T(8,128)(2,1)}, bf16[128,1024]{1,0:T(8,128)(2,1)S(1)}, u32[]{:S(2)}) copy-start(bf16[128,1024]{1,0:T(8,128)(2,1)S(1)} %pad_maximum_fusion.rest_0_) | copy-start | bytes 786436
  1.6 30.7 %collective-permute-start.2 = (bf16[128,1024]{1,0:T(8,128)(2,1)S(1)}, bf16[128,1024]{1,0:T(8,128)(2,1)S(1)}, u32[]{:S(2)}, u32[]{:S(2)}) collective-permute-start(bf16[128,1024]{1,0:T(8,128)(2,1)S(1)} %pad_maximum_fusion.rest_0_), channel_id=1, source_target_pairs={{0,3},{1,0},{2,1},{3,2},{4,7},{5,4},{6,5},{7,6},{8,11},{9,8},{10,9... | collective-permute-start | bytes 786440 | tf_op jit(solution)/shard_map/ppermute | solution.py:105
  6.7 25.6 %collective-permute-start.1 = (bf16[128,1024]{1,0:T(8,128)(2,1)S(1)}, bf16[128,1024]{1,0:T(8,128)(2,1)S(1)}, u32[]{:S(2)}, u32[]{:S(2)}) collective-permute-start(bf16[128,1024]{1,0:T(8,128)(2,1)S(1)} %pad_maximum_fusion.rest_0_), channel_id=1, source_target_pairs={{0,2},{1,3},{2,0},{3,1},{4,6},{5,7},{6,4},{7,5},{8,10},{9,11},{10,... | collective-permute-start | bytes 786440 | tf_op jit(solution)/shard_map/ppermute | solution.py:105
  6.7 25.6 %collective-permute-start = (bf16[128,1024]{1,0:T(8,128)(2,1)S(1)}, bf16[128,1024]{1,0:T(8,128)(2,1)S(1)}, u32[]{:S(2)}, u32[]{:S(2)}) collective-permute-start(bf16[128,1024]{1,0:T(8,128)(2,1)S(1)} %pad_maximum_fusion.rest_0_), channel_id=1, source_target_pairs={{0,1},{1,2},{2,3},{3,0},{4,5},{5,6},{6,7},{7,4},{8,9},{9,10},{10,1... | collective-permute-start | bytes 786440 | tf_op jit(solution)/shard_map/ppermute | solution.py:105
  32.3 0.7 copy-start.1
  32.3 0.8 %copy-start.2 = (bf16[128,1024]{1,0:T(8,128)(2,1)}, bf16[128,1024]{1,0:T(8,128)(2,1)S(1)}, u32[]{:S(2)}) copy-start(bf16[128,1024]{1,0:T(8,128)(2,1)S(1)} %collective-permute-done.1.rest_2_) | copy-start | bytes 786436
  32.4 0.9 %copy-start.3 = (bf16[128,1024]{1,0:T(8,128)(2,1)}, bf16[128,1024]{1,0:T(8,128)(2,1)S(1)}, u32[]{:S(2)}) copy-start(bf16[128,1024]{1,0:T(8,128)(2,1)S(1)} %collective-permute-done.rest_1_) | copy-start | bytes 786436
  41.5 12.5 %collective-permute-start.3 = (bf16[128,1024]{1,0:T(8,128)(2,1)}, bf16[128,1024]{1,0:T(8,128)(2,1)S(1)}, u32[]{:S(2)}, u32[]{:S(2)}) collective-permute-start(bf16[128,1024]{1,0:T(8,128)(2,1)} %get-tuple-element.28), channel_id=1, source_target_pairs={{0,3},{1,0},{2,1},{3,2},{4,7},{5,4},{6,5},{7,6},{8,11},{9,8},{10,9... | collective-permute-start | bytes 786440 | tf_op jit(solution)/shard_map/ppermute | solution.py:105
  46.8 20.4 %collective-permute-start.4 = (bf16[128,1024]{1,0:T(8,128)(2,1)}, bf16[128,1024]{1,0:T(8,128)(2,1)S(1)}, u32[]{:S(2)}, u32[]{:S(2)}) collective-permute-start(bf16[128,1024]{1,0:T(8,128)(2,1)} %get-tuple-element.29), channel_id=1, source_target_pairs={{0,2},{1,3},{2,0},{3,1},{4,6},{5,7},{6,4},{7,5},{8,10},{9,11},{10,... | collective-permute-start | bytes 786440 | tf_op jit(solution)/shard_map/ppermute | solution.py:105
  46.8 20.4 %collective-permute-start.5 = (bf16[128,1024]{1,0:T(8,128)(2,1)}, bf16[128,1024]{1,0:T(8,128)(2,1)S(1)}, u32[]{:S(2)}, u32[]{:S(2)}) collective-permute-start(bf16[128,1024]{1,0:T(8,128)(2,1)} %get-tuple-element.30), channel_id=1, source_target_pairs={{0,1},{1,2},{2,3},{3,0},{4,5},{5,6},{6,7},{7,4},{8,9},{9,10},{10,1... | collective-permute-start | bytes 786440 | tf_op jit(solution)/shard_map/ppermute | solution.py:105

commit v4 on v1

v4 whole, which is shorter than its diff:
```python
import functools
import math

import jax
import jax.numpy as jnp
from jax import lax
from jax.experimental import pallas as pl
from jax.experimental.pallas import tpu as pltpu
from jax.sharding import PartitionSpec as P

HEADS = 64
KV_HEADS = 4
HEAD_DIM = 128


loss_beta = 0.5
masked_score = -1e30


def attention_kernel(n_pieces, factor_ref, q_ref, cot_ref, kown_ref, vown_ref, *rest):
    piece_refs = rest[:n_pieces]
    dq_ref, dkown_ref, dvown_ref = rest[n_pieces:n_pieces + 3]
    part_refs = rest[n_pieces + 3:]
    group_size = HEADS // KV_HEADS
    resp_len = q_ref.shape[0]
    piece_len = piece_refs[0].shape[1]
    scaling = 1.0 / math.sqrt(HEAD_DIM)
    rows = group_size * resp_len
    factor = factor_ref[...]
    contract_minor = (((1,), (1,)), ((), ()))
    contract_major = (((0,), (0,)), ((), ()))
    q_all = q_ref[...]
    g_all = (cot_ref[...].astype(jnp.float32) * factor).astype(jnp.bfloat16)
    q_rows = jnp.concatenate([q_all[:, h * HEAD_DIM:(h + 1) * HEAD_DIM] for h in range(group_size)], axis=0)
    g_rows = jnp.concatenate([g_all[:, h * HEAD_DIM:(h + 1) * HEAD_DIM] for h in range(group_size)], axis=0)
    k_pre = jnp.concatenate([r[0] for r in piece_refs], axis=0)
    v_pre = jnp.concatenate([r[1] for r in piece_refs], axis=0)
    k_own = kown_ref[...]
    v_own = vown_ref[...]
    s_pre = lax.dot_general(k_pre, q_rows, contract_minor, preferred_element_type=jnp.float32) * scaling
    s_own = lax.dot_general(k_own, q_rows, contract_minor, preferred_element_type=jnp.float32) * scaling
    own_pos = lax.broadcasted_iota(jnp.int32, (resp_len, rows), 0)
    token_of_col = lax.broadcasted_iota(jnp.int32, (resp_len, rows), 1) % resp_len
    s_own = jnp.where(token_of_col >= own_pos, s_own, masked_score)
    peak = jnp.maximum(jnp.max(s_pre, axis=0, keepdims=True), jnp.max(s_own, axis=0, keepdims=True))
    e_pre = jnp.exp(s_pre - peak)
    e_own = jnp.exp(s_own - peak)
    total = jnp.sum(e_pre, axis=0, keepdims=True) + jnp.sum(e_own, axis=0, keepdims=True)
    inv_total = 1.0 / total
    p_pre = e_pre * inv_total
    p_own = e_own * inv_total
    dp_pre = lax.dot_general(v_pre, g_rows, contract_minor, preferred_element_type=jnp.float32)
    dp_own = lax.dot_general(v_own, g_rows, contract_minor, preferred_element_type=jnp.float32)
    centre = jnp.sum(p_pre * dp_pre, axis=0, keepdims=True) + jnp.sum(p_own * dp_own, axis=0, keepdims=True)
    ds_pre = (p_pre * (dp_pre - centre)).astype(jnp.bfloat16)
    ds_own = (p_own * (dp_own - centre)).astype(jnp.bfloat16)
    dk_pre = jnp.dot(ds_pre, q_rows, preferred_element_type=jnp.float32) * scaling
    dv_pre = jnp.dot(p_pre.astype(jnp.bfloat16), g_rows, preferred_element_type=jnp.float32)
    for i, r in enumerate(part_refs):
        r[0] = dk_pre[i * piece_len:(i + 1) * piece_len].astype(jnp.bfloat16)
        r[1] = dv_pre[i * piece_len:(i + 1) * piece_len].astype(jnp.bfloat16)
    dkown_ref[...] = (jnp.dot(ds_own, q_rows, preferred_element_type=jnp.float32) * scaling).astype(jnp.bfloat16)
    dvown_ref[...] = jnp.dot(p_own.astype(jnp.bfloat16), g_rows, preferred_element_type=jnp.float32).astype(
        jnp.bfloat16
    )
    dq_rows = (
        lax.dot_general(ds_pre, k_pre, contract_major, preferred_element_type=jnp.float32) * scaling
        + lax.dot_general(ds_own, k_own, contract_major, preferred_element_type=jnp.float32) * scaling
    )
    for h in range(group_size):
        dq_ref[:, h * HEAD_DIM:(h + 1) * HEAD_DIM] = dq_rows[h * resp_len:(h + 1) * resp_len].astype(jnp.bfloat16)


def shifted(value, shift, n):
    return lax.ppermute(value, "resp", [(i, (i + shift) % n) for i in range(n)])


def on_device(
    queries,
    cotangent,
    resp_keys,
    resp_values,
    prefix_keys,
    prefix_values,
    counts,
    lengths,
    policy_likelihood,
    reference_likelihood,
):
    n = lax.axis_size("resp")
    slot_count = queries.shape[1]
    assert slot_count == 1
    resp_len = queries.shape[2]
    piece_len = prefix_keys.shape[1]
    local_kv = jnp.stack([prefix_keys[0], prefix_values[0]])
    pieces = [local_kv] + [shifted(local_kv, k, n) for k in range(1, n)]
    live_count = counts[0]
    count_real = live_count.astype(jnp.float32)
    slot_ids = lax.axis_index("resp") * slot_count + jnp.arange(slot_count, dtype=jnp.int32)
    live_slots = slot_ids < live_count
    margin = policy_likelihood[0] - reference_likelihood[0]
    weight = jnp.where(live_slots, 2.0 * jax.nn.sigmoid(loss_beta * margin) / count_real, 0.0)
    loss_terms = jnp.where(live_slots, 2.0 / loss_beta * jax.nn.softplus(loss_beta * margin), 0.0)
    forget_loss = (lax.psum(jnp.sum(loss_terms), "resp") / count_real).reshape(1)
    positions = jnp.arange(resp_len, dtype=jnp.int32)
    factor = jnp.where(positions[None, :] < lengths[0][:, None], weight[:, None], 0.0)
    factor = factor.reshape(resp_len, 1).astype(jnp.float32)
    forget_loss, factor, *pieces = lax.optimization_barrier((forget_loss, factor, *pieces))
    group_width = (HEADS // KV_HEADS) * HEAD_DIM
    piece_block = pl.BlockSpec((2, piece_len, HEAD_DIM), lambda g: (0, 0, g))
    results = pl.pallas_call(
        functools.partial(attention_kernel, n),
        grid=(KV_HEADS,),
        in_specs=[
            pl.BlockSpec((resp_len, 1), lambda g: (0, 0)),
            pl.BlockSpec((resp_len, group_width), lambda g: (0, g)),
            pl.BlockSpec((resp_len, group_width), lambda g: (0, g)),
            pl.BlockSpec((resp_len, HEAD_DIM), lambda g: (0, g)),
            pl.BlockSpec((resp_len, HEAD_DIM), lambda g: (0, g)),
        ]
        + [piece_block] * n,
        out_specs=[
            pl.BlockSpec((resp_len, group_width), lambda g: (0, g)),
            pl.BlockSpec((resp_len, HEAD_DIM), lambda g: (0, g)),
            pl.BlockSpec((resp_len, HEAD_DIM), lambda g: (0, g)),
        ]
        + [piece_block] * n,
        out_shape=[
            jax.ShapeDtypeStruct(queries.shape[2:], jnp.bfloat16),
            jax.ShapeDtypeStruct(resp_keys.shape[2:], jnp.bfloat16),
            jax.ShapeDtypeStruct(resp_values.shape[2:], jnp.bfloat16),
        ]
        + [jax.ShapeDtypeStruct(local_kv.shape, jnp.bfloat16) for _ in range(n)],
    )(factor, queries[0, 0], cotangent[0, 0], resp_keys[0, 0], resp_values[0, 0], *pieces)
    grad_q, grad_k, grad_v = results[:3]
    parts = results[3:]
    returned = [parts[0]] + [shifted(parts[k], -k, n) for k in range(1, n)]
    summed_keys = sum(r[0].astype(jnp.float32) for r in returned).astype(jnp.bfloat16)
    summed_values = sum(r[1].astype(jnp.float32) for r in returned).astype(jnp.bfloat16)
    return (
        grad_q[None, None],
        grad_k[None, None],
        grad_v[None, None],
        summed_keys[None],
        summed_values[None],
        forget_loss,
    )


def solution(mesh):
    placed = (
        P(("groups", "prompt"), "resp", None, None),
        P(("groups", "prompt"), "resp", None, None),
        P(("groups", "prompt"), "resp", None, None),
        P(("groups", "prompt"), "resp", None, None),
        P(("groups", "prompt"), "resp", None),
        P(("groups", "prompt"), "resp", None),
        P(("groups", "prompt")),
        P(("groups", "prompt"), "resp"),
        P(("groups", "prompt"), "resp"),
        P(("groups", "prompt"), "resp"),
    )
    return jax.shard_map(
        on_device,
        mesh=mesh,
        in_specs=placed,
        out_specs=(
            P(("groups", "prompt"), "resp", None, None),
            P(("groups", "prompt"), "resp", None, None),
            P(("groups", "prompt"), "resp", None, None),
            P(("groups", "prompt"), "resp", None),
            P(("groups", "prompt"), "resp", None),
            P(("groups", "prompt")),
        ),
        check_vma=False,
    )
```

time: 73.3 us -> 70 us (0.955)
  blocking collectives: 0 us -> 20.5 us
  starting transfers between devices: 31.7 us -> 12.2 us
  waiting for transfers between devices: 22.2 us -> 19.8 us
  between operations: 6.66 us -> 5.32 us
    psum x0 -> x1, blocking collectives: none -> 20.5 us  [on_device(): lax.psum(jnp.sum(loss_terms), 'resp') / count_real]
    ppermute x9 -> x6, starting transfers between devices: 31.7 us -> 12.2 us  [shifted(): return lax.ppermute(value, 'resp', [(i, (i + shift) % n) for i in range(n)])]
    ppermute x9 -> x6, waiting for transfers between devices: 22.2 us -> 19.8 us  [shifted(): return lax.ppermute(value, 'resp', [(i, (i + shift) % n) for i in range(n)])]
    concatenate x1 -> x0, other arithmetic: 0.99 us -> none  [on_device(): local_kv = jnp.concatenate([prefix_keys[0], prefix_values[0]], axis=1)]
    unnamed x8 -> x11, local copies, waits for them, and re-layouts: 0.83 us -> 1.81 us
  transfers between devices with their start and end apart: 9 -> 6, of which waited for: 3 -> 2; matrix products, arithmetic and copies ran while one was open for 1% -> 1% of each run, Pallas kernels for 0% -> 0%
where the time goes in v4:
time: 70 us; the launch traced here: 69.7 us
  blocking collectives  20.5 us (29%)
  waiting for transfers between devices  19.8 us (28%)
  starting transfers between devices  12.2 us (17%)
  Pallas kernels  7.71 us (11%)
  between operations  5.32 us (8%)
  other arithmetic  2.41 us (3%)
  local copies, waits for them, and re-layouts  1.82 us (3%)
    psum x1, blocking collectives, on_device(): lax.psum(jnp.sum(loss_terms), 'resp') / count_real  20.5 us
    ppermute x6, waiting for transfers between devices, shifted(): return lax.ppermute(value, 'resp', [(i, (i + shift) % n) for i in range(n)])  19.8 us
    ppermute x6, starting transfers between devices, shifted(): return lax.ppermute(value, 'resp', [(i, (i + shift) % n) for i in range(n)])  12.2 us
    pallas_call x1, Pallas kernels, on_device(): pl.pallas_call(functools.partial(attention_kernel, n), grid=(KV_HEADS,),...  7.71 us
    unnamed x11, local copies, waits for them, and re-layouts  1.81 us
    convert_element_type x1, other arithmetic, on_device(): sum((r[1].astype(jnp.float32) for r in returned)).astype(jnp.bfloat16)  1.8 us
  transfers between devices with their start and end apart: 6, of which 2 were waited for; matrix products, arithmetic and copies ran while one was open for 1% of the time, Pallas kernels for 0%

profile of v4, /device:TPU:0, one launch (start us, length us, event | category | flops | bytes accessed | tf_op | source)
XLA Modules:
  0.0 69.7 jit_solution(9931450275766404897)
XLA Ops:
  0.6 0.0 copy-start.4
  0.6 0.9 %constant_dynamic-update-slice_fusion.1 = bf16[2,128,512]{2,1,0:T(8,128)(2,1)S(1)} fusion(bf16[1,128,512]{2,1,0:T(8,128)(2,1)} %param.14), kind=kLoop, calls=%fused_computation.5 | loop fusion | bytes 262144
  1.6 0.0 copy-done.4
  1.6 0.0 copy-start
  1.6 5.1 %collective-permute-start.2 = (bf16[2,128,512]{2,1,0:T(8,128)(2,1)S(1)}, bf16[2,128,512]{2,1,0:T(8,128)(2,1)S(1)}, u32[]{:S(2)}, u32[]{:S(2)}) collective-permute-start(bf16[2,128,512]{2,1,0:T(8,128)(2,1)S(1)} %constant_dynamic-update-slice_fusion.rest_0_), channel_id=1, source_target_pairs={{0,3},{1,0},{2,1},{3,2},{4,7},{5,4},{6,5},{7,6},{8,11},{9,8},{10,9... | collective-permute-start | bytes 786440 | tf_op jit(solution)/shard_map/ppermute | solution.py:75
  6.7 0.0 collective-permute-start.1
  6.7 1.0 %collective-permute-start = (bf16[2,128,512]{2,1,0:T(8,128)(2,1)S(1)}, bf16[2,128,512]{2,1,0:T(8,128)(2,1)S(1)}, u32[]{:S(2)}, u32[]{:S(2)}) collective-permute-start(bf16[2,128,512]{2,1,0:T(8,128)(2,1)S(1)} %constant_dynamic-update-slice_fusion.rest_0_), channel_id=1, source_target_pairs={{0,1},{1,2},{2,3},{3,0},{4,5},{5,6},{6,7},{7,4},{8,9},{9,10},{10,1... | collective-permute-start | bytes 786440 | tf_op jit(solution)/shard_map/ppermute | solution.py:75
  9.8 20.5 %psum.7 = f32[]{:T(128)} all-reduce(f32[]{:T(128)} %bitcast.2), channel_id=1, replica_groups=mesh['groups'=2,'prompt'=4,'resp'=4] {'resp'}, use_global_device_ids=true, to_apply=%region_0.1 | all-reduce | flops 1 | bytes 8 | tf_op jit(solution)/shard_map/psum | solution.py:104
  31.7 0.6 fusion.factor_ref
  32.3 0.0 collective-permute-done.2.rest_3_
  32.3 0.0 copy-start.1
  32.3 0.0 collective-permute-done.1.rest_2_
  32.3 0.0 copy-start.2
  32.4 0.0 collective-permute-done.rest_1_
  32.4 0.0 copy-start.3
  32.4 0.0 copy-done
  32.4 0.6 copy-done.1
  33.0 0.1 copy-done.2
  33.1 0.1 copy-done.3
  33.2 7.7 %shard_map.145 = (bf16[32,8192]{1,0:T(8,128)(2,1)}, bf16[32,512]{1,0:T(8,128)(2,1)}, bf16[32,512]{1,0:T(8,128)(2,1)}, bf16[2,128,512]{2,1,0:T(8,128)(2,1)}, bf16...) custom-call(f32[32,1]{1,0:T(8,128)} %fusion.factor_ref, ...), custom_call_target="tpu_custom_call" | custom-call | tf_op jit(solution)/shard_map/pallas_call | solution.py:111
  40.9 5.4 %collective-permute-start.3 = (bf16[2,128,512]{2,1,0:T(8,128)(2,1)}, bf16[2,128,512]{2,1,0:T(8,128)(2,1)S(1)}, u32[]{:S(2)}, u32[]{:S(2)}) collective-permute-start(bf16[2,128,512]{2,1,0:T(8,128)(2,1)} %get-tuple-element.28), channel_id=1, source_target_pairs={{0,3},{1,0},{2,1},{3,2},{4,7},{5,4},{6,5},{7,6},{8,11},{9,8},{10,9... | collective-permute-start | bytes 786440 | tf_op jit(solution)/shard_map/ppermute | solution.py:75
  46.3 0.0 collective-permute-start.4
  46.3 0.6 collective-permute-start.5
  47.0 6.5 %collective-permute-done.3 = bf16[2,128,512]{2,1,0:T(8,128)(2,1)S(1)} collective-permute-done((bf16[2,128,512]{2,1,0:T(8,128)(2,1)}, bf16[2,128,512]{2,1,0:T(8,128)(2,1)S(1)}, u32[]{:S(2)}, u32[]{:S(2)}) %collective-permute-start.3) | collective-permute-done | bytes 262176 | tf_op jit(solution)/shard_map/ppermute | solution.py:75
  53.5 13.3 %collective-permute-done.4 = bf16[2,128,512]{2,1,0:T(8,128)(2,1)S(1)} collective-permute-done((bf16[2,128,512]{2,1,0:T(8,128)(2,1)}, bf16[2,128,512]{2,1,0:T(8,128)(2,1)S(1)}, u32[]{:S(2)}, u32[]{:S(2)}) %collective-permute-start.4) | collective-permute-done | bytes 262176 | tf_op jit(solution)/shard_map/ppermute | solution.py:75
  66.8 0.0 collective-permute-done.5
  66.8 1.8 %add_convert_fusion = (bf16[1,128,512]{2,1,0:T(8,128)(2,1)}, bf16[1,128,512]{2,1,0:T(8,128)(2,1)}) fusion(bf16[2,128,512]{2,1,0:T(8,128)(2,1)S(1)} %collective-permute-done.5, bf16[2,128,512]{2,1,0:T(8,128)(2,1)S(1)} %collective-permute-done.4, bf16[2,128,512]{2,1,0:T(8,128)(2,1)S(1)} %collective-permute-done.3, bf16[2,128,512]{2,1,0:T(8,128)(2,1)} %get-tuple-element.27), kind=kLoop, calls=%fused_computation | loop fusion | flops 1048576 | bytes 1310720 | tf_op jit(solution)/shard_map/convert_element_type | solution.py:139
  (1 shorter events, 0.0 us)
Async XLA Ops:
  0.6 1.0 %copy-start.4 = (bf16[1,128,512]{2,1,0:T(8,128)(2,1)S(1)}, bf16[1,128,512]{2,1,0:T(8,128)(2,1)}, u32[]{:S(2)}) copy-start(bf16[1,128,512]{2,1,0:T(8,128)(2,1)} %param.15) | copy-start | bytes 393220
  1.6 30.8 %copy-start = (bf16[2,128,512]{2,1,0:T(8,128)(2,1)}, bf16[2,128,512]{2,1,0:T(8,128)(2,1)S(1)}, u32[]{:S(2)}) copy-start(bf16[2,128,512]{2,1,0:T(8,128)(2,1)S(1)} %constant_dynamic-update-slice_fusion.rest_0_) | copy-start | bytes 786436
  1.6 30.7 %collective-permute-start.2 = (bf16[2,128,512]{2,1,0:T(8,128)(2,1)S(1)}, bf16[2,128,512]{2,1,0:T(8,128)(2,1)S(1)}, u32[]{:S(2)}, u32[]{:S(2)}) collective-permute-start(bf16[2,128,512]{2,1,0:T(8,128)(2,1)S(1)} %constant_dynamic-update-slice_fusion.rest_0_), channel_id=1, source_target_pairs={{0,3},{1,0},{2,1},{3,2},{4,7},{5,4},{6,5},{7,6},{8,11},{9,8},{10,9... | collective-permute-start | bytes 786440 | tf_op jit(solution)/shard_map/ppermute | solution.py:75
  6.7 25.6 %collective-permute-start.1 = (bf16[2,128,512]{2,1,0:T(8,128)(2,1)S(1)}, bf16[2,128,512]{2,1,0:T(8,128)(2,1)S(1)}, u32[]{:S(2)}, u32[]{:S(2)}) collective-permute-start(bf16[2,128,512]{2,1,0:T(8,128)(2,1)S(1)} %constant_dynamic-update-slice_fusion.rest_0_), channel_id=1, source_target_pairs={{0,2},{1,3},{2,0},{3,1},{4,6},{5,7},{6,4},{7,5},{8,10},{9,11},{10,... | collective-permute-start | bytes 786440 | tf_op jit(solution)/shard_map/ppermute | solution.py:75
  6.7 25.6 %collective-permute-start = (bf16[2,128,512]{2,1,0:T(8,128)(2,1)S(1)}, bf16[2,128,512]{2,1,0:T(8,128)(2,1)S(1)}, u32[]{:S(2)}, u32[]{:S(2)}) collective-permute-start(bf16[2,128,512]{2,1,0:T(8,128)(2,1)S(1)} %constant_dynamic-update-slice_fusion.rest_0_), channel_id=1, source_target_pairs={{0,1},{1,2},{2,3},{3,0},{4,5},{5,6},{6,7},{7,4},{8,9},{9,10},{10,1... | collective-permute-start | bytes 786440 | tf_op jit(solution)/shard_map/ppermute | solution.py:75
  32.3 0.7 copy-start.1
  32.3 0.8 %copy-start.2 = (bf16[2,128,512]{2,1,0:T(8,128)(2,1)}, bf16[2,128,512]{2,1,0:T(8,128)(2,1)S(1)}, u32[]{:S(2)}) copy-start(bf16[2,128,512]{2,1,0:T(8,128)(2,1)S(1)} %collective-permute-done.1.rest_2_) | copy-start | bytes 786436
  32.4 0.9 %copy-start.3 = (bf16[2,128,512]{2,1,0:T(8,128)(2,1)}, bf16[2,128,512]{2,1,0:T(8,128)(2,1)S(1)}, u32[]{:S(2)}) copy-start(bf16[2,128,512]{2,1,0:T(8,128)(2,1)S(1)} %collective-permute-done.rest_1_) | copy-start | bytes 786436
  40.9 12.5 %collective-permute-start.3 = (bf16[2,128,512]{2,1,0:T(8,128)(2,1)}, bf16[2,128,512]{2,1,0:T(8,128)(2,1)S(1)}, u32[]{:S(2)}, u32[]{:S(2)}) collective-permute-start(bf16[2,128,512]{2,1,0:T(8,128)(2,1)} %get-tuple-element.28), channel_id=1, source_target_pairs={{0,3},{1,0},{2,1},{3,2},{4,7},{5,4},{6,5},{7,6},{8,11},{9,8},{10,9... | collective-permute-start | bytes 786440 | tf_op jit(solution)/shard_map/ppermute | solution.py:75
  46.3 20.4 %collective-permute-start.4 = (bf16[2,128,512]{2,1,0:T(8,128)(2,1)}, bf16[2,128,512]{2,1,0:T(8,128)(2,1)S(1)}, u32[]{:S(2)}, u32[]{:S(2)}) collective-permute-start(bf16[2,128,512]{2,1,0:T(8,128)(2,1)} %get-tuple-element.29), channel_id=1, source_target_pairs={{0,2},{1,3},{2,0},{3,1},{4,6},{5,7},{6,4},{7,5},{8,10},{9,11},{10,... | collective-permute-start | bytes 786440 | tf_op jit(solution)/shard_map/ppermute | solution.py:75
  46.3 20.4 %collective-permute-start.5 = (bf16[2,128,512]{2,1,0:T(8,128)(2,1)}, bf16[2,128,512]{2,1,0:T(8,128)(2,1)S(1)}, u32[]{:S(2)}, u32[]{:S(2)}) collective-permute-start(bf16[2,128,512]{2,1,0:T(8,128)(2,1)} %get-tuple-element.30), channel_id=1, source_target_pairs={{0,1},{1,2},{2,3},{3,0},{4,5},{5,6},{6,7},{7,4},{8,9},{9,10},{10,1... | collective-permute-start | bytes 786440 | tf_op jit(solution)/shard_map/ppermute | solution.py:75

commit v5 on v4

--- a/solution.py
+++ b/solution.py
@@ -93,7 +93,11 @@
     resp_len = queries.shape[2]
     piece_len = prefix_keys.shape[1]
     local_kv = jnp.stack([prefix_keys[0], prefix_values[0]])
-    pieces = [local_kv] + [shifted(local_kv, k, n) for k in range(1, n)]
+    if n == 4:
+        from_left = shifted(local_kv, 1, n)
+        pieces = [local_kv, from_left, shifted(local_kv, -1, n), shifted(from_left, 1, n)]
+    else:
+        pieces = [local_kv] + [shifted(local_kv, k, n) for k in range(1, n)]
     live_count = counts[0]
     count_real = live_count.astype(jnp.float32)
     slot_ids = lax.axis_index("resp") * slot_count + jnp.arange(slot_count, dtype=jnp.int32)
@@ -134,7 +138,12 @@
     )(factor, queries[0, 0], cotangent[0, 0], resp_keys[0, 0], resp_values[0, 0], *pieces)
     grad_q, grad_k, grad_v = results[:3]
     parts = results[3:]
-    returned = [parts[0]] + [shifted(parts[k], -k, n) for k in range(1, n)]
+    if n == 4:
+        relayed = shifted(parts[3], -1, n)
+        merged = (parts[1].astype(jnp.float32) + relayed.astype(jnp.float32)).astype(jnp.bfloat16)
+        returned = [parts[0], shifted(parts[2], 1, n), shifted(merged, -1, n)]
+    else:
+        returned = [parts[0]] + [shifted(parts[k], -k, n) for k in range(1, n)]
     summed_keys = sum(r[0].astype(jnp.float32) for r in returned).astype(jnp.bfloat16)
     summed_values = sum(r[1].astype(jnp.float32) for r in returned).astype(jnp.bfloat16)
     return (

time: 70 us -> 59 us (0.84)
  blocking collectives: 20.5 us -> 15 us
  waiting for transfers between devices: 19.8 us -> 17 us
  starting transfers between devices: 12.2 us -> 9.48 us
    psum x1, blocking collectives: 20.5 us -> 15 us  [on_device(): lax.psum(jnp.sum(loss_terms), 'resp') / count_real]
    ppermute x6, waiting for transfers between devices: 19.8 us -> 17 us  [shifted(): return lax.ppermute(value, 'resp', [(i, (i + shift) % n) for i in range(n)])]
    ppermute x6, starting transfers between devices: 12.2 us -> 9.48 us  [shifted(): return lax.ppermute(value, 'resp', [(i, (i + shift) % n) for i in range(n)])]
    convert_element_type x0 -> x1, other arithmetic: none -> 1.06 us  [on_device(): (parts[1].astype(jnp.float32) + relayed.astype(jnp.float32)).astype(jnp.b...]
    convert_element_type x1, other arithmetic: 1.8 us -> 0.8 us  [on_device(): sum((r[1].astype(jnp.float32) for r in returned)).astype(jnp.bfloat16)]
    unnamed x11 -> x13, local copies, waits for them, and re-layouts: 1.81 us -> 1.72 us
  transfers between devices with their start and end apart: 6 -> 6, of which waited for: 2 -> 4; matrix products, arithmetic and copies ran while one was open for 1% -> 3% of each run, Pallas kernels for 0% -> 0%
where the time goes in v5:
time: 59 us; the launch traced here: 58.7 us
  waiting for transfers between devices  17 us (29%)
  blocking collectives  15 us (25%)
  starting transfers between devices  9.48 us (16%)
  Pallas kernels  7.71 us (13%)
  between operations  5.32 us (9%)
  other arithmetic  2.47 us (4%)
  local copies, waits for them, and re-layouts  1.73 us (3%)
    ppermute x6, waiting for transfers between devices, shifted(): return lax.ppermute(value, 'resp', [(i, (i + shift) % n) for i in range(n)])  17 us
    psum x1, blocking collectives, on_device(): lax.psum(jnp.sum(loss_terms), 'resp') / count_real  15 us
    ppermute x6, starting transfers between devices, shifted(): return lax.ppermute(value, 'resp', [(i, (i + shift) % n) for i in range(n)])  9.48 us
    pallas_call x1, Pallas kernels, on_device(): pl.pallas_call(functools.partial(attention_kernel, n), grid=(KV_HEADS,),...  7.71 us
    unnamed x13, local copies, waits for them, and re-layouts  1.72 us
  transfers between devices with their start and end apart: 6, of which 4 were waited for; matrix products, arithmetic and copies ran while one was open for 3% of the time, Pallas kernels for 0%

profile of v5, /device:TPU:0, one launch (start us, length us, event | category | flops | bytes accessed | tf_op | source)
XLA Modules:
  0.0 58.7 jit_solution(7527662749298427649)
XLA Ops:
  0.6 0.0 copy-start.5
  0.6 0.9 %constant_dynamic-update-slice_fusion.1 = bf16[2,128,512]{2,1,0:T(8,128)(2,1)S(1)} fusion(bf16[1,128,512]{2,1,0:T(8,128)(2,1)} %param.14), kind=kLoop, calls=%fused_computation.6 | loop fusion | bytes 262144
  1.6 0.0 copy-done.5
  1.6 0.0 copy-start
  1.6 3.1 %collective-permute-start = (bf16[2,128,512]{2,1,0:T(8,128)(2,1)S(1)}, bf16[2,128,512]{2,1,0:T(8,128)(2,1)S(1)}, u32[]{:S(2)}, u32[]{:S(2)}) collective-permute-start(bf16[2,128,512]{2,1,0:T(8,128)(2,1)S(1)} %constant_dynamic-update-slice_fusion.rest_0_), channel_id=1, source_target_pairs={{0,1},{1,2},{2,3},{3,0},{4,5},{5,6},{6,7},{7,4},{8,9},{9,10},{10,1... | collective-permute-start | bytes 786440 | tf_op jit(solution)/shard_map/ppermute | solution.py:75
  4.7 2.1 %collective-permute-start.1 = (bf16[2,128,512]{2,1,0:T(8,128)(2,1)S(1)}, bf16[2,128,512]{2,1,0:T(8,128)(2,1)S(1)}, u32[]{:S(2)}, u32[]{:S(2)}) collective-permute-start(bf16[2,128,512]{2,1,0:T(8,128)(2,1)S(1)} %constant_dynamic-update-slice_fusion.rest_0_), channel_id=1, source_target_pairs={{0,3},{1,0},{2,1},{3,2},{4,7},{5,4},{6,5},{7,6},{8,11},{9,8},{10,9... | collective-permute-start | bytes 786440 | tf_op jit(solution)/shard_map/ppermute | solution.py:75
  6.8 7.1 %collective-permute-done.rest_1_ = bf16[2,128,512]{2,1,0:T(8,128)(2,1)S(1)} collective-permute-done((bf16[2,128,512]{2,1,0:T(8,128)(2,1)S(1)}, bf16[2,128,512]{2,1,0:T(8,128)(2,1)S(1)}, u32[]{:S(2)}, u32[]{:S(2)}) %collective-permute-start) | collective-permute-done | bytes 262176 | tf_op jit(solution)/shard_map/ppermute | solution.py:75
  13.9 0.0 copy-start.1
  13.9 0.0 collective-permute-start.2
  16.0 15.0 %psum.7 = f32[]{:T(128)} all-reduce(f32[]{:T(128)} %bitcast.2), channel_id=1, replica_groups=mesh['groups'=2,'prompt'=4,'resp'=4] {'resp'}, use_global_device_ids=true, to_apply=%region_0.1 | all-reduce | flops 1 | bytes 8 | tf_op jit(solution)/shard_map/psum | solution.py:108
  32.4 0.6 %fusion.factor_ref = f32[32,1]{1,0:T(8,128)} fusion(f32[]{:T(128)} %bitcast.6, s32[]{:T(128)} %bitcast.14), kind=kLoop, calls=%fused_computation.4 | loop fusion | flops 64 | bytes 136 | tf_op jit(solution)/shard_map/jit(_where)/select_n | solution.py:110
  33.0 0.0 collective-permute-done.1.rest_2_
  33.0 0.0 copy-start.2
  33.0 0.0 collective-permute-done.2.rest_3_
  33.0 0.0 copy-start.3
  33.1 0.0 copy-done
  33.1 0.0 copy-done.1
  33.1 0.7 %copy-done.2 = bf16[2,128,512]{2,1,0:T(8,128)(2,1)} copy-done((bf16[2,128,512]{2,1,0:T(8,128)(2,1)}, bf16[2,128,512]{2,1,0:T(8,128)(2,1)S(1)}, u32[]{:S(2)}) %copy-start.2) | copy-done | bytes 262168
  33.7 0.1 copy-done.3
  33.8 7.7 %shard_map.145 = (bf16[32,8192]{1,0:T(8,128)(2,1)}, bf16[32,512]{1,0:T(8,128)(2,1)}, bf16[32,512]{1,0:T(8,128)(2,1)}, bf16[2,128,512]{2,1,0:T(8,128)(2,1)}, bf16...) custom-call(f32[32,1]{1,0:T(8,128)} %fusion.factor_ref, ...), custom_call_target="tpu_custom_call" | custom-call | tf_op jit(solution)/shard_map/pallas_call | solution.py:115
  41.5 0.3 collective-permute-start.4
  41.8 1.8 %collective-permute-start.3 = (bf16[2,128,512]{2,1,0:T(8,128)(2,1)}, bf16[2,128,512]{2,1,0:T(8,128)(2,1)S(1)}, u32[]{:S(2)}, u32[]{:S(2)}) collective-permute-start(bf16[2,128,512]{2,1,0:T(8,128)(2,1)} %get-tuple-element.28), channel_id=1, source_target_pairs={{0,1},{1,2},{2,3},{3,0},{4,5},{5,6},{6,7},{7,4},{8,9},{9,10},{10,1... | collective-permute-start | bytes 786440 | tf_op jit(solution)/shard_map/ppermute | solution.py:75
  43.6 4.6 %collective-permute-done.4 = bf16[2,128,512]{2,1,0:T(8,128)(2,1)S(1)} collective-permute-done((bf16[2,128,512]{2,1,0:T(8,128)(2,1)}, bf16[2,128,512]{2,1,0:T(8,128)(2,1)S(1)}, u32[]{:S(2)}, u32[]{:S(2)}) %collective-permute-start.4) | collective-permute-done | bytes 262176 | tf_op jit(solution)/shard_map/ppermute | solution.py:75
  48.2 0.0 copy-start.4
  48.2 1.1 %add_convert_fusion = bf16[2,128,512]{2,1,0:T(8,128)(2,1)S(1)} fusion(bf16[2,128,512]{2,1,0:T(8,128)(2,1)S(1)} %collective-permute-done.4, bf16[2,128,512]{2,1,0:T(8,128)(2,1)} %get-tuple-element.29), kind=kLoop, calls=%fused_computation | loop fusion | flops 524288 | bytes 786432 | tf_op jit(solution)/shard_map/convert_element_type | solution.py:143
  49.2 2.2 %collective-permute-start.5 = (bf16[2,128,512]{2,1,0:T(8,128)(2,1)S(1)}, bf16[2,128,512]{2,1,0:T(8,128)(2,1)S(1)}, u32[]{:S(2)}, u32[]{:S(2)}) collective-permute-start(bf16[2,128,512]{2,1,0:T(8,128)(2,1)S(1)} %add_convert_fusion), channel_id=1, source_target_pairs={{0,3},{1,0},{2,1},{3,2},{4,7},{5,4},{6,5},{7,6},{8,11},{9,8},{10,9... | collective-permute-start | bytes 786440 | tf_op jit(solution)/shard_map/ppermute | solution.py:75
  51.5 1.5 %collective-permute-done.3 = bf16[2,128,512]{2,1,0:T(8,128)(2,1)S(1)} collective-permute-done((bf16[2,128,512]{2,1,0:T(8,128)(2,1)}, bf16[2,128,512]{2,1,0:T(8,128)(2,1)S(1)}, u32[]{:S(2)}, u32[]{:S(2)}) %collective-permute-start.3) | collective-permute-done | bytes 262176 | tf_op jit(solution)/shard_map/ppermute | solution.py:75
  53.0 3.8 %collective-permute-done.5 = bf16[2,128,512]{2,1,0:T(8,128)(2,1)S(1)} collective-permute-done((bf16[2,128,512]{2,1,0:T(8,128)(2,1)S(1)}, bf16[2,128,512]{2,1,0:T(8,128)(2,1)S(1)}, u32[]{:S(2)}, u32[]{:S(2)}) %collective-permute-start.5) | collective-permute-done | bytes 262176 | tf_op jit(solution)/shard_map/ppermute | solution.py:75
  56.8 0.0 copy-done.4
  56.8 0.8 %add_convert_fusion.1 = (bf16[1,128,512]{2,1,0:T(8,128)(2,1)}, bf16[1,128,512]{2,1,0:T(8,128)(2,1)}) fusion(bf16[2,128,512]{2,1,0:T(8,128)(2,1)S(1)} %collective-permute-done.5, bf16[2,128,512]{2,1,0:T(8,128)(2,1)S(1)} %collective-permute-done.3, bf16[2,128,512]{2,1,0:T(8,128)(2,1)S(1)} %copy-done.4), kind=kLoop, calls=%fused_computation.1 | loop fusion | flops 786432 | bytes 1048576 | tf_op jit(solution)/shard_map/convert_element_type | solution.py:148
  (1 shorter events, 0.0 us)
Async XLA Ops:
  0.6 1.0 %copy-start.5 = (bf16[1,128,512]{2,1,0:T(8,128)(2,1)S(1)}, bf16[1,128,512]{2,1,0:T(8,128)(2,1)}, u32[]{:S(2)}) copy-start(bf16[1,128,512]{2,1,0:T(8,128)(2,1)} %param.15) | copy-start | bytes 393220
  1.6 31.4 %copy-start = (bf16[2,128,512]{2,1,0:T(8,128)(2,1)}, bf16[2,128,512]{2,1,0:T(8,128)(2,1)S(1)}, u32[]{:S(2)}) copy-start(bf16[2,128,512]{2,1,0:T(8,128)(2,1)S(1)} %constant_dynamic-update-slice_fusion.rest_0_) | copy-start | bytes 786436
  1.6 12.3 %collective-permute-start = (bf16[2,128,512]{2,1,0:T(8,128)(2,1)S(1)}, bf16[2,128,512]{2,1,0:T(8,128)(2,1)S(1)}, u32[]{:S(2)}, u32[]{:S(2)}) collective-permute-start(bf16[2,128,512]{2,1,0:T(8,128)(2,1)S(1)} %constant_dynamic-update-slice_fusion.rest_0_), channel_id=1, source_target_pairs={{0,1},{1,2},{2,3},{3,0},{4,5},{5,6},{6,7},{7,4},{8,9},{9,10},{10,1... | collective-permute-start | bytes 786440 | tf_op jit(solution)/shard_map/ppermute | solution.py:75
  4.7 28.3 %collective-permute-start.1 = (bf16[2,128,512]{2,1,0:T(8,128)(2,1)S(1)}, bf16[2,128,512]{2,1,0:T(8,128)(2,1)S(1)}, u32[]{:S(2)}, u32[]{:S(2)}) collective-permute-start(bf16[2,128,512]{2,1,0:T(8,128)(2,1)S(1)} %constant_dynamic-update-slice_fusion.rest_0_), channel_id=1, source_target_pairs={{0,3},{1,0},{2,1},{3,2},{4,7},{5,4},{6,5},{7,6},{8,11},{9,8},{10,9... | collective-permute-start | bytes 786440 | tf_op jit(solution)/shard_map/ppermute | solution.py:75
  13.9 19.1 %copy-start.1 = (bf16[2,128,512]{2,1,0:T(8,128)(2,1)}, bf16[2,128,512]{2,1,0:T(8,128)(2,1)S(1)}, u32[]{:S(2)}) copy-start(bf16[2,128,512]{2,1,0:T(8,128)(2,1)S(1)} %collective-permute-done.rest_1_) | copy-start | bytes 786436
  13.9 19.1 %collective-permute-start.2 = (bf16[2,128,512]{2,1,0:T(8,128)(2,1)S(1)}, bf16[2,128,512]{2,1,0:T(8,128)(2,1)S(1)}, u32[]{:S(2)}, u32[]{:S(2)}) collective-permute-start(bf16[2,128,512]{2,1,0:T(8,128)(2,1)S(1)} %collective-permute-done.rest_1_), channel_id=1, source_target_pairs={{0,1},{1,2},{2,3},{3,0},{4,5},{5,6},{6,7},{7,4},{8,9},{9,10},{10,1... | collective-permute-start | bytes 786440 | tf_op jit(solution)/shard_map/ppermute | solution.py:75
  33.0 0.7 %copy-start.2 = (bf16[2,128,512]{2,1,0:T(8,128)(2,1)}, bf16[2,128,512]{2,1,0:T(8,128)(2,1)S(1)}, u32[]{:S(2)}) copy-start(bf16[2,128,512]{2,1,0:T(8,128)(2,1)S(1)} %collective-permute-done.1.rest_2_) | copy-start | bytes 786436
  33.0 0.8 %copy-start.3 = (bf16[2,128,512]{2,1,0:T(8,128)(2,1)}, bf16[2,128,512]{2,1,0:T(8,128)(2,1)S(1)}, u32[]{:S(2)}) copy-start(bf16[2,128,512]{2,1,0:T(8,128)(2,1)S(1)} %collective-permute-done.2.rest_3_) | copy-start | bytes 786436
  41.5 6.6 %collective-permute-start.4 = (bf16[2,128,512]{2,1,0:T(8,128)(2,1)}, bf16[2,128,512]{2,1,0:T(8,128)(2,1)S(1)}, u32[]{:S(2)}, u32[]{:S(2)}) collective-permute-start(bf16[2,128,512]{2,1,0:T(8,128)(2,1)} %get-tuple-element.30), channel_id=1, source_target_pairs={{0,3},{1,0},{2,1},{3,2},{4,7},{5,4},{6,5},{7,6},{8,11},{9,8},{10,9... | collective-permute-start | bytes 786440 | tf_op jit(solution)/shard_map/ppermute | solution.py:75
  41.8 11.2 %collective-permute-start.3 = (bf16[2,128,512]{2,1,0:T(8,128)(2,1)}, bf16[2,128,512]{2,1,0:T(8,128)(2,1)S(1)}, u32[]{:S(2)}, u32[]{:S(2)}) collective-permute-start(bf16[2,128,512]{2,1,0:T(8,128)(2,1)} %get-tuple-element.28), channel_id=1, source_target_pairs={{0,1},{1,2},{2,3},{3,0},{4,5},{5,6},{6,7},{7,4},{8,9},{9,10},{10,1... | collective-permute-start | bytes 786440 | tf_op jit(solution)/shard_map/ppermute | solution.py:75
  48.2 8.6 %copy-start.4 = (bf16[2,128,512]{2,1,0:T(8,128)(2,1)S(1)}, bf16[2,128,512]{2,1,0:T(8,128)(2,1)}, u32[]{:S(2)}) copy-start(bf16[2,128,512]{2,1,0:T(8,128)(2,1)} %get-tuple-element.27) | copy-start | bytes 786436
  49.2 7.5 %collective-permute-start.5 = (bf16[2,128,512]{2,1,0:T(8,128)(2,1)S(1)}, bf16[2,128,512]{2,1,0:T(8,128)(2,1)S(1)}, u32[]{:S(2)}, u32[]{:S(2)}) collective-permute-start(bf16[2,128,512]{2,1,0:T(8,128)(2,1)S(1)} %add_convert_fusion), channel_id=1, source_target_pairs={{0,3},{1,0},{2,1},{3,2},{4,7},{5,4},{6,5},{7,6},{8,11},{9,8},{10,9... | collective-permute-start | bytes 786440 | tf_op jit(solution)/shard_map/ppermute | solution.py:75

commit v6 on v5

--- a/solution.py
+++ b/solution.py
@@ -17,24 +17,33 @@
 masked_score = -1e30
 
 
-def attention_kernel(n_pieces, factor_ref, q_ref, cot_ref, kown_ref, vown_ref, *rest):
+def attention_kernel(n_pieces, scalar_ref, q_ref, cot_ref, kown_ref, vown_ref, *rest):
     piece_refs = rest[:n_pieces]
     dq_ref, dkown_ref, dvown_ref = rest[n_pieces:n_pieces + 3]
-    part_refs = rest[n_pieces + 3:]
+    part_refs = rest[n_pieces + 3:-1]
+    loss_ref = rest[-1]
     group_size = HEADS // KV_HEADS
     resp_len = q_ref.shape[0]
-    piece_len = piece_refs[0].shape[1]
+    piece_len = part_refs[0].shape[1]
     scaling = 1.0 / math.sqrt(HEAD_DIM)
     rows = group_size * resp_len
-    factor = factor_ref[...]
+    token = lax.broadcasted_iota(jnp.int32, (resp_len, 1), 0).astype(jnp.float32)
+    factor = jnp.where(token < scalar_ref[1], scalar_ref[0], 0.0)
+
+    @pl.when(pl.program_id(0) == 0)
+    def _():
+        term_total = scalar_ref[2]
+        for r in piece_refs[1:]:
+            term_total = term_total + jnp.sum(r[0, piece_len:piece_len + 8, :].astype(jnp.float32))
+        loss_ref[0] = term_total / scalar_ref[3]
     contract_minor = (((1,), (1,)), ((), ()))
     contract_major = (((0,), (0,)), ((), ()))
     q_all = q_ref[...]
     g_all = (cot_ref[...].astype(jnp.float32) * factor).astype(jnp.bfloat16)
     q_rows = jnp.concatenate([q_all[:, h * HEAD_DIM:(h + 1) * HEAD_DIM] for h in range(group_size)], axis=0)
     g_rows = jnp.concatenate([g_all[:, h * HEAD_DIM:(h + 1) * HEAD_DIM] for h in range(group_size)], axis=0)
-    k_pre = jnp.concatenate([r[0] for r in piece_refs], axis=0)
-    v_pre = jnp.concatenate([r[1] for r in piece_refs], axis=0)
+    k_pre = jnp.concatenate([r[0, :piece_len] for r in piece_refs], axis=0)
+    v_pre = jnp.concatenate([r[1, :piece_len] for r in piece_refs], axis=0)
     k_own = kown_ref[...]
     v_own = vown_ref[...]
     s_pre = lax.dot_general(k_pre, q_rows, contract_minor, preferred_element_type=jnp.float32) * scaling
@@ -71,6 +80,14 @@
         dq_ref[:, h * HEAD_DIM:(h + 1) * HEAD_DIM] = dq_rows[h * resp_len:(h + 1) * resp_len].astype(jnp.bfloat16)
 
 
+def split_words(value):
+    high = value.astype(jnp.bfloat16)
+    rest = value - high.astype(jnp.float32)
+    middle = rest.astype(jnp.bfloat16)
+    low = (rest - middle.astype(jnp.float32)).astype(jnp.bfloat16)
+    return jnp.stack([high, middle, low])
+
+
 def shifted(value, shift, n):
     return lax.ppermute(value, "resp", [(i, (i + shift) % n) for i in range(n)])
 
@@ -92,12 +109,6 @@
     assert slot_count == 1
     resp_len = queries.shape[2]
     piece_len = prefix_keys.shape[1]
-    local_kv = jnp.stack([prefix_keys[0], prefix_values[0]])
-    if n == 4:
-        from_left = shifted(local_kv, 1, n)
-        pieces = [local_kv, from_left, shifted(local_kv, -1, n), shifted(from_left, 1, n)]
-    else:
-        pieces = [local_kv] + [shifted(local_kv, k, n) for k in range(1, n)]
     live_count = counts[0]
     count_real = live_count.astype(jnp.float32)
     slot_ids = lax.axis_index("resp") * slot_count + jnp.arange(slot_count, dtype=jnp.int32)
@@ -105,18 +116,24 @@
     margin = policy_likelihood[0] - reference_likelihood[0]
     weight = jnp.where(live_slots, 2.0 * jax.nn.sigmoid(loss_beta * margin) / count_real, 0.0)
     loss_terms = jnp.where(live_slots, 2.0 / loss_beta * jax.nn.softplus(loss_beta * margin), 0.0)
-    forget_loss = (lax.psum(jnp.sum(loss_terms), "resp") / count_real).reshape(1)
-    positions = jnp.arange(resp_len, dtype=jnp.int32)
-    factor = jnp.where(positions[None, :] < lengths[0][:, None], weight[:, None], 0.0)
-    factor = factor.reshape(resp_len, 1).astype(jnp.float32)
-    forget_loss, factor, *pieces = lax.optimization_barrier((forget_loss, factor, *pieces))
+    own_term = jnp.sum(loss_terms)
+    word_rows = jnp.zeros((2, 16, prefix_keys.shape[2]), jnp.bfloat16)
+    word_rows = word_rows.at[0, 0, 0:3].set(split_words(own_term))
+    local_kv = jnp.concatenate([jnp.stack([prefix_keys[0], prefix_values[0]]), word_rows], axis=1)
+    if n == 4:
+        from_left = shifted(local_kv, 1, n)
+        pieces = [local_kv, from_left, shifted(local_kv, -1, n), shifted(from_left, 1, n)]
+    else:
+        pieces = [local_kv] + [shifted(local_kv, k, n) for k in range(1, n)]
+    scalars = jnp.stack([weight[0], lengths[0][0].astype(jnp.float32), own_term, count_real])
     group_width = (HEADS // KV_HEADS) * HEAD_DIM
-    piece_block = pl.BlockSpec((2, piece_len, HEAD_DIM), lambda g: (0, 0, g))
+    piece_block = pl.BlockSpec((2, piece_len + 16, HEAD_DIM), lambda g: (0, 0, g))
+    part_block = pl.BlockSpec((2, piece_len, HEAD_DIM), lambda g: (0, 0, g))
     results = pl.pallas_call(
         functools.partial(attention_kernel, n),
         grid=(KV_HEADS,),
         in_specs=[
-            pl.BlockSpec((resp_len, 1), lambda g: (0, 0)),
+            pl.BlockSpec(memory_space=pltpu.SMEM),
             pl.BlockSpec((resp_len, group_width), lambda g: (0, g)),
             pl.BlockSpec((resp_len, group_width), lambda g: (0, g)),
             pl.BlockSpec((resp_len, HEAD_DIM), lambda g: (0, g)),
@@ -128,16 +145,19 @@
             pl.BlockSpec((resp_len, HEAD_DIM), lambda g: (0, g)),
             pl.BlockSpec((resp_len, HEAD_DIM), lambda g: (0, g)),
         ]
-        + [piece_block] * n,
+        + [part_block] * n
+        + [pl.BlockSpec(memory_space=pltpu.SMEM)],
         out_shape=[
             jax.ShapeDtypeStruct(queries.shape[2:], jnp.bfloat16),
             jax.ShapeDtypeStruct(resp_keys.shape[2:], jnp.bfloat16),
             jax.ShapeDtypeStruct(resp_values.shape[2:], jnp.bfloat16),
         ]
-        + [jax.ShapeDtypeStruct(local_kv.shape, jnp.bfloat16) for _ in range(n)],
-    )(factor, queries[0, 0], cotangent[0, 0], resp_keys[0, 0], resp_values[0, 0], *pieces)
+        + [jax.ShapeDtypeStruct((2,) + prefix_keys.shape[1:], jnp.bfloat16) for _ in range(n)]
+        + [jax.ShapeDtypeStruct((1,), jnp.float32)],
+    )(scalars, queries[0, 0], cotangent[0, 0], resp_keys[0, 0], resp_values[0, 0], *pieces)
     grad_q, grad_k, grad_v = results[:3]
-    parts = results[3:]
+    parts = results[3:-1]
+    forget_loss = results[-1]
     if n == 4:
         relayed = shifted(parts[3], -1, n)
         merged = (parts[1].astype(jnp.float32) + relayed.astype(jnp.float32)).astype(jnp.bfloat16)

time: 59 us -> 56 us (0.949)
  blocking collectives: 15 us -> 0 us
  waiting for transfers between devices: 17 us -> 30.1 us
  between operations: 5.32 us -> 3.54 us
  other arithmetic: 2.47 us -> 3.51 us
  local copies, waits for them, and re-layouts: 1.73 us -> 0.71 us
    psum x1 -> x0, blocking collectives: 15 us -> none  [on_device(): lax.psum(jnp.sum(loss_terms), 'resp') / count_real]
    ppermute x6, waiting for transfers between devices: 17 us -> 30.1 us  [shifted(): return lax.ppermute(value, 'resp', [(i, (i + shift) % n) for i in range(n)])]
    unnamed x13 -> x10, local copies, waits for them, and re-layouts: 1.72 us -> 0.71 us
    concatenate x0 -> x1, other arithmetic: none -> 0.99 us  [on_device(): jnp.concatenate([jnp.stack([prefix_keys[0], prefix_values[0]]), word_rows...]
    another operation x0 -> x2, other arithmetic: none -> 0.67 us  [the longest x1 0.59 us: on_device(): jnp.stack([weight[0], lengths[0][0].astype(jnp.float32), own_term, count_...]
    select_n x1 -> x0, other arithmetic: 0.61 us -> none  [on_device(): jnp.where(positions[None, :] < lengths[0][:, None], weight[:, None], 0.0)]
  transfers between devices with their start and end apart: 6 -> 6, of which waited for: 4 -> 6; matrix products, arithmetic and copies ran while one was open for 3% -> 3% of each run, Pallas kernels for 0% -> 0%
where the time goes in v6:
time: 56 us; the launch traced here: 55.8 us
  waiting for transfers between devices  30.1 us (54%)
  starting transfers between devices  9.81 us (18%)
  Pallas kernels  8.09 us (14%)
  between operations  3.54 us (6%)
  other arithmetic  3.51 us (6%)
  local copies, waits for them, and re-layouts  0.71 us (1%)
    ppermute x6, waiting for transfers between devices, shifted(): return lax.ppermute(value, 'resp', [(i, (i + shift) % n) for i in range(n)])  30.1 us
    ppermute x6, starting transfers between devices, shifted(): return lax.ppermute(value, 'resp', [(i, (i + shift) % n) for i in range(n)])  9.81 us
    pallas_call x1, Pallas kernels, on_device(): pl.pallas_call(functools.partial(attention_kernel, n), grid=(KV_HEADS,),...  8.09 us
  transfers between devices with their start and end apart: 6, of which 6 were waited for; matrix products, arithmetic and copies ran while one was open for 3% of the time, Pallas kernels for 0%

profile of v6, /device:TPU:0, one launch (start us, length us, event | category | flops | bytes accessed | tf_op | source)
XLA Modules:
  0.0 55.8 jit_solution(69149058070258507)
XLA Ops:
  2.7 0.1 maximum_bitcast_fusion
  2.8 1.0 %fusion.1.rest_0_ = bf16[2,144,512]{2,1,0:T(8,128)(2,1)S(1)} fusion(bf16[1,1,3]{2,1,0:T(2,128)(2,1)S(1)} %maximum_bitcast_fusion, bf16[1,128,512]{2,1,0:T(8,128)(2,1)} %param.17, bf16[1,128,512]{2,1,0:T(8,128)(2,1)} %param.16), kind=kLoop, calls=%fused_computation.3 | loop fusion | flops 1179648 | bytes 557062 | tf_op jit(solution)/shard_map/concatenate | solution.py:122
  3.8 0.0 copy-start
  3.8 3.1 %collective-permute-start = (bf16[2,144,512]{2,1,0:T(8,128)(2,1)S(1)}, bf16[2,144,512]{2,1,0:T(8,128)(2,1)S(1)}, u32[]{:S(2)}, u32[]{:S(2)}) collective-permute-start(bf16[2,144,512]{2,1,0:T(8,128)(2,1)S(1)} %fusion.1.rest_0_), channel_id=1, source_target_pairs={{0,1},{1,2},{2,3},{3,0},{4,5},{5,6},{6,7},{7,4},{8,9},{9,10},{10,1... | collective-permute-start | bytes 884744 | tf_op jit(solution)/shard_map/ppermute | solution.py:92
  6.8 2.1 %collective-permute-start.1 = (bf16[2,144,512]{2,1,0:T(8,128)(2,1)S(1)}, bf16[2,144,512]{2,1,0:T(8,128)(2,1)S(1)}, u32[]{:S(2)}, u32[]{:S(2)}) collective-permute-start(bf16[2,144,512]{2,1,0:T(8,128)(2,1)S(1)} %fusion.1.rest_0_), channel_id=1, source_target_pairs={{0,3},{1,0},{2,1},{3,2},{4,7},{5,4},{6,5},{7,6},{8,11},{9,8},{10,9... | collective-permute-start | bytes 884744 | tf_op jit(solution)/shard_map/ppermute | solution.py:92
  8.9 7.8 %collective-permute-done.rest_1_ = bf16[2,144,512]{2,1,0:T(8,128)(2,1)S(1)} collective-permute-done((bf16[2,144,512]{2,1,0:T(8,128)(2,1)S(1)}, bf16[2,144,512]{2,1,0:T(8,128)(2,1)S(1)}, u32[]{:S(2)}, u32[]{:S(2)}) %collective-permute-start) | collective-permute-done | bytes 294944 | tf_op jit(solution)/shard_map/ppermute | solution.py:92
  16.8 0.0 copy-start.1
  16.8 0.0 collective-permute-start.2
  17.6 0.6 %pad_maximum_fusion.scalar_ref = f32[4]{0:T(128)} fusion(f32[1]{0:T(128)S(6)} %convert_element_type.64, f32[1]{0:T(128)} %select_n.13, f32[1]{0:T(128)} %bitcast.2, f32[1]{0:T(128)S(6)} %select_n.11), kind=kLoop, calls=%fused_computation.6 | loop fusion | flops 12 | bytes 32 | tf_op jit(solution)/shard_map/stack | solution.py:128
  18.2 3.7 %collective-permute-done.1.rest_2_ = bf16[2,144,512]{2,1,0:T(8,128)(2,1)S(1)} collective-permute-done((bf16[2,144,512]{2,1,0:T(8,128)(2,1)S(1)}, bf16[2,144,512]{2,1,0:T(8,128)(2,1)S(1)}, u32[]{:S(2)}, u32[]{:S(2)}) %collective-permute-start.1) | collective-permute-done | bytes 294944 | tf_op jit(solution)/shard_map/ppermute | solution.py:92
  21.9 0.0 copy-start.2
  21.9 6.7 %collective-permute-done.2.rest_3_ = bf16[2,144,512]{2,1,0:T(8,128)(2,1)S(1)} collective-permute-done((bf16[2,144,512]{2,1,0:T(8,128)(2,1)S(1)}, bf16[2,144,512]{2,1,0:T(8,128)(2,1)S(1)}, u32[]{:S(2)}, u32[]{:S(2)}) %collective-permute-start.2) | collective-permute-done | bytes 294944 | tf_op jit(solution)/shard_map/ppermute | solution.py:92
  28.6 0.0 copy-start.3
  28.6 0.0 copy-done
  28.6 0.0 copy-done.1
  28.6 0.0 copy-done.2
  28.6 0.7 %copy-done.3 = bf16[2,144,512]{2,1,0:T(8,128)(2,1)} copy-done((bf16[2,144,512]{2,1,0:T(8,128)(2,1)}, bf16[2,144,512]{2,1,0:T(8,128)(2,1)S(1)}, u32[]{:S(2)}) %copy-start.3) | copy-done | bytes 294936
  29.3 8.1 %shard_map.145 = (bf16[32,8192]{1,0:T(8,128)(2,1)}, bf16[32,512]{1,0:T(8,128)(2,1)}, bf16[32,512]{1,0:T(8,128)(2,1)}, bf16[2,128,512]{2,1,0:T(8,128)(2,1)}, bf16...) custom-call(f32[4]{0:T(128)} %pad_maximum_fusion.scalar_ref, ...), custom_call_target="tpu_custom_call" | custom-call | tf_op jit(solution)/shard_map/pallas_call | solution.py:132
  37.4 1.7 %collective-permute-start.4 = (bf16[2,128,512]{2,1,0:T(8,128)(2,1)}, bf16[2,128,512]{2,1,0:T(8,128)(2,1)S(1)}, u32[]{:S(2)}, u32[]{:S(2)}) collective-permute-start(bf16[2,128,512]{2,1,0:T(8,128)(2,1)} %get-tuple-element.32), channel_id=1, source_target_pairs={{0,3},{1,0},{2,1},{3,2},{4,7},{5,4},{6,5},{7,6},{8,11},{9,8},{10,9... | collective-permute-start | bytes 786440 | tf_op jit(solution)/shard_map/ppermute | solution.py:92
  39.1 0.3 collective-permute-start.3
  39.4 7.9 %collective-permute-done.4 = bf16[2,128,512]{2,1,0:T(8,128)(2,1)S(1)} collective-permute-done((bf16[2,128,512]{2,1,0:T(8,128)(2,1)}, bf16[2,128,512]{2,1,0:T(8,128)(2,1)S(1)}, u32[]{:S(2)}, u32[]{:S(2)}) %collective-permute-start.4) | collective-permute-done | bytes 262176 | tf_op jit(solution)/shard_map/ppermute | solution.py:92
  47.4 0.0 copy-start.4
  47.4 1.1 %add_convert_fusion = bf16[2,128,512]{2,1,0:T(8,128)(2,1)S(1)} fusion(bf16[2,128,512]{2,1,0:T(8,128)(2,1)S(1)} %collective-permute-done.4, bf16[2,128,512]{2,1,0:T(8,128)(2,1)} %get-tuple-element.31), kind=kLoop, calls=%fused_computation.2 | loop fusion | flops 524288 | bytes 786432 | tf_op jit(solution)/shard_map/convert_element_type | solution.py:163
  48.4 2.6 %collective-permute-start.5 = (bf16[2,128,512]{2,1,0:T(8,128)(2,1)S(1)}, bf16[2,128,512]{2,1,0:T(8,128)(2,1)S(1)}, u32[]{:S(2)}, u32[]{:S(2)}) collective-permute-start(bf16[2,128,512]{2,1,0:T(8,128)(2,1)S(1)} %add_convert_fusion), channel_id=1, source_target_pairs={{0,3},{1,0},{2,1},{3,2},{4,7},{5,4},{6,5},{7,6},{8,11},{9,8},{10,9... | collective-permute-start | bytes 786440 | tf_op jit(solution)/shard_map/ppermute | solution.py:92
  51.0 1.2 %collective-permute-done.3 = bf16[2,128,512]{2,1,0:T(8,128)(2,1)S(1)} collective-permute-done((bf16[2,128,512]{2,1,0:T(8,128)(2,1)}, bf16[2,128,512]{2,1,0:T(8,128)(2,1)S(1)}, u32[]{:S(2)}, u32[]{:S(2)}) %collective-permute-start.3) | collective-permute-done | bytes 262176 | tf_op jit(solution)/shard_map/ppermute | solution.py:92
  52.2 2.8 %collective-permute-done.5 = bf16[2,128,512]{2,1,0:T(8,128)(2,1)S(1)} collective-permute-done((bf16[2,128,512]{2,1,0:T(8,128)(2,1)S(1)}, bf16[2,128,512]{2,1,0:T(8,128)(2,1)S(1)}, u32[]{:S(2)}, u32[]{:S(2)}) %collective-permute-start.5) | collective-permute-done | bytes 262176 | tf_op jit(solution)/shard_map/ppermute | solution.py:92
  55.0 0.0 copy-done.4
  55.0 0.8 %add_convert_fusion.1 = (bf16[1,128,512]{2,1,0:T(8,128)(2,1)}, bf16[1,128,512]{2,1,0:T(8,128)(2,1)}) fusion(bf16[2,128,512]{2,1,0:T(8,128)(2,1)S(1)} %collective-permute-done.5, bf16[2,128,512]{2,1,0:T(8,128)(2,1)S(1)} %collective-permute-done.3, bf16[2,128,512]{2,1,0:T(8,128)(2,1)S(1)} %copy-done.4), kind=kLoop, calls=%fused_computation.4 | loop fusion | flops 786432 | bytes 1048576 | tf_op jit(solution)/shard_map/convert_element_type | solution.py:168
Async XLA Ops:
  3.8 24.8 %copy-start = (bf16[2,144,512]{2,1,0:T(8,128)(2,1)}, bf16[2,144,512]{2,1,0:T(8,128)(2,1)S(1)}, u32[]{:S(2)}) copy-start(bf16[2,144,512]{2,1,0:T(8,128)(2,1)S(1)} %fusion.1.rest_0_) | copy-start | bytes 884740
  3.8 13.0 %collective-permute-start = (bf16[2,144,512]{2,1,0:T(8,128)(2,1)S(1)}, bf16[2,144,512]{2,1,0:T(8,128)(2,1)S(1)}, u32[]{:S(2)}, u32[]{:S(2)}) collective-permute-start(bf16[2,144,512]{2,1,0:T(8,128)(2,1)S(1)} %fusion.1.rest_0_), channel_id=1, source_target_pairs={{0,1},{1,2},{2,3},{3,0},{4,5},{5,6},{6,7},{7,4},{8,9},{9,10},{10,1... | collective-permute-start | bytes 884744 | tf_op jit(solution)/shard_map/ppermute | solution.py:92
  6.8 15.0 %collective-permute-start.1 = (bf16[2,144,512]{2,1,0:T(8,128)(2,1)S(1)}, bf16[2,144,512]{2,1,0:T(8,128)(2,1)S(1)}, u32[]{:S(2)}, u32[]{:S(2)}) collective-permute-start(bf16[2,144,512]{2,1,0:T(8,128)(2,1)S(1)} %fusion.1.rest_0_), channel_id=1, source_target_pairs={{0,3},{1,0},{2,1},{3,2},{4,7},{5,4},{6,5},{7,6},{8,11},{9,8},{10,9... | collective-permute-start | bytes 884744 | tf_op jit(solution)/shard_map/ppermute | solution.py:92
  16.8 11.8 %copy-start.1 = (bf16[2,144,512]{2,1,0:T(8,128)(2,1)}, bf16[2,144,512]{2,1,0:T(8,128)(2,1)S(1)}, u32[]{:S(2)}) copy-start(bf16[2,144,512]{2,1,0:T(8,128)(2,1)S(1)} %collective-permute-done.rest_1_) | copy-start | bytes 884740
  16.8 11.8 %collective-permute-start.2 = (bf16[2,144,512]{2,1,0:T(8,128)(2,1)S(1)}, bf16[2,144,512]{2,1,0:T(8,128)(2,1)S(1)}, u32[]{:S(2)}, u32[]{:S(2)}) collective-permute-start(bf16[2,144,512]{2,1,0:T(8,128)(2,1)S(1)} %collective-permute-done.rest_1_), channel_id=1, source_target_pairs={{0,1},{1,2},{2,3},{3,0},{4,5},{5,6},{6,7},{7,4},{8,9},{9,10},{10,1... | collective-permute-start | bytes 884744 | tf_op jit(solution)/shard_map/ppermute | solution.py:92
  21.9 6.7 %copy-start.2 = (bf16[2,144,512]{2,1,0:T(8,128)(2,1)}, bf16[2,144,512]{2,1,0:T(8,128)(2,1)S(1)}, u32[]{:S(2)}) copy-start(bf16[2,144,512]{2,1,0:T(8,128)(2,1)S(1)} %collective-permute-done.1.rest_2_) | copy-start | bytes 884740
  28.6 0.7 %copy-start.3 = (bf16[2,144,512]{2,1,0:T(8,128)(2,1)}, bf16[2,144,512]{2,1,0:T(8,128)(2,1)S(1)}, u32[]{:S(2)}) copy-start(bf16[2,144,512]{2,1,0:T(8,128)(2,1)S(1)} %collective-permute-done.2.rest_3_) | copy-start | bytes 884740
  37.4 10.0 %collective-permute-start.4 = (bf16[2,128,512]{2,1,0:T(8,128)(2,1)}, bf16[2,128,512]{2,1,0:T(8,128)(2,1)S(1)}, u32[]{:S(2)}, u32[]{:S(2)}) collective-permute-start(bf16[2,128,512]{2,1,0:T(8,128)(2,1)} %get-tuple-element.32), channel_id=1, source_target_pairs={{0,3},{1,0},{2,1},{3,2},{4,7},{5,4},{6,5},{7,6},{8,11},{9,8},{10,9... | collective-permute-start | bytes 786440 | tf_op jit(solution)/shard_map/ppermute | solution.py:92
  39.1 13.1 %collective-permute-start.3 = (bf16[2,128,512]{2,1,0:T(8,128)(2,1)}, bf16[2,128,512]{2,1,0:T(8,128)(2,1)S(1)}, u32[]{:S(2)}, u32[]{:S(2)}) collective-permute-start(bf16[2,128,512]{2,1,0:T(8,128)(2,1)} %get-tuple-element.30), channel_id=1, source_target_pairs={{0,1},{1,2},{2,3},{3,0},{4,5},{5,6},{6,7},{7,4},{8,9},{9,10},{10,1... | collective-permute-start | bytes 786440 | tf_op jit(solution)/shard_map/ppermute | solution.py:92
  47.4 7.7 %copy-start.4 = (bf16[2,128,512]{2,1,0:T(8,128)(2,1)S(1)}, bf16[2,128,512]{2,1,0:T(8,128)(2,1)}, u32[]{:S(2)}) copy-start(bf16[2,128,512]{2,1,0:T(8,128)(2,1)} %get-tuple-element.29) | copy-start | bytes 786436
  48.4 6.6 %collective-permute-start.5 = (bf16[2,128,512]{2,1,0:T(8,128)(2,1)S(1)}, bf16[2,128,512]{2,1,0:T(8,128)(2,1)S(1)}, u32[]{:S(2)}, u32[]{:S(2)}) collective-permute-start(bf16[2,128,512]{2,1,0:T(8,128)(2,1)S(1)} %add_convert_fusion), channel_id=1, source_target_pairs={{0,3},{1,0},{2,1},{3,2},{4,7},{5,4},{6,5},{7,6},{8,11},{9,8},{10,9... | collective-permute-start | bytes 786440 | tf_op jit(solution)/shard_map/ppermute | solution.py:92

commit v7 on v6

--- a/solution.py
+++ b/solution.py
@@ -34,7 +34,7 @@
     def _():
         term_total = scalar_ref[2]
         for r in piece_refs[1:]:
-            term_total = term_total + jnp.sum(r[0, piece_len:piece_len + 8, :].astype(jnp.float32))
+            term_total = term_total + jnp.sum(r[2 * piece_len:2 * piece_len + 8, :].astype(jnp.float32))
         loss_ref[0] = term_total / scalar_ref[3]
     contract_minor = (((1,), (1,)), ((), ()))
     contract_major = (((0,), (0,)), ((), ()))
@@ -42,18 +42,19 @@
     g_all = (cot_ref[...].astype(jnp.float32) * factor).astype(jnp.bfloat16)
     q_rows = jnp.concatenate([q_all[:, h * HEAD_DIM:(h + 1) * HEAD_DIM] for h in range(group_size)], axis=0)
     g_rows = jnp.concatenate([g_all[:, h * HEAD_DIM:(h + 1) * HEAD_DIM] for h in range(group_size)], axis=0)
-    k_pre = jnp.concatenate([r[0, :piece_len] for r in piece_refs], axis=0)
-    v_pre = jnp.concatenate([r[1, :piece_len] for r in piece_refs], axis=0)
+    k_pre = jnp.concatenate([r[:piece_len] for r in piece_refs], axis=0)
+    v_pre = jnp.concatenate([r[piece_len:2 * piece_len] for r in piece_refs], axis=0)
     k_own = kown_ref[...]
     v_own = vown_ref[...]
-    s_pre = lax.dot_general(k_pre, q_rows, contract_minor, preferred_element_type=jnp.float32) * scaling
-    s_own = lax.dot_general(k_own, q_rows, contract_minor, preferred_element_type=jnp.float32) * scaling
+    s_pre = lax.dot_general(k_pre, q_rows, contract_minor, preferred_element_type=jnp.float32)
+    s_own = lax.dot_general(k_own, q_rows, contract_minor, preferred_element_type=jnp.float32)
     own_pos = lax.broadcasted_iota(jnp.int32, (resp_len, rows), 0)
     token_of_col = lax.broadcasted_iota(jnp.int32, (resp_len, rows), 1) % resp_len
     s_own = jnp.where(token_of_col >= own_pos, s_own, masked_score)
     peak = jnp.maximum(jnp.max(s_pre, axis=0, keepdims=True), jnp.max(s_own, axis=0, keepdims=True))
-    e_pre = jnp.exp(s_pre - peak)
-    e_own = jnp.exp(s_own - peak)
+    exp_scale = scaling * math.log2(math.e)
+    e_pre = jnp.exp2((s_pre - peak) * exp_scale)
+    e_own = jnp.exp2((s_own - peak) * exp_scale)
     total = jnp.sum(e_pre, axis=0, keepdims=True) + jnp.sum(e_own, axis=0, keepdims=True)
     inv_total = 1.0 / total
     p_pre = e_pre * inv_total
@@ -117,9 +118,9 @@
     weight = jnp.where(live_slots, 2.0 * jax.nn.sigmoid(loss_beta * margin) / count_real, 0.0)
     loss_terms = jnp.where(live_slots, 2.0 / loss_beta * jax.nn.softplus(loss_beta * margin), 0.0)
     own_term = jnp.sum(loss_terms)
-    word_rows = jnp.zeros((2, 16, prefix_keys.shape[2]), jnp.bfloat16)
-    word_rows = word_rows.at[0, 0, 0:3].set(split_words(own_term))
-    local_kv = jnp.concatenate([jnp.stack([prefix_keys[0], prefix_values[0]]), word_rows], axis=1)
+    word_rows = jnp.zeros((16, prefix_keys.shape[2]), jnp.bfloat16)
+    word_rows = word_rows.at[0, 0:3].set(split_words(own_term))
+    local_kv = jnp.concatenate([prefix_keys[0], prefix_values[0], word_rows], axis=0)
     if n == 4:
         from_left = shifted(local_kv, 1, n)
         pieces = [local_kv, from_left, shifted(local_kv, -1, n), shifted(from_left, 1, n)]
@@ -127,7 +128,7 @@
         pieces = [local_kv] + [shifted(local_kv, k, n) for k in range(1, n)]
     scalars = jnp.stack([weight[0], lengths[0][0].astype(jnp.float32), own_term, count_real])
     group_width = (HEADS // KV_HEADS) * HEAD_DIM
-    piece_block = pl.BlockSpec((2, piece_len + 16, HEAD_DIM), lambda g: (0, 0, g))
+    piece_block = pl.BlockSpec((2 * piece_len + 16, HEAD_DIM), lambda g: (0, g))
     part_block = pl.BlockSpec((2, piece_len, HEAD_DIM), lambda g: (0, 0, g))
     results = pl.pallas_call(
         functools.partial(attention_kernel, n),

time: 56 us -> 54.7 us (0.977)
  waiting for transfers between devices: 30.1 us -> 29.1 us
    ppermute x6, waiting for transfers between devices: 30.1 us -> 29.1 us  [shifted(): return lax.ppermute(value, 'resp', [(i, (i + shift) % n) for i in range(n)])]
where the time goes in v7:
time: 54.7 us; the launch traced here: 54.5 us
  waiting for transfers between devices  29.1 us (53%)
  starting transfers between devices  9.79 us (18%)
  Pallas kernels  7.78 us (14%)
  between operations  3.53 us (6%)
  other arithmetic  3.51 us (6%)
  local copies, waits for them, and re-layouts  0.72 us (1%)
    ppermute x6, waiting for transfers between devices, shifted(): return lax.ppermute(value, 'resp', [(i, (i + shift) % n) for i in range(n)])  29.1 us
    ppermute x6, starting transfers between devices, shifted(): return lax.ppermute(value, 'resp', [(i, (i + shift) % n) for i in range(n)])  9.79 us
    pallas_call x1, Pallas kernels, on_device(): pl.pallas_call(functools.partial(attention_kernel, n), grid=(KV_HEADS,),...  7.78 us
  transfers between devices with their start and end apart: 6, of which 6 were waited for; matrix products, arithmetic and copies ran while one was open for 3% of the time, Pallas kernels for 0%

profile of v7, /device:TPU:0, one launch (start us, length us, event | category | flops | bytes accessed | tf_op | source)
XLA Modules:
  0.0 54.5 jit_solution(1712240317618086965)
XLA Ops:
  2.7 0.1 maximum_bitcast_fusion
  2.8 1.0 %fusion.1.rest_0_ = bf16[272,512]{1,0:T(8,128)(2,1)S(1)} fusion(bf16[1,3]{1,0:T(2,128)(2,1)S(1)} %maximum_bitcast_fusion, bf16[128,512]{1,0:T(8,128)(2,1)} %bitcast.20, bf16[128,512]{1,0:T(8,128)(2,1)} %bitcast.21), kind=kLoop, calls=%fused_computation.3 | loop fusion | flops 1114112 | bytes 540678 | tf_op jit(solution)/shard_map/concatenate | solution.py:123
  3.8 0.0 copy-start
  3.8 3.1 %collective-permute-start = (bf16[272,512]{1,0:T(8,128)(2,1)S(1)}, bf16[272,512]{1,0:T(8,128)(2,1)S(1)}, u32[]{:S(2)}, u32[]{:S(2)}) collective-permute-start(bf16[272,512]{1,0:T(8,128)(2,1)S(1)} %fusion.1.rest_0_), channel_id=1, source_target_pairs={{0,1},{1,2},{2,3},{3,0},{4,5},{5,6},{6,7},{7,4},{8,9},{9,10},{10,1... | collective-permute-start | bytes 835592 | tf_op jit(solution)/shard_map/ppermute | solution.py:93
  6.8 2.1 %collective-permute-start.1 = (bf16[272,512]{1,0:T(8,128)(2,1)S(1)}, bf16[272,512]{1,0:T(8,128)(2,1)S(1)}, u32[]{:S(2)}, u32[]{:S(2)}) collective-permute-start(bf16[272,512]{1,0:T(8,128)(2,1)S(1)} %fusion.1.rest_0_), channel_id=1, source_target_pairs={{0,3},{1,0},{2,1},{3,2},{4,7},{5,4},{6,5},{7,6},{8,11},{9,8},{10,9... | collective-permute-start | bytes 835592 | tf_op jit(solution)/shard_map/ppermute | solution.py:93
  8.9 7.5 %collective-permute-done.rest_1_ = bf16[272,512]{1,0:T(8,128)(2,1)S(1)} collective-permute-done((bf16[272,512]{1,0:T(8,128)(2,1)S(1)}, bf16[272,512]{1,0:T(8,128)(2,1)S(1)}, u32[]{:S(2)}, u32[]{:S(2)}) %collective-permute-start) | collective-permute-done | bytes 278560 | tf_op jit(solution)/shard_map/ppermute | solution.py:93
  16.4 0.0 copy-start.1
  16.4 0.0 collective-permute-start.2
  17.2 0.6 %pad_maximum_fusion.scalar_ref = f32[4]{0:T(128)} fusion(f32[1]{0:T(128)S(6)} %convert_element_type.64, f32[1]{0:T(128)} %select_n.13, f32[1]{0:T(128)} %bitcast.2, f32[1]{0:T(128)S(6)} %select_n.11), kind=kLoop, calls=%fused_computation.6 | loop fusion | flops 12 | bytes 32 | tf_op jit(solution)/shard_map/stack | solution.py:129
  17.8 3.3 %collective-permute-done.1.rest_2_ = bf16[272,512]{1,0:T(8,128)(2,1)S(1)} collective-permute-done((bf16[272,512]{1,0:T(8,128)(2,1)S(1)}, bf16[272,512]{1,0:T(8,128)(2,1)S(1)}, u32[]{:S(2)}, u32[]{:S(2)}) %collective-permute-start.1) | collective-permute-done | bytes 278560 | tf_op jit(solution)/shard_map/ppermute | solution.py:93
  21.2 0.0 copy-start.2
  21.2 6.4 %collective-permute-done.2.rest_3_ = bf16[272,512]{1,0:T(8,128)(2,1)S(1)} collective-permute-done((bf16[272,512]{1,0:T(8,128)(2,1)S(1)}, bf16[272,512]{1,0:T(8,128)(2,1)S(1)}, u32[]{:S(2)}, u32[]{:S(2)}) %collective-permute-start.2) | collective-permute-done | bytes 278560 | tf_op jit(solution)/shard_map/ppermute | solution.py:93
  27.5 0.0 copy-start.3
  27.5 0.0 copy-done
  27.5 0.0 copy-done.1
  27.5 0.0 copy-done.2
  27.5 0.7 %copy-done.3 = bf16[272,512]{1,0:T(8,128)(2,1)} copy-done((bf16[272,512]{1,0:T(8,128)(2,1)}, bf16[272,512]{1,0:T(8,128)(2,1)S(1)}, u32[]{:S(2)}) %copy-start.3) | copy-done | bytes 278552
  28.2 7.8 %shard_map.145 = (bf16[32,8192]{1,0:T(8,128)(2,1)}, bf16[32,512]{1,0:T(8,128)(2,1)}, bf16[32,512]{1,0:T(8,128)(2,1)}, bf16[2,128,512]{2,1,0:T(8,128)(2,1)}, bf16...) custom-call(f32[4]{0:T(128)} %pad_maximum_fusion.scalar_ref, ...), custom_call_target="tpu_custom_call" | custom-call | tf_op jit(solution)/shard_map/pallas_call | solution.py:133
  36.0 1.8 %collective-permute-start.4 = (bf16[2,128,512]{2,1,0:T(8,128)(2,1)}, bf16[2,128,512]{2,1,0:T(8,128)(2,1)S(1)}, u32[]{:S(2)}, u32[]{:S(2)}) collective-permute-start(bf16[2,128,512]{2,1,0:T(8,128)(2,1)} %get-tuple-element.32), channel_id=1, source_target_pairs={{0,3},{1,0},{2,1},{3,2},{4,7},{5,4},{6,5},{7,6},{8,11},{9,8},{10,9... | collective-permute-start | bytes 786440 | tf_op jit(solution)/shard_map/ppermute | solution.py:93
  37.8 0.3 collective-permute-start.3
  38.1 8.0 %collective-permute-done.4 = bf16[2,128,512]{2,1,0:T(8,128)(2,1)S(1)} collective-permute-done((bf16[2,128,512]{2,1,0:T(8,128)(2,1)}, bf16[2,128,512]{2,1,0:T(8,128)(2,1)S(1)}, u32[]{:S(2)}, u32[]{:S(2)}) %collective-permute-start.4) | collective-permute-done | bytes 262176 | tf_op jit(solution)/shard_map/ppermute | solution.py:93
  46.1 0.0 copy-start.4
  46.1 1.1 %add_convert_fusion = bf16[2,128,512]{2,1,0:T(8,128)(2,1)S(1)} fusion(bf16[2,128,512]{2,1,0:T(8,128)(2,1)S(1)} %collective-permute-done.4, bf16[2,128,512]{2,1,0:T(8,128)(2,1)} %get-tuple-element.31), kind=kLoop, calls=%fused_computation.2 | loop fusion | flops 524288 | bytes 786432 | tf_op jit(solution)/shard_map/convert_element_type | solution.py:164
  47.1 2.5 %collective-permute-start.5 = (bf16[2,128,512]{2,1,0:T(8,128)(2,1)S(1)}, bf16[2,128,512]{2,1,0:T(8,128)(2,1)S(1)}, u32[]{:S(2)}, u32[]{:S(2)}) collective-permute-start(bf16[2,128,512]{2,1,0:T(8,128)(2,1)S(1)} %add_convert_fusion), channel_id=1, source_target_pairs={{0,3},{1,0},{2,1},{3,2},{4,7},{5,4},{6,5},{7,6},{8,11},{9,8},{10,9... | collective-permute-start | bytes 786440 | tf_op jit(solution)/shard_map/ppermute | solution.py:93
  49.7 1.2 %collective-permute-done.3 = bf16[2,128,512]{2,1,0:T(8,128)(2,1)S(1)} collective-permute-done((bf16[2,128,512]{2,1,0:T(8,128)(2,1)}, bf16[2,128,512]{2,1,0:T(8,128)(2,1)S(1)}, u32[]{:S(2)}, u32[]{:S(2)}) %collective-permute-start.3) | collective-permute-done | bytes 262176 | tf_op jit(solution)/shard_map/ppermute | solution.py:93
  50.9 2.8 %collective-permute-done.5 = bf16[2,128,512]{2,1,0:T(8,128)(2,1)S(1)} collective-permute-done((bf16[2,128,512]{2,1,0:T(8,128)(2,1)S(1)}, bf16[2,128,512]{2,1,0:T(8,128)(2,1)S(1)}, u32[]{:S(2)}, u32[]{:S(2)}) %collective-permute-start.5) | collective-permute-done | bytes 262176 | tf_op jit(solution)/shard_map/ppermute | solution.py:93
  53.7 0.0 copy-done.4
  53.7 0.8 %add_convert_fusion.1 = (bf16[1,128,512]{2,1,0:T(8,128)(2,1)}, bf16[1,128,512]{2,1,0:T(8,128)(2,1)}) fusion(bf16[2,128,512]{2,1,0:T(8,128)(2,1)S(1)} %collective-permute-done.5, bf16[2,128,512]{2,1,0:T(8,128)(2,1)S(1)} %collective-permute-done.3, bf16[2,128,512]{2,1,0:T(8,128)(2,1)S(1)} %copy-done.4), kind=kLoop, calls=%fused_computation.4 | loop fusion | flops 786432 | bytes 1048576 | tf_op jit(solution)/shard_map/convert_element_type | solution.py:169
Async XLA Ops:
  3.8 23.8 %copy-start = (bf16[272,512]{1,0:T(8,128)(2,1)}, bf16[272,512]{1,0:T(8,128)(2,1)S(1)}, u32[]{:S(2)}) copy-start(bf16[272,512]{1,0:T(8,128)(2,1)S(1)} %fusion.1.rest_0_) | copy-start | bytes 835588
  3.8 12.6 %collective-permute-start = (bf16[272,512]{1,0:T(8,128)(2,1)S(1)}, bf16[272,512]{1,0:T(8,128)(2,1)S(1)}, u32[]{:S(2)}, u32[]{:S(2)}) collective-permute-start(bf16[272,512]{1,0:T(8,128)(2,1)S(1)} %fusion.1.rest_0_), channel_id=1, source_target_pairs={{0,1},{1,2},{2,3},{3,0},{4,5},{5,6},{6,7},{7,4},{8,9},{9,10},{10,1... | collective-permute-start | bytes 835592 | tf_op jit(solution)/shard_map/ppermute | solution.py:93
  6.8 14.3 %collective-permute-start.1 = (bf16[272,512]{1,0:T(8,128)(2,1)S(1)}, bf16[272,512]{1,0:T(8,128)(2,1)S(1)}, u32[]{:S(2)}, u32[]{:S(2)}) collective-permute-start(bf16[272,512]{1,0:T(8,128)(2,1)S(1)} %fusion.1.rest_0_), channel_id=1, source_target_pairs={{0,3},{1,0},{2,1},{3,2},{4,7},{5,4},{6,5},{7,6},{8,11},{9,8},{10,9... | collective-permute-start | bytes 835592 | tf_op jit(solution)/shard_map/ppermute | solution.py:93
  16.4 11.1 %copy-start.1 = (bf16[272,512]{1,0:T(8,128)(2,1)}, bf16[272,512]{1,0:T(8,128)(2,1)S(1)}, u32[]{:S(2)}) copy-start(bf16[272,512]{1,0:T(8,128)(2,1)S(1)} %collective-permute-done.rest_1_) | copy-start | bytes 835588
  16.4 11.1 %collective-permute-start.2 = (bf16[272,512]{1,0:T(8,128)(2,1)S(1)}, bf16[272,512]{1,0:T(8,128)(2,1)S(1)}, u32[]{:S(2)}, u32[]{:S(2)}) collective-permute-start(bf16[272,512]{1,0:T(8,128)(2,1)S(1)} %collective-permute-done.rest_1_), channel_id=1, source_target_pairs={{0,1},{1,2},{2,3},{3,0},{4,5},{5,6},{6,7},{7,4},{8,9},{9,10},{10,1... | collective-permute-start | bytes 835592 | tf_op jit(solution)/shard_map/ppermute | solution.py:93
  21.2 6.4 %copy-start.2 = (bf16[272,512]{1,0:T(8,128)(2,1)}, bf16[272,512]{1,0:T(8,128)(2,1)S(1)}, u32[]{:S(2)}) copy-start(bf16[272,512]{1,0:T(8,128)(2,1)S(1)} %collective-permute-done.1.rest_2_) | copy-start | bytes 835588
  27.5 0.7 %copy-start.3 = (bf16[272,512]{1,0:T(8,128)(2,1)}, bf16[272,512]{1,0:T(8,128)(2,1)S(1)}, u32[]{:S(2)}) copy-start(bf16[272,512]{1,0:T(8,128)(2,1)S(1)} %collective-permute-done.2.rest_3_) | copy-start | bytes 835588
  36.0 10.0 %collective-permute-start.4 = (bf16[2,128,512]{2,1,0:T(8,128)(2,1)}, bf16[2,128,512]{2,1,0:T(8,128)(2,1)S(1)}, u32[]{:S(2)}, u32[]{:S(2)}) collective-permute-start(bf16[2,128,512]{2,1,0:T(8,128)(2,1)} %get-tuple-element.32), channel_id=1, source_target_pairs={{0,3},{1,0},{2,1},{3,2},{4,7},{5,4},{6,5},{7,6},{8,11},{9,8},{10,9... | collective-permute-start | bytes 786440 | tf_op jit(solution)/shard_map/ppermute | solution.py:93
  37.8 13.1 %collective-permute-start.3 = (bf16[2,128,512]{2,1,0:T(8,128)(2,1)}, bf16[2,128,512]{2,1,0:T(8,128)(2,1)S(1)}, u32[]{:S(2)}, u32[]{:S(2)}) collective-permute-start(bf16[2,128,512]{2,1,0:T(8,128)(2,1)} %get-tuple-element.30), channel_id=1, source_target_pairs={{0,1},{1,2},{2,3},{3,0},{4,5},{5,6},{6,7},{7,4},{8,9},{9,10},{10,1... | collective-permute-start | bytes 786440 | tf_op jit(solution)/shard_map/ppermute | solution.py:93
  46.1 7.6 %copy-start.4 = (bf16[2,128,512]{2,1,0:T(8,128)(2,1)S(1)}, bf16[2,128,512]{2,1,0:T(8,128)(2,1)}, u32[]{:S(2)}) copy-start(bf16[2,128,512]{2,1,0:T(8,128)(2,1)} %get-tuple-element.29) | copy-start | bytes 786436
  47.1 6.6 %collective-permute-start.5 = (bf16[2,128,512]{2,1,0:T(8,128)(2,1)S(1)}, bf16[2,128,512]{2,1,0:T(8,128)(2,1)S(1)}, u32[]{:S(2)}, u32[]{:S(2)}) collective-permute-start(bf16[2,128,512]{2,1,0:T(8,128)(2,1)S(1)} %add_convert_fusion), channel_id=1, source_target_pairs={{0,3},{1,0},{2,1},{3,2},{4,7},{5,4},{6,5},{7,6},{8,11},{9,8},{10,9... | collective-permute-start | bytes 786440 | tf_op jit(solution)/shard_map/ppermute | solution.py:93

commit v8 on v7

--- a/solution.py
+++ b/solution.py
@@ -20,13 +20,19 @@
 def attention_kernel(n_pieces, scalar_ref, q_ref, cot_ref, kown_ref, vown_ref, *rest):
     piece_refs = rest[:n_pieces]
     dq_ref, dkown_ref, dvown_ref = rest[n_pieces:n_pieces + 3]
-    part_refs = rest[n_pieces + 3:-1]
-    loss_ref = rest[-1]
+    part_refs = rest[n_pieces + 3:2 * n_pieces + 3]
+    loss_ref = rest[2 * n_pieces + 3]
+    s_ref, dp_ref, e_ref, ds_ref, pb_ref = rest[2 * n_pieces + 4:]
     group_size = HEADS // KV_HEADS
     resp_len = q_ref.shape[0]
     piece_len = part_refs[0].shape[1]
+    prefix_rows = n_pieces * piece_len
+    all_rows = prefix_rows + resp_len
     scaling = 1.0 / math.sqrt(HEAD_DIM)
+    exp_scale = scaling * math.log2(math.e)
     rows = group_size * resp_len
+    chunk = 32
+    chunks = prefix_rows // chunk
     token = lax.broadcasted_iota(jnp.int32, (resp_len, 1), 0).astype(jnp.float32)
     factor = jnp.where(token < scalar_ref[1], scalar_ref[0], 0.0)
 
@@ -36,47 +42,68 @@
         for r in piece_refs[1:]:
             term_total = term_total + jnp.sum(r[2 * piece_len:2 * piece_len + 8, :].astype(jnp.float32))
         loss_ref[0] = term_total / scalar_ref[3]
+
     contract_minor = (((1,), (1,)), ((), ()))
     contract_major = (((0,), (0,)), ((), ()))
     q_all = q_ref[...]
     g_all = (cot_ref[...].astype(jnp.float32) * factor).astype(jnp.bfloat16)
     q_rows = jnp.concatenate([q_all[:, h * HEAD_DIM:(h + 1) * HEAD_DIM] for h in range(group_size)], axis=0)
     g_rows = jnp.concatenate([g_all[:, h * HEAD_DIM:(h + 1) * HEAD_DIM] for h in range(group_size)], axis=0)
-    k_pre = jnp.concatenate([r[:piece_len] for r in piece_refs], axis=0)
-    v_pre = jnp.concatenate([r[piece_len:2 * piece_len] for r in piece_refs], axis=0)
-    k_own = kown_ref[...]
-    v_own = vown_ref[...]
-    s_pre = lax.dot_general(k_pre, q_rows, contract_minor, preferred_element_type=jnp.float32)
-    s_own = lax.dot_general(k_own, q_rows, contract_minor, preferred_element_type=jnp.float32)
+    k_all = jnp.concatenate([r[:piece_len] for r in piece_refs] + [kown_ref[...]], axis=0)
+    v_all = jnp.concatenate([r[piece_len:2 * piece_len] for r in piece_refs] + [vown_ref[...]], axis=0)
+    s_ref[...] = lax.dot_general(k_all, q_rows, contract_minor, preferred_element_type=jnp.float32)
+    dp_ref[...] = lax.dot_general(v_all, g_rows, contract_minor, preferred_element_type=jnp.float32)
     own_pos = lax.broadcasted_iota(jnp.int32, (resp_len, rows), 0)
     token_of_col = lax.broadcasted_iota(jnp.int32, (resp_len, rows), 1) % resp_len
-    s_own = jnp.where(token_of_col >= own_pos, s_own, masked_score)
-    peak = jnp.maximum(jnp.max(s_pre, axis=0, keepdims=True), jnp.max(s_own, axis=0, keepdims=True))
-    exp_scale = scaling * math.log2(math.e)
-    e_pre = jnp.exp2((s_pre - peak) * exp_scale)
+    s_own = jnp.where(token_of_col >= own_pos, s_ref[prefix_rows:all_rows], masked_score)
+
+    def block(c):
+        return pl.ds(pl.multiple_of(c * chunk, chunk), chunk)
+
+    def max_step(c, running):
+        return jnp.maximum(running, s_ref[block(c)])
+
+    running = lax.fori_loop(0, chunks, max_step, jnp.full((chunk, rows), masked_score, jnp.float32), unroll=True)
+    peak = jnp.maximum(jnp.max(running, axis=0, keepdims=True), jnp.max(s_own, axis=0, keepdims=True))
+
+    def exp_step(c, running):
+        e = jnp.exp2((s_ref[block(c)] - peak) * exp_scale)
+        e_ref[block(c)] = e
+        return running + e
+
+    running = lax.fori_loop(0, chunks, exp_step, jnp.zeros((chunk, rows), jnp.float32), unroll=True)
     e_own = jnp.exp2((s_own - peak) * exp_scale)
-    total = jnp.sum(e_pre, axis=0, keepdims=True) + jnp.sum(e_own, axis=0, keepdims=True)
+    e_ref[prefix_rows:all_rows] = e_own
+    total = jnp.sum(running, axis=0, keepdims=True) + jnp.sum(e_own, axis=0, keepdims=True)
     inv_total = 1.0 / total
-    p_pre = e_pre * inv_total
+
+    def centre_step(c, running):
+        return running + (e_ref[block(c)] * inv_total) * dp_ref[block(c)]
+
+    running = lax.fori_loop(0, chunks, centre_step, jnp.zeros((chunk, rows), jnp.float32), unroll=True)
     p_own = e_own * inv_total
-    dp_pre = lax.dot_general(v_pre, g_rows, contract_minor, preferred_element_type=jnp.float32)
-    dp_own = lax.dot_general(v_own, g_rows, contract_minor, preferred_element_type=jnp.float32)
-    centre = jnp.sum(p_pre * dp_pre, axis=0, keepdims=True) + jnp.sum(p_own * dp_own, axis=0, keepdims=True)
-    ds_pre = (p_pre * (dp_pre - centre)).astype(jnp.bfloat16)
-    ds_own = (p_own * (dp_own - centre)).astype(jnp.bfloat16)
-    dk_pre = jnp.dot(ds_pre, q_rows, preferred_element_type=jnp.float32) * scaling
-    dv_pre = jnp.dot(p_pre.astype(jnp.bfloat16), g_rows, preferred_element_type=jnp.float32)
+    centre = jnp.sum(running, axis=0, keepdims=True) + jnp.sum(
+        p_own * dp_ref[prefix_rows:all_rows], axis=0, keepdims=True
+    )
+
+    def shift_step(c, carry):
+        p = e_ref[block(c)] * inv_total
+        ds_ref[block(c)] = (p * (dp_ref[block(c)] - centre)).astype(jnp.bfloat16)
+        pb_ref[block(c)] = p.astype(jnp.bfloat16)
+        return carry
+
+    lax.fori_loop(0, chunks, shift_step, 0, unroll=True)
+    ds_ref[prefix_rows:all_rows] = (p_own * (dp_ref[prefix_rows:all_rows] - centre)).astype(jnp.bfloat16)
+    pb_ref[prefix_rows:all_rows] = p_own.astype(jnp.bfloat16)
+    ds_all = ds_ref[...]
+    dk_all = jnp.dot(ds_all, q_rows, preferred_element_type=jnp.float32) * scaling
+    dv_all = jnp.dot(pb_ref[...], g_rows, preferred_element_type=jnp.float32)
     for i, r in enumerate(part_refs):
-        r[0] = dk_pre[i * piece_len:(i + 1) * piece_len].astype(jnp.bfloat16)
-        r[1] = dv_pre[i * piece_len:(i + 1) * piece_len].astype(jnp.bfloat16)
-    dkown_ref[...] = (jnp.dot(ds_own, q_rows, preferred_element_type=jnp.float32) * scaling).astype(jnp.bfloat16)
-    dvown_ref[...] = jnp.dot(p_own.astype(jnp.bfloat16), g_rows, preferred_element_type=jnp.float32).astype(
-        jnp.bfloat16
-    )
-    dq_rows = (
-        lax.dot_general(ds_pre, k_pre, contract_major, preferred_element_type=jnp.float32) * scaling
-        + lax.dot_general(ds_own, k_own, contract_major, preferred_element_type=jnp.float32) * scaling
-    )
+        r[0] = dk_all[i * piece_len:(i + 1) * piece_len].astype(jnp.bfloat16)
+        r[1] = dv_all[i * piece_len:(i + 1) * piece_len].astype(jnp.bfloat16)
+    dkown_ref[...] = dk_all[prefix_rows:all_rows].astype(jnp.bfloat16)
+    dvown_ref[...] = dv_all[prefix_rows:all_rows].astype(jnp.bfloat16)
+    dq_rows = lax.dot_general(ds_all, k_all, contract_major, preferred_element_type=jnp.float32) * scaling
     for h in range(group_size):
         dq_ref[:, h * HEAD_DIM:(h + 1) * HEAD_DIM] = dq_rows[h * resp_len:(h + 1) * resp_len].astype(jnp.bfloat16)
 
@@ -128,6 +155,8 @@
         pieces = [local_kv] + [shifted(local_kv, k, n) for k in range(1, n)]
     scalars = jnp.stack([weight[0], lengths[0][0].astype(jnp.float32), own_term, count_real])
     group_width = (HEADS // KV_HEADS) * HEAD_DIM
+    group_rows = (HEADS // KV_HEADS) * resp_len
+    all_rows = n * piece_len + resp_len
     piece_block = pl.BlockSpec((2 * piece_len + 16, HEAD_DIM), lambda g: (0, g))
     part_block = pl.BlockSpec((2, piece_len, HEAD_DIM), lambda g: (0, 0, g))
     results = pl.pallas_call(
@@ -155,6 +184,9 @@
         ]
         + [jax.ShapeDtypeStruct((2,) + prefix_keys.shape[1:], jnp.bfloat16) for _ in range(n)]
         + [jax.ShapeDtypeStruct((1,), jnp.float32)],
+        scratch_shapes=[pltpu.VMEM((all_rows, group_rows), jnp.float32) for _ in range(3)]
+        + [pltpu.VMEM((all_rows, group_rows), jnp.bfloat16) for _ in range(2)],
+        compiler_params=pltpu.CompilerParams(vmem_limit_bytes=48 * 1024 * 1024),
     )(scalars, queries[0, 0], cotangent[0, 0], resp_keys[0, 0], resp_values[0, 0], *pieces)
     grad_q, grad_k, grad_v = results[:3]
     parts = results[3:-1]

time: 54.7 us -> 54.1 us (0.989)
  waiting for transfers between devices: 29.1 us -> 30.8 us
  other arithmetic: 3.51 us -> 2.02 us
  Pallas kernels: 7.78 us -> 7.08 us
    ppermute x6, waiting for transfers between devices: 29.1 us -> 30.8 us  [shifted(): return lax.ppermute(value, 'resp', [(i, (i + shift) % n) for i in range(n)])]
    convert_element_type x1, other arithmetic: 1.06 us -> 0.07 us  [on_device(): (parts[1].astype(jnp.float32) + relayed.astype(jnp.float32)).astype(jnp.b...]
    pallas_call x1, Pallas kernels: 7.78 us -> 7.08 us  [on_device(): pl.pallas_call(functools.partial(attention_kernel, n), grid=(KV_HEADS,),...]
  transfers between devices with their start and end apart: 6 -> 6, of which waited for: 6 -> 6; matrix products, arithmetic and copies ran while one was open for 3% -> 0% of each run, Pallas kernels for 0% -> 0%
where the time goes in v8:
time: 54.1 us; the launch traced here: 53.9 us
  waiting for transfers between devices  30.8 us (57%)
  starting transfers between devices  9.39 us (17%)
  Pallas kernels  7.08 us (13%)
  between operations  3.57 us (7%)
  other arithmetic  2.02 us (4%)
  local copies, waits for them, and re-layouts  1.05 us (2%)
    ppermute x6, waiting for transfers between devices, shifted(): return lax.ppermute(value, 'resp', [(i, (i + shift) % n) for i in range(n)])  30.8 us
    ppermute x6, starting transfers between devices, shifted(): return lax.ppermute(value, 'resp', [(i, (i + shift) % n) for i in range(n)])  9.39 us
    pallas_call x1, Pallas kernels, on_device(): pl.pallas_call(functools.partial(attention_kernel, n), grid=(KV_HEADS,),...  7.08 us
  transfers between devices with their start and end apart: 6, of which 6 were waited for; matrix products, arithmetic and copies ran while one was open for 0% of the time, Pallas kernels for 0%

profile of v8, /device:TPU:0, one launch (start us, length us, event | category | flops | bytes accessed | tf_op | source)
XLA Modules:
  0.0 53.9 jit_solution(9911798336678789626)
XLA Ops:
  0.6 0.0 copy-start
  2.8 0.1 maximum_bitcast_fusion
  2.8 0.0 copy-start.2
  2.8 0.0 copy-start.3
  2.8 1.0 %fusion.1.rest_0_ = bf16[272,512]{1,0:T(8,128)(2,1)S(1)} fusion(bf16[1,3]{1,0:T(2,128)(2,1)S(1)} %maximum_bitcast_fusion, bf16[128,512]{1,0:T(8,128)(2,1)} %bitcast.22, bf16[128,512]{1,0:T(8,128)(2,1)} %bitcast.23), kind=kLoop, calls=%fused_computation.3 | loop fusion | flops 1114112 | bytes 540678 | tf_op jit(solution)/shard_map/concatenate | solution.py:150
  3.8 3.1 %collective-permute-start = (bf16[272,512]{1,0:T(8,128)(2,1)S(1)}, bf16[272,512]{1,0:T(8,128)(2,1)S(1)}, u32[]{:S(2)}, u32[]{:S(2)}) collective-permute-start(bf16[272,512]{1,0:T(8,128)(2,1)S(1)} %fusion.1.rest_0_), channel_id=1, source_target_pairs={{0,1},{1,2},{2,3},{3,0},{4,5},{5,6},{6,7},{7,4},{8,9},{9,10},{10,1... | collective-permute-start | bytes 835592 | tf_op jit(solution)/shard_map/ppermute | solution.py:120
  6.9 2.1 %collective-permute-start.1 = (bf16[272,512]{1,0:T(8,128)(2,1)S(1)}, bf16[272,512]{1,0:T(8,128)(2,1)S(1)}, u32[]{:S(2)}, u32[]{:S(2)}) collective-permute-start(bf16[272,512]{1,0:T(8,128)(2,1)S(1)} %fusion.1.rest_0_), channel_id=1, source_target_pairs={{0,3},{1,0},{2,1},{3,2},{4,7},{5,4},{6,5},{7,6},{8,11},{9,8},{10,9... | collective-permute-start | bytes 835592 | tf_op jit(solution)/shard_map/ppermute | solution.py:120
  9.0 7.5 %collective-permute-done.rest_1_ = bf16[272,512]{1,0:T(8,128)(2,1)S(1)} collective-permute-done((bf16[272,512]{1,0:T(8,128)(2,1)S(1)}, bf16[272,512]{1,0:T(8,128)(2,1)S(1)}, u32[]{:S(2)}, u32[]{:S(2)}) %collective-permute-start) | collective-permute-done | bytes 278560 | tf_op jit(solution)/shard_map/ppermute | solution.py:120
  16.5 0.0 collective-permute-start.2
  17.3 0.1 pad_maximum_fusion.scalar_ref
  17.3 3.9 %collective-permute-done.1.rest_2_ = bf16[272,512]{1,0:T(8,128)(2,1)S(1)} collective-permute-done((bf16[272,512]{1,0:T(8,128)(2,1)S(1)}, bf16[272,512]{1,0:T(8,128)(2,1)S(1)}, u32[]{:S(2)}, u32[]{:S(2)}) %collective-permute-start.1) | collective-permute-done | bytes 278560 | tf_op jit(solution)/shard_map/ppermute | solution.py:120
  21.2 6.4 %collective-permute-done.2.rest_3_ = bf16[272,512]{1,0:T(8,128)(2,1)S(1)} collective-permute-done((bf16[272,512]{1,0:T(8,128)(2,1)S(1)}, bf16[272,512]{1,0:T(8,128)(2,1)S(1)}, u32[]{:S(2)}, u32[]{:S(2)}) %collective-permute-start.2) | collective-permute-done | bytes 278560 | tf_op jit(solution)/shard_map/ppermute | solution.py:120
  27.6 0.0 copy-done
  27.6 0.0 copy-done.2
  27.6 0.0 copy-done.3
  27.6 0.0 copy-start.1
  27.6 1.0 %copy-done.1 = bf16[1,1,32,8192]{3,2,1,0:T(8,128)(2,1)S(1)} copy-done((bf16[1,1,32,8192]{3,2,1,0:T(8,128)(2,1)S(1)}, bf16[1,1,32,8192]{3,2,1,0:T(8,128)(2,1)}, u32[]{:S(2)}) %copy-start.1) | copy-done | bytes 524312
  28.6 7.1 %shard_map.145 = (bf16[32,8192]{1,0:T(8,128)(2,1)}, bf16[32,512]{1,0:T(8,128)(2,1)}, bf16[32,512]{1,0:T(8,128)(2,1)}, bf16[2,128,512]{2,1,0:T(8,128)(2,1)S(1)}, ...) custom-call(f32[4]{0:T(128)S(1)} %pad_maximum_fusion.scalar_ref, ...), custom_call_target="tpu_custom_call" | custom-call | tf_op jit(solution)/shard_map/pallas_call | solution.py:162
  35.7 1.7 %collective-permute-start.4 = (bf16[2,128,512]{2,1,0:T(8,128)(2,1)S(1)}, bf16[2,128,512]{2,1,0:T(8,128)(2,1)S(1)}, u32[]{:S(2)}, u32[]{:S(2)}) collective-permute-start(bf16[2,128,512]{2,1,0:T(8,128)(2,1)S(1)} %get-tuple-element.32), channel_id=1, source_target_pairs={{0,3},{1,0},{2,1},{3,2},{4,7},{5,4},{6,5},{7,6},{8,11},{9,8},{10,9... | collective-permute-start | bytes 786440 | tf_op jit(solution)/shard_map/ppermute | solution.py:120
  37.4 0.3 collective-permute-start.3
  37.7 8.7 %collective-permute-done.4 = bf16[2,128,512]{2,1,0:T(8,128)(2,1)S(1)} collective-permute-done((bf16[2,128,512]{2,1,0:T(8,128)(2,1)S(1)}, bf16[2,128,512]{2,1,0:T(8,128)(2,1)S(1)}, u32[]{:S(2)}, u32[]{:S(2)}) %collective-permute-start.4) | collective-permute-done | bytes 262176 | tf_op jit(solution)/shard_map/ppermute | solution.py:120
  46.5 0.1 add_convert_fusion
  46.5 2.2 %collective-permute-start.5 = (bf16[2,128,512]{2,1,0:T(8,128)(2,1)S(1)}, bf16[2,128,512]{2,1,0:T(8,128)(2,1)S(1)}, u32[]{:S(2)}, u32[]{:S(2)}) collective-permute-start(bf16[2,128,512]{2,1,0:T(8,128)(2,1)S(1)} %add_convert_fusion), channel_id=1, source_target_pairs={{0,3},{1,0},{2,1},{3,2},{4,7},{5,4},{6,5},{7,6},{8,11},{9,8},{10,9... | collective-permute-start | bytes 786440 | tf_op jit(solution)/shard_map/ppermute | solution.py:120
  48.7 1.6 %collective-permute-done.3 = bf16[2,128,512]{2,1,0:T(8,128)(2,1)S(1)} collective-permute-done((bf16[2,128,512]{2,1,0:T(8,128)(2,1)S(1)}, bf16[2,128,512]{2,1,0:T(8,128)(2,1)S(1)}, u32[]{:S(2)}, u32[]{:S(2)}) %collective-permute-start.3) | collective-permute-done | bytes 262176 | tf_op jit(solution)/shard_map/ppermute | solution.py:120
  50.3 2.8 %collective-permute-done.5 = bf16[2,128,512]{2,1,0:T(8,128)(2,1)S(1)} collective-permute-done((bf16[2,128,512]{2,1,0:T(8,128)(2,1)S(1)}, bf16[2,128,512]{2,1,0:T(8,128)(2,1)S(1)}, u32[]{:S(2)}, u32[]{:S(2)}) %collective-permute-start.5) | collective-permute-done | bytes 262176 | tf_op jit(solution)/shard_map/ppermute | solution.py:120
  53.1 0.8 %add_convert_fusion.1 = (bf16[1,128,512]{2,1,0:T(8,128)(2,1)}, bf16[1,128,512]{2,1,0:T(8,128)(2,1)}) fusion(bf16[2,128,512]{2,1,0:T(8,128)(2,1)S(1)} %collective-permute-done.5, bf16[2,128,512]{2,1,0:T(8,128)(2,1)S(1)} %collective-permute-done.3, bf16[2,128,512]{2,1,0:T(8,128)(2,1)S(1)} %get-tuple-element.29), kind=kLoop, calls=%fused_computation.4 | loop fusion | flops 786432 | bytes 1048576 | tf_op jit(solution)/shard_map/convert_element_type | solution.py:201
Async XLA Ops:
  0.6 26.9 %copy-start = (bf16[1,1,32,8192]{3,2,1,0:T(8,128)(2,1)S(1)}, bf16[1,1,32,8192]{3,2,1,0:T(8,128)(2,1)}, u32[]{:S(2)}) copy-start(bf16[1,1,32,8192]{3,2,1,0:T(8,128)(2,1)} %param.12) | copy-start | bytes 1572868
  2.8 24.7 %copy-start.2 = (bf16[1,1,32,512]{3,2,1,0:T(8,128)(2,1)S(1)}, bf16[1,1,32,512]{3,2,1,0:T(8,128)(2,1)}, u32[]{:S(2)}) copy-start(bf16[1,1,32,512]{3,2,1,0:T(8,128)(2,1)} %param.14) | copy-start | bytes 98308
  2.8 24.7 %copy-start.3 = (bf16[1,1,32,512]{3,2,1,0:T(8,128)(2,1)S(1)}, bf16[1,1,32,512]{3,2,1,0:T(8,128)(2,1)}, u32[]{:S(2)}) copy-start(bf16[1,1,32,512]{3,2,1,0:T(8,128)(2,1)} %param.15) | copy-start | bytes 98308
  3.8 12.6 %collective-permute-start = (bf16[272,512]{1,0:T(8,128)(2,1)S(1)}, bf16[272,512]{1,0:T(8,128)(2,1)S(1)}, u32[]{:S(2)}, u32[]{:S(2)}) collective-permute-start(bf16[272,512]{1,0:T(8,128)(2,1)S(1)} %fusion.1.rest_0_), channel_id=1, source_target_pairs={{0,1},{1,2},{2,3},{3,0},{4,5},{5,6},{6,7},{7,4},{8,9},{9,10},{10,1... | collective-permute-start | bytes 835592 | tf_op jit(solution)/shard_map/ppermute | solution.py:120
  6.9 14.3 %collective-permute-start.1 = (bf16[272,512]{1,0:T(8,128)(2,1)S(1)}, bf16[272,512]{1,0:T(8,128)(2,1)S(1)}, u32[]{:S(2)}, u32[]{:S(2)}) collective-permute-start(bf16[272,512]{1,0:T(8,128)(2,1)S(1)} %fusion.1.rest_0_), channel_id=1, source_target_pairs={{0,3},{1,0},{2,1},{3,2},{4,7},{5,4},{6,5},{7,6},{8,11},{9,8},{10,9... | collective-permute-start | bytes 835592 | tf_op jit(solution)/shard_map/ppermute | solution.py:120
  16.5 11.1 %collective-permute-start.2 = (bf16[272,512]{1,0:T(8,128)(2,1)S(1)}, bf16[272,512]{1,0:T(8,128)(2,1)S(1)}, u32[]{:S(2)}, u32[]{:S(2)}) collective-permute-start(bf16[272,512]{1,0:T(8,128)(2,1)S(1)} %collective-permute-done.rest_1_), channel_id=1, source_target_pairs={{0,1},{1,2},{2,3},{3,0},{4,5},{5,6},{6,7},{7,4},{8,9},{9,10},{10,1... | collective-permute-start | bytes 835592 | tf_op jit(solution)/shard_map/ppermute | solution.py:120
  27.6 1.0 %copy-start.1 = (bf16[1,1,32,8192]{3,2,1,0:T(8,128)(2,1)S(1)}, bf16[1,1,32,8192]{3,2,1,0:T(8,128)(2,1)}, u32[]{:S(2)}) copy-start(bf16[1,1,32,8192]{3,2,1,0:T(8,128)(2,1)} %param.13) | copy-start | bytes 1572868
  35.7 10.8 %collective-permute-start.4 = (bf16[2,128,512]{2,1,0:T(8,128)(2,1)S(1)}, bf16[2,128,512]{2,1,0:T(8,128)(2,1)S(1)}, u32[]{:S(2)}, u32[]{:S(2)}) collective-permute-start(bf16[2,128,512]{2,1,0:T(8,128)(2,1)S(1)} %get-tuple-element.32), channel_id=1, source_target_pairs={{0,3},{1,0},{2,1},{3,2},{4,7},{5,4},{6,5},{7,6},{8,11},{9,8},{10,9... | collective-permute-start | bytes 786440 | tf_op jit(solution)/shard_map/ppermute | solution.py:120
  37.4 12.9 %collective-permute-start.3 = (bf16[2,128,512]{2,1,0:T(8,128)(2,1)S(1)}, bf16[2,128,512]{2,1,0:T(8,128)(2,1)S(1)}, u32[]{:S(2)}, u32[]{:S(2)}) collective-permute-start(bf16[2,128,512]{2,1,0:T(8,128)(2,1)S(1)} %get-tuple-element.30), channel_id=1, source_target_pairs={{0,1},{1,2},{2,3},{3,0},{4,5},{5,6},{6,7},{7,4},{8,9},{9,10},{10,1... | collective-permute-start | bytes 786440 | tf_op jit(solution)/shard_map/ppermute | solution.py:120
  46.5 6.6 %collective-permute-start.5 = (bf16[2,128,512]{2,1,0:T(8,128)(2,1)S(1)}, bf16[2,128,512]{2,1,0:T(8,128)(2,1)S(1)}, u32[]{:S(2)}, u32[]{:S(2)}) collective-permute-start(bf16[2,128,512]{2,1,0:T(8,128)(2,1)S(1)} %add_convert_fusion), channel_id=1, source_target_pairs={{0,3},{1,0},{2,1},{3,2},{4,7},{5,4},{6,5},{7,6},{8,11},{9,8},{10,9... | collective-permute-start | bytes 786440 | tf_op jit(solution)/shard_map/ppermute | solution.py:120

commit v9 on v8

--- a/solution.py
+++ b/solution.py
@@ -49,8 +49,9 @@
     g_all = (cot_ref[...].astype(jnp.float32) * factor).astype(jnp.bfloat16)
     q_rows = jnp.concatenate([q_all[:, h * HEAD_DIM:(h + 1) * HEAD_DIM] for h in range(group_size)], axis=0)
     g_rows = jnp.concatenate([g_all[:, h * HEAD_DIM:(h + 1) * HEAD_DIM] for h in range(group_size)], axis=0)
-    k_all = jnp.concatenate([r[:piece_len] for r in piece_refs] + [kown_ref[...]], axis=0)
-    v_all = jnp.concatenate([r[piece_len:2 * piece_len] for r in piece_refs] + [vown_ref[...]], axis=0)
+    cols = pl.ds(pl.multiple_of(pl.program_id(0) * HEAD_DIM, HEAD_DIM), HEAD_DIM)
+    k_all = jnp.concatenate([r[:piece_len, cols] for r in piece_refs] + [kown_ref[...]], axis=0)
+    v_all = jnp.concatenate([r[piece_len:2 * piece_len, cols] for r in piece_refs] + [vown_ref[...]], axis=0)
     s_ref[...] = lax.dot_general(k_all, q_rows, contract_minor, preferred_element_type=jnp.float32)
     dp_ref[...] = lax.dot_general(v_all, g_rows, contract_minor, preferred_element_type=jnp.float32)
     own_pos = lax.broadcasted_iota(jnp.int32, (resp_len, rows), 0)
@@ -99,8 +100,8 @@
     dk_all = jnp.dot(ds_all, q_rows, preferred_element_type=jnp.float32) * scaling
     dv_all = jnp.dot(pb_ref[...], g_rows, preferred_element_type=jnp.float32)
     for i, r in enumerate(part_refs):
-        r[0] = dk_all[i * piece_len:(i + 1) * piece_len].astype(jnp.bfloat16)
-        r[1] = dv_all[i * piece_len:(i + 1) * piece_len].astype(jnp.bfloat16)
+        r[0, :, cols] = dk_all[i * piece_len:(i + 1) * piece_len].astype(jnp.bfloat16)
+        r[1, :, cols] = dv_all[i * piece_len:(i + 1) * piece_len].astype(jnp.bfloat16)
     dkown_ref[...] = dk_all[prefix_rows:all_rows].astype(jnp.bfloat16)
     dvown_ref[...] = dv_all[prefix_rows:all_rows].astype(jnp.bfloat16)
     dq_rows = lax.dot_general(ds_all, k_all, contract_major, preferred_element_type=jnp.float32) * scaling
@@ -157,8 +158,8 @@
     group_width = (HEADS // KV_HEADS) * HEAD_DIM
     group_rows = (HEADS // KV_HEADS) * resp_len
     all_rows = n * piece_len + resp_len
-    piece_block = pl.BlockSpec((2 * piece_len + 16, HEAD_DIM), lambda g: (0, g))
-    part_block = pl.BlockSpec((2, piece_len, HEAD_DIM), lambda g: (0, 0, g))
+    piece_block = pl.BlockSpec(memory_space=pltpu.VMEM)
+    part_block = pl.BlockSpec(memory_space=pltpu.VMEM)
     results = pl.pallas_call(
         functools.partial(attention_kernel, n),
         grid=(KV_HEADS,),

time: 54.1 us -> 53.9 us (level)
  no operation moved by 1% of the time
where the time goes in v9:
time: 53.9 us; the launch traced here: 53.6 us
  waiting for transfers between devices  30.8 us (57%)
  starting transfers between devices  9.36 us (17%)
  Pallas kernels  6.8 us (13%)
  between operations  3.57 us (7%)
  other arithmetic  2.02 us (4%)
  local copies, waits for them, and re-layouts  1.05 us (2%)
    ppermute x6, waiting for transfers between devices, shifted(): return lax.ppermute(value, 'resp', [(i, (i + shift) % n) for i in range(n)])  30.8 us
    ppermute x6, starting transfers between devices, shifted(): return lax.ppermute(value, 'resp', [(i, (i + shift) % n) for i in range(n)])  9.36 us
    pallas_call x1, Pallas kernels, on_device(): pl.pallas_call(functools.partial(attention_kernel, n), grid=(KV_HEADS,),...  6.8 us
  transfers between devices with their start and end apart: 6, of which 6 were waited for; matrix products, arithmetic and copies ran while one was open for 0% of the time, Pallas kernels for 0%

profile of v9, /device:TPU:0, one launch (start us, length us, event | category | flops | bytes accessed | tf_op | source)
XLA Modules:
  0.0 53.6 jit_solution(11652355486245681136)
XLA Ops:
  0.6 0.0 copy-start
  2.8 0.1 maximum_bitcast_fusion
  2.8 0.0 copy-start.2
  2.8 0.0 copy-start.3
  2.8 1.0 %fusion.1.rest_0_ = bf16[272,512]{1,0:T(8,128)(2,1)S(1)} fusion(bf16[1,3]{1,0:T(2,128)(2,1)S(1)} %maximum_bitcast_fusion, bf16[128,512]{1,0:T(8,128)(2,1)} %bitcast.22, bf16[128,512]{1,0:T(8,128)(2,1)} %bitcast.23), kind=kLoop, calls=%fused_computation.3 | loop fusion | flops 1114112 | bytes 540678 | tf_op jit(solution)/shard_map/concatenate | solution.py:151
  3.8 3.1 %collective-permute-start = (bf16[272,512]{1,0:T(8,128)(2,1)S(1)}, bf16[272,512]{1,0:T(8,128)(2,1)S(1)}, u32[]{:S(2)}, u32[]{:S(2)}) collective-permute-start(bf16[272,512]{1,0:T(8,128)(2,1)S(1)} %fusion.1.rest_0_), channel_id=1, source_target_pairs={{0,1},{1,2},{2,3},{3,0},{4,5},{5,6},{6,7},{7,4},{8,9},{9,10},{10,1... | collective-permute-start | bytes 835592 | tf_op jit(solution)/shard_map/ppermute | solution.py:121
  6.9 2.1 %collective-permute-start.1 = (bf16[272,512]{1,0:T(8,128)(2,1)S(1)}, bf16[272,512]{1,0:T(8,128)(2,1)S(1)}, u32[]{:S(2)}, u32[]{:S(2)}) collective-permute-start(bf16[272,512]{1,0:T(8,128)(2,1)S(1)} %fusion.1.rest_0_), channel_id=1, source_target_pairs={{0,3},{1,0},{2,1},{3,2},{4,7},{5,4},{6,5},{7,6},{8,11},{9,8},{10,9... | collective-permute-start | bytes 835592 | tf_op jit(solution)/shard_map/ppermute | solution.py:121
  9.0 7.5 %collective-permute-done.rest_1_ = bf16[272,512]{1,0:T(8,128)(2,1)S(1)} collective-permute-done((bf16[272,512]{1,0:T(8,128)(2,1)S(1)}, bf16[272,512]{1,0:T(8,128)(2,1)S(1)}, u32[]{:S(2)}, u32[]{:S(2)}) %collective-permute-start) | collective-permute-done | bytes 278560 | tf_op jit(solution)/shard_map/ppermute | solution.py:121
  16.5 0.0 collective-permute-start.2
  17.3 0.1 pad_maximum_fusion.scalar_ref
  17.3 3.9 %collective-permute-done.1.rest_2_ = bf16[272,512]{1,0:T(8,128)(2,1)S(1)} collective-permute-done((bf16[272,512]{1,0:T(8,128)(2,1)S(1)}, bf16[272,512]{1,0:T(8,128)(2,1)S(1)}, u32[]{:S(2)}, u32[]{:S(2)}) %collective-permute-start.1) | collective-permute-done | bytes 278560 | tf_op jit(solution)/shard_map/ppermute | solution.py:121
  21.2 6.4 %collective-permute-done.2.rest_3_ = bf16[272,512]{1,0:T(8,128)(2,1)S(1)} collective-permute-done((bf16[272,512]{1,0:T(8,128)(2,1)S(1)}, bf16[272,512]{1,0:T(8,128)(2,1)S(1)}, u32[]{:S(2)}, u32[]{:S(2)}) %collective-permute-start.2) | collective-permute-done | bytes 278560 | tf_op jit(solution)/shard_map/ppermute | solution.py:121
  27.6 0.0 copy-done
  27.6 0.0 copy-done.2
  27.6 0.0 copy-done.3
  27.6 0.0 copy-start.1
  27.6 1.0 %copy-done.1 = bf16[1,1,32,8192]{3,2,1,0:T(8,128)(2,1)S(1)} copy-done((bf16[1,1,32,8192]{3,2,1,0:T(8,128)(2,1)S(1)}, bf16[1,1,32,8192]{3,2,1,0:T(8,128)(2,1)}, u32[]{:S(2)}) %copy-start.1) | copy-done | bytes 524312
  28.6 6.8 %shard_map.145 = (bf16[32,8192]{1,0:T(8,128)(2,1)}, bf16[32,512]{1,0:T(8,128)(2,1)}, bf16[32,512]{1,0:T(8,128)(2,1)}, bf16[2,128,512]{2,1,0:T(8,128)(2,1)S(1)}, ...) custom-call(f32[4]{0:T(128)S(1)} %pad_maximum_fusion.scalar_ref, ...), custom_call_target="tpu_custom_call" | custom-call | tf_op jit(solution)/shard_map/pallas_call | solution.py:163
  35.4 1.7 %collective-permute-start.4 = (bf16[2,128,512]{2,1,0:T(8,128)(2,1)S(1)}, bf16[2,128,512]{2,1,0:T(8,128)(2,1)S(1)}, u32[]{:S(2)}, u32[]{:S(2)}) collective-permute-start(bf16[2,128,512]{2,1,0:T(8,128)(2,1)S(1)} %get-tuple-element.32), channel_id=1, source_target_pairs={{0,3},{1,0},{2,1},{3,2},{4,7},{5,4},{6,5},{7,6},{8,11},{9,8},{10,9... | collective-permute-start | bytes 786440 | tf_op jit(solution)/shard_map/ppermute | solution.py:121
  37.1 0.3 collective-permute-start.3
  37.5 8.8 %collective-permute-done.4 = bf16[2,128,512]{2,1,0:T(8,128)(2,1)S(1)} collective-permute-done((bf16[2,128,512]{2,1,0:T(8,128)(2,1)S(1)}, bf16[2,128,512]{2,1,0:T(8,128)(2,1)S(1)}, u32[]{:S(2)}, u32[]{:S(2)}) %collective-permute-start.4) | collective-permute-done | bytes 262176 | tf_op jit(solution)/shard_map/ppermute | solution.py:121
  46.2 0.1 add_convert_fusion
  46.3 2.2 %collective-permute-start.5 = (bf16[2,128,512]{2,1,0:T(8,128)(2,1)S(1)}, bf16[2,128,512]{2,1,0:T(8,128)(2,1)S(1)}, u32[]{:S(2)}, u32[]{:S(2)}) collective-permute-start(bf16[2,128,512]{2,1,0:T(8,128)(2,1)S(1)} %add_convert_fusion), channel_id=1, source_target_pairs={{0,3},{1,0},{2,1},{3,2},{4,7},{5,4},{6,5},{7,6},{8,11},{9,8},{10,9... | collective-permute-start | bytes 786440 | tf_op jit(solution)/shard_map/ppermute | solution.py:121
  48.5 1.6 %collective-permute-done.3 = bf16[2,128,512]{2,1,0:T(8,128)(2,1)S(1)} collective-permute-done((bf16[2,128,512]{2,1,0:T(8,128)(2,1)S(1)}, bf16[2,128,512]{2,1,0:T(8,128)(2,1)S(1)}, u32[]{:S(2)}, u32[]{:S(2)}) %collective-permute-start.3) | collective-permute-done | bytes 262176 | tf_op jit(solution)/shard_map/ppermute | solution.py:121
  50.0 2.8 %collective-permute-done.5 = bf16[2,128,512]{2,1,0:T(8,128)(2,1)S(1)} collective-permute-done((bf16[2,128,512]{2,1,0:T(8,128)(2,1)S(1)}, bf16[2,128,512]{2,1,0:T(8,128)(2,1)S(1)}, u32[]{:S(2)}, u32[]{:S(2)}) %collective-permute-start.5) | collective-permute-done | bytes 262176 | tf_op jit(solution)/shard_map/ppermute | solution.py:121
  52.8 0.8 %add_convert_fusion.1 = (bf16[1,128,512]{2,1,0:T(8,128)(2,1)}, bf16[1,128,512]{2,1,0:T(8,128)(2,1)}) fusion(bf16[2,128,512]{2,1,0:T(8,128)(2,1)S(1)} %collective-permute-done.5, bf16[2,128,512]{2,1,0:T(8,128)(2,1)S(1)} %collective-permute-done.3, bf16[2,128,512]{2,1,0:T(8,128)(2,1)S(1)} %get-tuple-element.29), kind=kLoop, calls=%fused_computation.4 | loop fusion | flops 786432 | bytes 1048576 | tf_op jit(solution)/shard_map/convert_element_type | solution.py:202
Async XLA Ops:
  0.6 26.9 %copy-start = (bf16[1,1,32,8192]{3,2,1,0:T(8,128)(2,1)S(1)}, bf16[1,1,32,8192]{3,2,1,0:T(8,128)(2,1)}, u32[]{:S(2)}) copy-start(bf16[1,1,32,8192]{3,2,1,0:T(8,128)(2,1)} %param.12) | copy-start | bytes 1572868
  2.8 24.7 %copy-start.2 = (bf16[1,1,32,512]{3,2,1,0:T(8,128)(2,1)S(1)}, bf16[1,1,32,512]{3,2,1,0:T(8,128)(2,1)}, u32[]{:S(2)}) copy-start(bf16[1,1,32,512]{3,2,1,0:T(8,128)(2,1)} %param.14) | copy-start | bytes 98308
  2.8 24.7 %copy-start.3 = (bf16[1,1,32,512]{3,2,1,0:T(8,128)(2,1)S(1)}, bf16[1,1,32,512]{3,2,1,0:T(8,128)(2,1)}, u32[]{:S(2)}) copy-start(bf16[1,1,32,512]{3,2,1,0:T(8,128)(2,1)} %param.15) | copy-start | bytes 98308
  3.8 12.6 %collective-permute-start = (bf16[272,512]{1,0:T(8,128)(2,1)S(1)}, bf16[272,512]{1,0:T(8,128)(2,1)S(1)}, u32[]{:S(2)}, u32[]{:S(2)}) collective-permute-start(bf16[272,512]{1,0:T(8,128)(2,1)S(1)} %fusion.1.rest_0_), channel_id=1, source_target_pairs={{0,1},{1,2},{2,3},{3,0},{4,5},{5,6},{6,7},{7,4},{8,9},{9,10},{10,1... | collective-permute-start | bytes 835592 | tf_op jit(solution)/shard_map/ppermute | solution.py:121
  6.9 14.3 %collective-permute-start.1 = (bf16[272,512]{1,0:T(8,128)(2,1)S(1)}, bf16[272,512]{1,0:T(8,128)(2,1)S(1)}, u32[]{:S(2)}, u32[]{:S(2)}) collective-permute-start(bf16[272,512]{1,0:T(8,128)(2,1)S(1)} %fusion.1.rest_0_), channel_id=1, source_target_pairs={{0,3},{1,0},{2,1},{3,2},{4,7},{5,4},{6,5},{7,6},{8,11},{9,8},{10,9... | collective-permute-start | bytes 835592 | tf_op jit(solution)/shard_map/ppermute | solution.py:121
  16.5 11.1 %collective-permute-start.2 = (bf16[272,512]{1,0:T(8,128)(2,1)S(1)}, bf16[272,512]{1,0:T(8,128)(2,1)S(1)}, u32[]{:S(2)}, u32[]{:S(2)}) collective-permute-start(bf16[272,512]{1,0:T(8,128)(2,1)S(1)} %collective-permute-done.rest_1_), channel_id=1, source_target_pairs={{0,1},{1,2},{2,3},{3,0},{4,5},{5,6},{6,7},{7,4},{8,9},{9,10},{10,1... | collective-permute-start | bytes 835592 | tf_op jit(solution)/shard_map/ppermute | solution.py:121
  27.6 1.0 %copy-start.1 = (bf16[1,1,32,8192]{3,2,1,0:T(8,128)(2,1)S(1)}, bf16[1,1,32,8192]{3,2,1,0:T(8,128)(2,1)}, u32[]{:S(2)}) copy-start(bf16[1,1,32,8192]{3,2,1,0:T(8,128)(2,1)} %param.13) | copy-start | bytes 1572868
  35.4 10.8 %collective-permute-start.4 = (bf16[2,128,512]{2,1,0:T(8,128)(2,1)S(1)}, bf16[2,128,512]{2,1,0:T(8,128)(2,1)S(1)}, u32[]{:S(2)}, u32[]{:S(2)}) collective-permute-start(bf16[2,128,512]{2,1,0:T(8,128)(2,1)S(1)} %get-tuple-element.32), channel_id=1, source_target_pairs={{0,3},{1,0},{2,1},{3,2},{4,7},{5,4},{6,5},{7,6},{8,11},{9,8},{10,9... | collective-permute-start | bytes 786440 | tf_op jit(solution)/shard_map/ppermute | solution.py:121
  37.1 12.9 %collective-permute-start.3 = (bf16[2,128,512]{2,1,0:T(8,128)(2,1)S(1)}, bf16[2,128,512]{2,1,0:T(8,128)(2,1)S(1)}, u32[]{:S(2)}, u32[]{:S(2)}) collective-permute-start(bf16[2,128,512]{2,1,0:T(8,128)(2,1)S(1)} %get-tuple-element.30), channel_id=1, source_target_pairs={{0,1},{1,2},{2,3},{3,0},{4,5},{5,6},{6,7},{7,4},{8,9},{9,10},{10,1... | collective-permute-start | bytes 786440 | tf_op jit(solution)/shard_map/ppermute | solution.py:121
  46.3 6.5 %collective-permute-start.5 = (bf16[2,128,512]{2,1,0:T(8,128)(2,1)S(1)}, bf16[2,128,512]{2,1,0:T(8,128)(2,1)S(1)}, u32[]{:S(2)}, u32[]{:S(2)}) collective-permute-start(bf16[2,128,512]{2,1,0:T(8,128)(2,1)S(1)} %add_convert_fusion), channel_id=1, source_target_pairs={{0,3},{1,0},{2,1},{3,2},{4,7},{5,4},{6,5},{7,6},{8,11},{9,8},{10,9... | collective-permute-start | bytes 786440 | tf_op jit(solution)/shard_map/ppermute | solution.py:121

commit v10 on v9

--- a/solution.py
+++ b/solution.py
@@ -45,8 +45,9 @@
 
     contract_minor = (((1,), (1,)), ((), ()))
     contract_major = (((0,), (0,)), ((), ()))
-    q_all = q_ref[...]
-    g_all = (cot_ref[...].astype(jnp.float32) * factor).astype(jnp.bfloat16)
+    group_cols = pl.ds(pl.multiple_of(pl.program_id(0) * rows * HEAD_DIM // resp_len, HEAD_DIM), rows * HEAD_DIM // resp_len)
+    q_all = q_ref[:, group_cols]
+    g_all = (cot_ref[:, group_cols].astype(jnp.float32) * factor).astype(jnp.bfloat16)
     q_rows = jnp.concatenate([q_all[:, h * HEAD_DIM:(h + 1) * HEAD_DIM] for h in range(group_size)], axis=0)
     g_rows = jnp.concatenate([g_all[:, h * HEAD_DIM:(h + 1) * HEAD_DIM] for h in range(group_size)], axis=0)
     cols = pl.ds(pl.multiple_of(pl.program_id(0) * HEAD_DIM, HEAD_DIM), HEAD_DIM)
@@ -165,8 +166,8 @@
         grid=(KV_HEADS,),
         in_specs=[
             pl.BlockSpec(memory_space=pltpu.SMEM),
-            pl.BlockSpec((resp_len, group_width), lambda g: (0, g)),
-            pl.BlockSpec((resp_len, group_width), lambda g: (0, g)),
+            pl.BlockSpec(memory_space=pltpu.VMEM),
+            pl.BlockSpec(memory_space=pltpu.VMEM),
             pl.BlockSpec((resp_len, HEAD_DIM), lambda g: (0, g)),
             pl.BlockSpec((resp_len, HEAD_DIM), lambda g: (0, g)),
         ]
@@ -198,8 +199,10 @@
         returned = [parts[0], shifted(parts[2], 1, n), shifted(merged, -1, n)]
     else:
         returned = [parts[0]] + [shifted(parts[k], -k, n) for k in range(1, n)]
-    summed_keys = sum(r[0].astype(jnp.float32) for r in returned).astype(jnp.bfloat16)
-    summed_values = sum(r[1].astype(jnp.float32) for r in returned).astype(jnp.bfloat16)
+    early_sum = lax.optimization_barrier(sum(r.astype(jnp.float32) for r in returned[:-1]))
+    summed = early_sum + returned[-1].astype(jnp.float32)
+    summed_keys = summed[0].astype(jnp.bfloat16)
+    summed_values = summed[1].astype(jnp.bfloat16)
     return (
         grad_q[None, None],
         grad_k[None, None],

time: 53.9 us -> 53.8 us (level)
  local copies, waits for them, and re-layouts: 1.05 us -> 1.76 us
  other arithmetic: 2.02 us -> 1.36 us
    convert_element_type x1 -> x0, other arithmetic: 0.8 us -> none  [on_device(): sum((r[1].astype(jnp.float32) for r in returned)).astype(jnp.bfloat16)]
    slice x0 -> x1, local copies, waits for them, and re-layouts: none -> 0.72 us  [on_device(): summed_values = summed[1].astype(jnp.bfloat16)]
where the time goes in v10:
time: 53.8 us; the launch traced here: 53.6 us
  waiting for transfers between devices  30.7 us (57%)
  starting transfers between devices  9.39 us (17%)
  Pallas kernels  6.73 us (13%)
  between operations  3.58 us (7%)
  local copies, waits for them, and re-layouts  1.76 us (3%)
  other arithmetic  1.36 us (3%)
    ppermute x6, waiting for transfers between devices, shifted(): return lax.ppermute(value, 'resp', [(i, (i + shift) % n) for i in range(n)])  30.7 us
    ppermute x6, starting transfers between devices, shifted(): return lax.ppermute(value, 'resp', [(i, (i + shift) % n) for i in range(n)])  9.39 us
    pallas_call x1, Pallas kernels, on_device(): pl.pallas_call(functools.partial(attention_kernel, n), grid=(KV_HEADS,),...  6.73 us
  transfers between devices with their start and end apart: 6, of which 6 were waited for; matrix products, arithmetic and copies ran while one was open for 0% of the time, Pallas kernels for 0%

profile of v10, /device:TPU:0, one launch (start us, length us, event | category | flops | bytes accessed | tf_op | source)
XLA Modules:
  0.0 53.6 jit_solution(17260805956143042013)
XLA Ops:
  0.6 0.0 copy-start
  2.8 0.1 maximum_bitcast_fusion
  2.8 0.0 copy-start.2
  2.8 0.0 copy-start.3
  2.8 1.0 %fusion.1.rest_0_ = bf16[272,512]{1,0:T(8,128)(2,1)S(1)} fusion(bf16[1,3]{1,0:T(2,128)(2,1)S(1)} %maximum_bitcast_fusion, bf16[128,512]{1,0:T(8,128)(2,1)} %bitcast.22, bf16[128,512]{1,0:T(8,128)(2,1)} %bitcast.23), kind=kLoop, calls=%fused_computation.5 | loop fusion | flops 1114112 | bytes 540678 | tf_op jit(solution)/shard_map/concatenate | solution.py:152
  3.8 3.1 %collective-permute-start = (bf16[272,512]{1,0:T(8,128)(2,1)S(1)}, bf16[272,512]{1,0:T(8,128)(2,1)S(1)}, u32[]{:S(2)}, u32[]{:S(2)}) collective-permute-start(bf16[272,512]{1,0:T(8,128)(2,1)S(1)} %fusion.1.rest_0_), channel_id=1, source_target_pairs={{0,1},{1,2},{2,3},{3,0},{4,5},{5,6},{6,7},{7,4},{8,9},{9,10},{10,1... | collective-permute-start | bytes 835592 | tf_op jit(solution)/shard_map/ppermute | solution.py:122
  6.9 2.1 %collective-permute-start.1 = (bf16[272,512]{1,0:T(8,128)(2,1)S(1)}, bf16[272,512]{1,0:T(8,128)(2,1)S(1)}, u32[]{:S(2)}, u32[]{:S(2)}) collective-permute-start(bf16[272,512]{1,0:T(8,128)(2,1)S(1)} %fusion.1.rest_0_), channel_id=1, source_target_pairs={{0,3},{1,0},{2,1},{3,2},{4,7},{5,4},{6,5},{7,6},{8,11},{9,8},{10,9... | collective-permute-start | bytes 835592 | tf_op jit(solution)/shard_map/ppermute | solution.py:122
  9.0 7.5 %collective-permute-done.rest_1_ = bf16[272,512]{1,0:T(8,128)(2,1)S(1)} collective-permute-done((bf16[272,512]{1,0:T(8,128)(2,1)S(1)}, bf16[272,512]{1,0:T(8,128)(2,1)S(1)}, u32[]{:S(2)}, u32[]{:S(2)}) %collective-permute-start) | collective-permute-done | bytes 278560 | tf_op jit(solution)/shard_map/ppermute | solution.py:122
  16.5 0.0 collective-permute-start.2
  17.3 0.1 pad_maximum_fusion.scalar_ref
  17.3 3.9 %collective-permute-done.1.rest_2_ = bf16[272,512]{1,0:T(8,128)(2,1)S(1)} collective-permute-done((bf16[272,512]{1,0:T(8,128)(2,1)S(1)}, bf16[272,512]{1,0:T(8,128)(2,1)S(1)}, u32[]{:S(2)}, u32[]{:S(2)}) %collective-permute-start.1) | collective-permute-done | bytes 278560 | tf_op jit(solution)/shard_map/ppermute | solution.py:122
  21.2 6.4 %collective-permute-done.2.rest_3_ = bf16[272,512]{1,0:T(8,128)(2,1)S(1)} collective-permute-done((bf16[272,512]{1,0:T(8,128)(2,1)S(1)}, bf16[272,512]{1,0:T(8,128)(2,1)S(1)}, u32[]{:S(2)}, u32[]{:S(2)}) %collective-permute-start.2) | collective-permute-done | bytes 278560 | tf_op jit(solution)/shard_map/ppermute | solution.py:122
  27.6 0.0 copy-done
  27.6 0.0 copy-done.2
  27.6 0.0 copy-done.3
  27.6 0.0 copy-start.1
  27.6 1.0 %copy-done.1 = bf16[1,1,32,8192]{3,2,1,0:T(8,128)(2,1)S(1)} copy-done((bf16[1,1,32,8192]{3,2,1,0:T(8,128)(2,1)S(1)}, bf16[1,1,32,8192]{3,2,1,0:T(8,128)(2,1)}, u32[]{:S(2)}) %copy-start.1) | copy-done | bytes 524312
  28.6 6.7 %shard_map.145 = (bf16[32,8192]{1,0:T(8,128)(2,1)}, bf16[32,512]{1,0:T(8,128)(2,1)}, bf16[32,512]{1,0:T(8,128)(2,1)}, bf16[2,128,512]{2,1,0:T(8,128)(2,1)S(1)}, ...) custom-call(f32[4]{0:T(128)S(1)} %pad_maximum_fusion.scalar_ref, ...), custom_call_target="tpu_custom_call" | custom-call | tf_op jit(solution)/shard_map/pallas_call | solution.py:164
  35.4 1.7 %collective-permute-start.4 = (bf16[2,128,512]{2,1,0:T(8,128)(2,1)S(1)}, bf16[2,128,512]{2,1,0:T(8,128)(2,1)S(1)}, u32[]{:S(2)}, u32[]{:S(2)}) collective-permute-start(bf16[2,128,512]{2,1,0:T(8,128)(2,1)S(1)} %get-tuple-element.32), channel_id=1, source_target_pairs={{0,3},{1,0},{2,1},{3,2},{4,7},{5,4},{6,5},{7,6},{8,11},{9,8},{10,9... | collective-permute-start | bytes 786440 | tf_op jit(solution)/shard_map/ppermute | solution.py:122
  37.1 0.3 collective-permute-start.3
  37.4 8.7 %collective-permute-done.4 = bf16[2,128,512]{2,1,0:T(8,128)(2,1)S(1)} collective-permute-done((bf16[2,128,512]{2,1,0:T(8,128)(2,1)S(1)}, bf16[2,128,512]{2,1,0:T(8,128)(2,1)S(1)}, u32[]{:S(2)}, u32[]{:S(2)}) %collective-permute-start.4) | collective-permute-done | bytes 262176 | tf_op jit(solution)/shard_map/ppermute | solution.py:122
  46.1 0.1 add_convert_fusion.1
  46.2 2.2 %collective-permute-start.5 = (bf16[2,128,512]{2,1,0:T(8,128)(2,1)S(1)}, bf16[2,128,512]{2,1,0:T(8,128)(2,1)S(1)}, u32[]{:S(2)}, u32[]{:S(2)}) collective-permute-start(bf16[2,128,512]{2,1,0:T(8,128)(2,1)S(1)} %add_convert_fusion.1), channel_id=1, source_target_pairs={{0,3},{1,0},{2,1},{3,2},{4,7},{5,4},{6,5},{7,6},{8,11},{9,8},{10,9... | collective-permute-start | bytes 786440 | tf_op jit(solution)/shard_map/ppermute | solution.py:122
  48.4 1.6 %collective-permute-done.3 = bf16[2,128,512]{2,1,0:T(8,128)(2,1)S(1)} collective-permute-done((bf16[2,128,512]{2,1,0:T(8,128)(2,1)S(1)}, bf16[2,128,512]{2,1,0:T(8,128)(2,1)S(1)}, u32[]{:S(2)}, u32[]{:S(2)}) %collective-permute-start.3) | collective-permute-done | bytes 262176 | tf_op jit(solution)/shard_map/ppermute | solution.py:122
  50.0 0.1 convert_add_fusion
  50.1 2.7 %collective-permute-done.5 = bf16[2,128,512]{2,1,0:T(8,128)(2,1)S(1)} collective-permute-done((bf16[2,128,512]{2,1,0:T(8,128)(2,1)S(1)}, bf16[2,128,512]{2,1,0:T(8,128)(2,1)S(1)}, u32[]{:S(2)}, u32[]{:S(2)}) %collective-permute-start.5) | collective-permute-done | bytes 262176 | tf_op jit(solution)/shard_map/ppermute | solution.py:122
  52.8 0.1 add_convert_fusion
  52.8 0.7 %fusion.2 = (bf16[1,128,512]{2,1,0:T(8,128)(2,1)}, bf16[1,128,512]{2,1,0:T(8,128)(2,1)}) fusion(bf16[2,128,512]{2,1,0:T(8,128)(2,1)S(1)} %add_convert_fusion), kind=kLoop, calls=%fused_computation.8 | loop fusion | bytes 524288 | tf_op jit(solution)/shard_map/slice | solution.py:205
Async XLA Ops:
  0.6 26.9 %copy-start = (bf16[1,1,32,8192]{3,2,1,0:T(8,128)(2,1)S(1)}, bf16[1,1,32,8192]{3,2,1,0:T(8,128)(2,1)}, u32[]{:S(2)}) copy-start(bf16[1,1,32,8192]{3,2,1,0:T(8,128)(2,1)} %param.12) | copy-start | bytes 1572868
  2.8 24.7 %copy-start.2 = (bf16[1,1,32,512]{3,2,1,0:T(8,128)(2,1)S(1)}, bf16[1,1,32,512]{3,2,1,0:T(8,128)(2,1)}, u32[]{:S(2)}) copy-start(bf16[1,1,32,512]{3,2,1,0:T(8,128)(2,1)} %param.14) | copy-start | bytes 98308
  2.8 24.7 %copy-start.3 = (bf16[1,1,32,512]{3,2,1,0:T(8,128)(2,1)S(1)}, bf16[1,1,32,512]{3,2,1,0:T(8,128)(2,1)}, u32[]{:S(2)}) copy-start(bf16[1,1,32,512]{3,2,1,0:T(8,128)(2,1)} %param.15) | copy-start | bytes 98308
  3.8 12.6 %collective-permute-start = (bf16[272,512]{1,0:T(8,128)(2,1)S(1)}, bf16[272,512]{1,0:T(8,128)(2,1)S(1)}, u32[]{:S(2)}, u32[]{:S(2)}) collective-permute-start(bf16[272,512]{1,0:T(8,128)(2,1)S(1)} %fusion.1.rest_0_), channel_id=1, source_target_pairs={{0,1},{1,2},{2,3},{3,0},{4,5},{5,6},{6,7},{7,4},{8,9},{9,10},{10,1... | collective-permute-start | bytes 835592 | tf_op jit(solution)/shard_map/ppermute | solution.py:122
  6.9 14.3 %collective-permute-start.1 = (bf16[272,512]{1,0:T(8,128)(2,1)S(1)}, bf16[272,512]{1,0:T(8,128)(2,1)S(1)}, u32[]{:S(2)}, u32[]{:S(2)}) collective-permute-start(bf16[272,512]{1,0:T(8,128)(2,1)S(1)} %fusion.1.rest_0_), channel_id=1, source_target_pairs={{0,3},{1,0},{2,1},{3,2},{4,7},{5,4},{6,5},{7,6},{8,11},{9,8},{10,9... | collective-permute-start | bytes 835592 | tf_op jit(solution)/shard_map/ppermute | solution.py:122
  16.5 11.1 %collective-permute-start.2 = (bf16[272,512]{1,0:T(8,128)(2,1)S(1)}, bf16[272,512]{1,0:T(8,128)(2,1)S(1)}, u32[]{:S(2)}, u32[]{:S(2)}) collective-permute-start(bf16[272,512]{1,0:T(8,128)(2,1)S(1)} %collective-permute-done.rest_1_), channel_id=1, source_target_pairs={{0,1},{1,2},{2,3},{3,0},{4,5},{5,6},{6,7},{7,4},{8,9},{9,10},{10,1... | collective-permute-start | bytes 835592 | tf_op jit(solution)/shard_map/ppermute | solution.py:122
  27.6 1.0 %copy-start.1 = (bf16[1,1,32,8192]{3,2,1,0:T(8,128)(2,1)S(1)}, bf16[1,1,32,8192]{3,2,1,0:T(8,128)(2,1)}, u32[]{:S(2)}) copy-start(bf16[1,1,32,8192]{3,2,1,0:T(8,128)(2,1)} %param.13) | copy-start | bytes 1572868
  35.4 10.7 %collective-permute-start.4 = (bf16[2,128,512]{2,1,0:T(8,128)(2,1)S(1)}, bf16[2,128,512]{2,1,0:T(8,128)(2,1)S(1)}, u32[]{:S(2)}, u32[]{:S(2)}) collective-permute-start(bf16[2,128,512]{2,1,0:T(8,128)(2,1)S(1)} %get-tuple-element.32), channel_id=1, source_target_pairs={{0,3},{1,0},{2,1},{3,2},{4,7},{5,4},{6,5},{7,6},{8,11},{9,8},{10,9... | collective-permute-start | bytes 786440 | tf_op jit(solution)/shard_map/ppermute | solution.py:122
  37.1 12.9 %collective-permute-start.3 = (bf16[2,128,512]{2,1,0:T(8,128)(2,1)S(1)}, bf16[2,128,512]{2,1,0:T(8,128)(2,1)S(1)}, u32[]{:S(2)}, u32[]{:S(2)}) collective-permute-start(bf16[2,128,512]{2,1,0:T(8,128)(2,1)S(1)} %get-tuple-element.30), channel_id=1, source_target_pairs={{0,1},{1,2},{2,3},{3,0},{4,5},{5,6},{6,7},{7,4},{8,9},{9,10},{10,1... | collective-permute-start | bytes 786440 | tf_op jit(solution)/shard_map/ppermute | solution.py:122
  46.2 6.6 %collective-permute-start.5 = (bf16[2,128,512]{2,1,0:T(8,128)(2,1)S(1)}, bf16[2,128,512]{2,1,0:T(8,128)(2,1)S(1)}, u32[]{:S(2)}, u32[]{:S(2)}) collective-permute-start(bf16[2,128,512]{2,1,0:T(8,128)(2,1)S(1)} %add_convert_fusion.1), channel_id=1, source_target_pairs={{0,3},{1,0},{2,1},{3,2},{4,7},{5,4},{6,5},{7,6},{8,11},{9,8},{10,9... | collective-permute-start | bytes 786440 | tf_op jit(solution)/shard_map/ppermute | solution.py:122

commit v11 on v9

--- a/solution.py
+++ b/solution.py
@@ -46,7 +46,7 @@
     contract_minor = (((1,), (1,)), ((), ()))
     contract_major = (((0,), (0,)), ((), ()))
     q_all = q_ref[...]
-    g_all = (cot_ref[...].astype(jnp.float32) * factor).astype(jnp.bfloat16)
+    g_all = cot_ref[...]
     q_rows = jnp.concatenate([q_all[:, h * HEAD_DIM:(h + 1) * HEAD_DIM] for h in range(group_size)], axis=0)
     g_rows = jnp.concatenate([g_all[:, h * HEAD_DIM:(h + 1) * HEAD_DIM] for h in range(group_size)], axis=0)
     cols = pl.ds(pl.multiple_of(pl.program_id(0) * HEAD_DIM, HEAD_DIM), HEAD_DIM)
@@ -155,6 +155,9 @@
     else:
         pieces = [local_kv] + [shifted(local_kv, k, n) for k in range(1, n)]
     scalars = jnp.stack([weight[0], lengths[0][0].astype(jnp.float32), own_term, count_real])
+    positions = jnp.arange(resp_len, dtype=jnp.int32)
+    factor = jnp.where(positions < lengths[0][0], weight[0], 0.0)
+    grad_out = (cotangent[0, 0].astype(jnp.float32) * factor[:, None]).astype(jnp.bfloat16)
     group_width = (HEADS // KV_HEADS) * HEAD_DIM
     group_rows = (HEADS // KV_HEADS) * resp_len
     all_rows = n * piece_len + resp_len
@@ -188,7 +191,7 @@
         scratch_shapes=[pltpu.VMEM((all_rows, group_rows), jnp.float32) for _ in range(3)]
         + [pltpu.VMEM((all_rows, group_rows), jnp.bfloat16) for _ in range(2)],
         compiler_params=pltpu.CompilerParams(vmem_limit_bytes=48 * 1024 * 1024),
-    )(scalars, queries[0, 0], cotangent[0, 0], resp_keys[0, 0], resp_values[0, 0], *pieces)
+    )(scalars, queries[0, 0], grad_out, resp_keys[0, 0], resp_values[0, 0], *pieces)
     grad_q, grad_k, grad_v = results[:3]
     parts = results[3:-1]
     forget_loss = results[-1]

time: 53.9 us -> 52.7 us (0.978)
  local copies, waits for them, and re-layouts: 1.05 us -> 0.02 us
    unnamed x8, local copies, waits for them, and re-layouts: 1.05 us -> 0.02 us
  transfers between devices with their start and end apart: 6 -> 6, of which waited for: 6 -> 6; matrix products, arithmetic and copies ran while one was open for 0% -> 1% of each run, Pallas kernels for 0% -> 0%
where the time goes in v11:
time: 52.7 us; the launch traced here: 52.6 us
  waiting for transfers between devices  30.6 us (58%)
  starting transfers between devices  9.41 us (18%)
  Pallas kernels  6.79 us (13%)
  between operations  3.59 us (7%)
  other arithmetic  2.17 us (4%)
    ppermute x6, waiting for transfers between devices, shifted(): return lax.ppermute(value, 'resp', [(i, (i + shift) % n) for i in range(n)])  30.6 us
    ppermute x6, starting transfers between devices, shifted(): return lax.ppermute(value, 'resp', [(i, (i + shift) % n) for i in range(n)])  9.41 us
    pallas_call x1, Pallas kernels, on_device(): pl.pallas_call(functools.partial(attention_kernel, n), grid=(KV_HEADS,),...  6.79 us
  transfers between devices with their start and end apart: 6, of which 6 were waited for; matrix products, arithmetic and copies ran while one was open for 1% of the time, Pallas kernels for 0%

profile of v11, /device:TPU:0, one launch (start us, length us, event | category | flops | bytes accessed | tf_op | source)
XLA Modules:
  0.0 52.6 jit_solution(5724616272960178301)
XLA Ops:
  0.6 0.0 copy-start.3
  2.8 0.1 maximum_bitcast_fusion
  2.8 1.0 %fusion.2.rest_0_ = bf16[272,512]{1,0:T(8,128)(2,1)S(1)} fusion(bf16[1,3]{1,0:T(2,128)(2,1)S(1)} %maximum_bitcast_fusion, bf16[128,512]{1,0:T(8,128)(2,1)} %bitcast.27, bf16[128,512]{1,0:T(8,128)(2,1)} %bitcast.28), kind=kLoop, calls=%fused_computation.5 | loop fusion | flops 1114112 | bytes 540678 | tf_op jit(solution)/shard_map/concatenate | solution.py:151
  3.8 3.1 %collective-permute-start = (bf16[272,512]{1,0:T(8,128)(2,1)S(1)}, bf16[272,512]{1,0:T(8,128)(2,1)S(1)}, u32[]{:S(2)}, u32[]{:S(2)}) collective-permute-start(bf16[272,512]{1,0:T(8,128)(2,1)S(1)} %fusion.2.rest_0_), channel_id=1, source_target_pairs={{0,1},{1,2},{2,3},{3,0},{4,5},{5,6},{6,7},{7,4},{8,9},{9,10},{10,1... | collective-permute-start | bytes 835592 | tf_op jit(solution)/shard_map/ppermute | solution.py:121
  6.9 2.1 %collective-permute-start.1 = (bf16[272,512]{1,0:T(8,128)(2,1)S(1)}, bf16[272,512]{1,0:T(8,128)(2,1)S(1)}, u32[]{:S(2)}, u32[]{:S(2)}) collective-permute-start(bf16[272,512]{1,0:T(8,128)(2,1)S(1)} %fusion.2.rest_0_), channel_id=1, source_target_pairs={{0,3},{1,0},{2,1},{3,2},{4,7},{5,4},{6,5},{7,6},{8,11},{9,8},{10,9... | collective-permute-start | bytes 835592 | tf_op jit(solution)/shard_map/ppermute | solution.py:121
  9.8 0.0 copy-start
  9.8 6.7 %collective-permute-done.rest_1_ = bf16[272,512]{1,0:T(8,128)(2,1)S(1)} collective-permute-done((bf16[272,512]{1,0:T(8,128)(2,1)S(1)}, bf16[272,512]{1,0:T(8,128)(2,1)S(1)}, u32[]{:S(2)}, u32[]{:S(2)}) %collective-permute-start) | collective-permute-done | bytes 278560 | tf_op jit(solution)/shard_map/ppermute | solution.py:121
  16.5 0.0 collective-permute-start.2
  16.5 0.0 copy-done.3
  16.5 0.0 copy-start.1
  16.5 0.0 copy-start.2
  16.5 0.2 fusion.cot_ref
  16.6 0.1 pad_maximum_fusion.scalar_ref
  16.7 4.5 %collective-permute-done.1.rest_2_ = bf16[272,512]{1,0:T(8,128)(2,1)S(1)} collective-permute-done((bf16[272,512]{1,0:T(8,128)(2,1)S(1)}, bf16[272,512]{1,0:T(8,128)(2,1)S(1)}, u32[]{:S(2)}, u32[]{:S(2)}) %collective-permute-start.1) | collective-permute-done | bytes 278560 | tf_op jit(solution)/shard_map/ppermute | solution.py:121
  21.2 6.4 %collective-permute-done.2.rest_3_ = bf16[272,512]{1,0:T(8,128)(2,1)S(1)} collective-permute-done((bf16[272,512]{1,0:T(8,128)(2,1)S(1)}, bf16[272,512]{1,0:T(8,128)(2,1)S(1)}, u32[]{:S(2)}, u32[]{:S(2)}) %collective-permute-start.2) | collective-permute-done | bytes 278560 | tf_op jit(solution)/shard_map/ppermute | solution.py:121
  27.6 0.0 copy-done
  27.6 0.0 copy-done.1
  27.6 0.0 copy-done.2
  27.6 6.8 %shard_map.145 = (bf16[32,8192]{1,0:T(8,128)(2,1)}, bf16[32,512]{1,0:T(8,128)(2,1)}, bf16[32,512]{1,0:T(8,128)(2,1)}, bf16[2,128,512]{2,1,0:T(8,128)(2,1)S(1)}, ...) custom-call(f32[4]{0:T(128)S(1)} %pad_maximum_fusion.scalar_ref, ...), custom_call_target="tpu_custom_call" | custom-call | tf_op jit(solution)/shard_map/pallas_call | solution.py:166
  34.4 1.7 %collective-permute-start.4 = (bf16[2,128,512]{2,1,0:T(8,128)(2,1)S(1)}, bf16[2,128,512]{2,1,0:T(8,128)(2,1)S(1)}, u32[]{:S(2)}, u32[]{:S(2)}) collective-permute-start(bf16[2,128,512]{2,1,0:T(8,128)(2,1)S(1)} %get-tuple-element.32), channel_id=1, source_target_pairs={{0,3},{1,0},{2,1},{3,2},{4,7},{5,4},{6,5},{7,6},{8,11},{9,8},{10,9... | collective-permute-start | bytes 786440 | tf_op jit(solution)/shard_map/ppermute | solution.py:121
  36.1 0.3 collective-permute-start.3
  36.4 8.7 %collective-permute-done.4 = bf16[2,128,512]{2,1,0:T(8,128)(2,1)S(1)} collective-permute-done((bf16[2,128,512]{2,1,0:T(8,128)(2,1)S(1)}, bf16[2,128,512]{2,1,0:T(8,128)(2,1)S(1)}, u32[]{:S(2)}, u32[]{:S(2)}) %collective-permute-start.4) | collective-permute-done | bytes 262176 | tf_op jit(solution)/shard_map/ppermute | solution.py:121
  45.1 0.1 add_convert_fusion
  45.2 2.2 %collective-permute-start.5 = (bf16[2,128,512]{2,1,0:T(8,128)(2,1)S(1)}, bf16[2,128,512]{2,1,0:T(8,128)(2,1)S(1)}, u32[]{:S(2)}, u32[]{:S(2)}) collective-permute-start(bf16[2,128,512]{2,1,0:T(8,128)(2,1)S(1)} %add_convert_fusion), channel_id=1, source_target_pairs={{0,3},{1,0},{2,1},{3,2},{4,7},{5,4},{6,5},{7,6},{8,11},{9,8},{10,9... | collective-permute-start | bytes 786440 | tf_op jit(solution)/shard_map/ppermute | solution.py:121
  47.4 1.6 %collective-permute-done.3 = bf16[2,128,512]{2,1,0:T(8,128)(2,1)S(1)} collective-permute-done((bf16[2,128,512]{2,1,0:T(8,128)(2,1)S(1)}, bf16[2,128,512]{2,1,0:T(8,128)(2,1)S(1)}, u32[]{:S(2)}, u32[]{:S(2)}) %collective-permute-start.3) | collective-permute-done | bytes 262176 | tf_op jit(solution)/shard_map/ppermute | solution.py:121
  49.0 2.8 %collective-permute-done.5 = bf16[2,128,512]{2,1,0:T(8,128)(2,1)S(1)} collective-permute-done((bf16[2,128,512]{2,1,0:T(8,128)(2,1)S(1)}, bf16[2,128,512]{2,1,0:T(8,128)(2,1)S(1)}, u32[]{:S(2)}, u32[]{:S(2)}) %collective-permute-start.5) | collective-permute-done | bytes 262176 | tf_op jit(solution)/shard_map/ppermute | solution.py:121
  51.8 0.8 %add_convert_fusion.1 = (bf16[1,128,512]{2,1,0:T(8,128)(2,1)}, bf16[1,128,512]{2,1,0:T(8,128)(2,1)}) fusion(bf16[2,128,512]{2,1,0:T(8,128)(2,1)S(1)} %collective-permute-done.5, bf16[2,128,512]{2,1,0:T(8,128)(2,1)S(1)} %collective-permute-done.3, bf16[2,128,512]{2,1,0:T(8,128)(2,1)S(1)} %get-tuple-element.29), kind=kLoop, calls=%fused_computation.6 | loop fusion | flops 786432 | bytes 1048576 | tf_op jit(solution)/shard_map/convert_element_type | solution.py:205
  (1 shorter events, 0.0 us)
Async XLA Ops:
  0.6 15.8 %copy-start.3 = (bf16[1,1,32,8192]{3,2,1,0:T(8,128)(2,1)S(1)}, bf16[1,1,32,8192]{3,2,1,0:T(8,128)(2,1)}, u32[]{:S(2)}) copy-start(bf16[1,1,32,8192]{3,2,1,0:T(8,128)(2,1)} %param.13) | copy-start | bytes 1572868
  3.8 12.6 %collective-permute-start = (bf16[272,512]{1,0:T(8,128)(2,1)S(1)}, bf16[272,512]{1,0:T(8,128)(2,1)S(1)}, u32[]{:S(2)}, u32[]{:S(2)}) collective-permute-start(bf16[272,512]{1,0:T(8,128)(2,1)S(1)} %fusion.2.rest_0_), channel_id=1, source_target_pairs={{0,1},{1,2},{2,3},{3,0},{4,5},{5,6},{6,7},{7,4},{8,9},{9,10},{10,1... | collective-permute-start | bytes 835592 | tf_op jit(solution)/shard_map/ppermute | solution.py:121
  6.9 14.3 %collective-permute-start.1 = (bf16[272,512]{1,0:T(8,128)(2,1)S(1)}, bf16[272,512]{1,0:T(8,128)(2,1)S(1)}, u32[]{:S(2)}, u32[]{:S(2)}) collective-permute-start(bf16[272,512]{1,0:T(8,128)(2,1)S(1)} %fusion.2.rest_0_), channel_id=1, source_target_pairs={{0,3},{1,0},{2,1},{3,2},{4,7},{5,4},{6,5},{7,6},{8,11},{9,8},{10,9... | collective-permute-start | bytes 835592 | tf_op jit(solution)/shard_map/ppermute | solution.py:121
  9.8 17.8 %copy-start = (bf16[1,1,32,8192]{3,2,1,0:T(8,128)(2,1)S(1)}, bf16[1,1,32,8192]{3,2,1,0:T(8,128)(2,1)}, u32[]{:S(2)}) copy-start(bf16[1,1,32,8192]{3,2,1,0:T(8,128)(2,1)} %param.12) | copy-start | bytes 1572868
  16.5 11.1 %collective-permute-start.2 = (bf16[272,512]{1,0:T(8,128)(2,1)S(1)}, bf16[272,512]{1,0:T(8,128)(2,1)S(1)}, u32[]{:S(2)}, u32[]{:S(2)}) collective-permute-start(bf16[272,512]{1,0:T(8,128)(2,1)S(1)} %collective-permute-done.rest_1_), channel_id=1, source_target_pairs={{0,1},{1,2},{2,3},{3,0},{4,5},{5,6},{6,7},{7,4},{8,9},{9,10},{10,1... | collective-permute-start | bytes 835592 | tf_op jit(solution)/shard_map/ppermute | solution.py:121
  16.5 11.1 %copy-start.1 = (bf16[1,1,32,512]{3,2,1,0:T(8,128)(2,1)S(1)}, bf16[1,1,32,512]{3,2,1,0:T(8,128)(2,1)}, u32[]{:S(2)}) copy-start(bf16[1,1,32,512]{3,2,1,0:T(8,128)(2,1)} %param.14) | copy-start | bytes 98308
  16.5 11.1 %copy-start.2 = (bf16[1,1,32,512]{3,2,1,0:T(8,128)(2,1)S(1)}, bf16[1,1,32,512]{3,2,1,0:T(8,128)(2,1)}, u32[]{:S(2)}) copy-start(bf16[1,1,32,512]{3,2,1,0:T(8,128)(2,1)} %param.15) | copy-start | bytes 98308
  34.4 10.7 %collective-permute-start.4 = (bf16[2,128,512]{2,1,0:T(8,128)(2,1)S(1)}, bf16[2,128,512]{2,1,0:T(8,128)(2,1)S(1)}, u32[]{:S(2)}, u32[]{:S(2)}) collective-permute-start(bf16[2,128,512]{2,1,0:T(8,128)(2,1)S(1)} %get-tuple-element.32), channel_id=1, source_target_pairs={{0,3},{1,0},{2,1},{3,2},{4,7},{5,4},{6,5},{7,6},{8,11},{9,8},{10,9... | collective-permute-start | bytes 786440 | tf_op jit(solution)/shard_map/ppermute | solution.py:121
  36.1 12.9 %collective-permute-start.3 = (bf16[2,128,512]{2,1,0:T(8,128)(2,1)S(1)}, bf16[2,128,512]{2,1,0:T(8,128)(2,1)S(1)}, u32[]{:S(2)}, u32[]{:S(2)}) collective-permute-start(bf16[2,128,512]{2,1,0:T(8,128)(2,1)S(1)} %get-tuple-element.30), channel_id=1, source_target_pairs={{0,1},{1,2},{2,3},{3,0},{4,5},{5,6},{6,7},{7,4},{8,9},{9,10},{10,1... | collective-permute-start | bytes 786440 | tf_op jit(solution)/shard_map/ppermute | solution.py:121
  45.2 6.6 %collective-permute-start.5 = (bf16[2,128,512]{2,1,0:T(8,128)(2,1)S(1)}, bf16[2,128,512]{2,1,0:T(8,128)(2,1)S(1)}, u32[]{:S(2)}, u32[]{:S(2)}) collective-permute-start(bf16[2,128,512]{2,1,0:T(8,128)(2,1)S(1)} %add_convert_fusion), channel_id=1, source_target_pairs={{0,3},{1,0},{2,1},{3,2},{4,7},{5,4},{6,5},{7,6},{8,11},{9,8},{10,9... | collective-permute-start | bytes 786440 | tf_op jit(solution)/shard_map/ppermute | solution.py:121
